TPU v7x, 768 devices: a whole 4x8x12 slice. The times are simulated.
768 devices in a mesh: rad: 32 (over x_lo, y, core), az: 24 (over x_hi, z).
Axes of the slice: x: 4 (x_hi: 2, x_lo: 2; x = x_hi * 2 + x_lo), y: 8, z: 12, core: 2. Of those that a mesh axis runs over, the one named last changes fastest.
Arguments:
- fields: float32 [5, 192, 8, 6144], P(None, 'rad', None, 'az'), may hold values from -0.9 to 4, as said below
- shifts: int32 [192], P('rad'), may hold values from 0 to 768, as said below
Outputs:
- advanced: float32 [5, 192, 8, 6144], P(None, 'rad', None, 'az')
Inputs may be any that keep to these rules, and one draw needn't show every extreme that they name: `fields`: components 0 (density) and 4 (pressure) lie in 2.0 to 4.0; components 1 to 3 (velocities) lie in -0.9 to 0.9. The first radius row shifts by 768 cells and the last one by 0.
All inputs are finite; a program needn't handle non-finite values.
Results may differ from a plain program's by a relative error of at most 0.0003.
Values sent between devices are 32-bit elements; how exact they have to be, the bound alone decides.
No kernel may reach another device: no remote copies, remote signals or barrier semaphores. Data moves between devices by JAX's collectives and lax.ppermute only.
A program may use at most 64 MiB of HBM per device.

v0:
```python
import jax
import jax.numpy as jnp
from jax import lax
from jax.sharding import PartitionSpec as P

ADIABATIC = 1.4
COURANT_RADIAL = 0.09
COURANT_POLAR = 0.08
COURANT_AZIMUTH = 0.18


def padded_2(shard, sides, width, wrap):
    for axis, dim in sides:
        count, length = (lax.axis_size(axis), shard.shape[dim])
        up = [(i, (i + 1) % count) for i in range(count if wrap else count - 1)]
        down = [(j, i) for i, j in up]
        last = lax.slice_in_dim(shard, length - width, length, axis=dim)
        initial = lax.slice_in_dim(shard, 0, width, axis=dim)
        before = lax.ppermute(last, axis, up)
        after = lax.ppermute(initial, axis, down)
        shard = jnp.concatenate([before, shard, after], axis=dim)
    return shard


def shifted(block, axis, distance):
    devices = range(lax.axis_size(axis))
    route = [((i - distance) % len(devices), i) for i in devices]
    return lax.ppermute(block, axis, route)


def cut_along(values, first_cell, finish, along):
    return lax.slice_in_dim(values, first_cell, finish, axis=along)


def edge_states(values, along):
    length = values.shape[along]
    before = cut_along(values, 0, length - 3, along)
    centre = cut_along(values, 1, length - 2, along)
    follow = cut_along(values, 2, length - 1, along)
    beyond = cut_along(values, 3, length, along)
    interface = 7.0 / 12.0 * (centre + follow) - 1.0 / 12.0 * (before + beyond)
    interface = jnp.clip(interface, jnp.minimum(centre, follow), jnp.maximum(centre, follow))
    count = length - 3
    left_edge = cut_along(interface, 0, count - 1, along)
    right_edge = cut_along(interface, 1, count, along)
    middle_cell = cut_along(values, 2, length - 2, along)
    no_slope = (right_edge - middle_cell) * (middle_cell - left_edge) <= 0.0
    left_edge = jnp.where(no_slope, middle_cell, left_edge)
    right_edge = jnp.where(no_slope, middle_cell, right_edge)
    spread = right_edge - left_edge
    middle = middle_cell - 0.5 * (left_edge + right_edge)
    new_left = jnp.where(
        spread * middle > spread * spread / 6.0, 3.0 * middle_cell - 2.0 * right_edge, left_edge
    )
    new_right = jnp.where(
        spread * middle < -spread * spread / 6.0, 3.0 * middle_cell - 2.0 * left_edge, right_edge
    )
    return (new_left, new_right)


def primitive_parts(state, normal):
    density = state[0]
    pressure = state[4]
    normal_speed = state[normal]
    squared = state[1] * state[1] + state[2] * state[2] + state[3] * state[3]
    energy = pressure / (ADIABATIC - 1.0) + 0.5 * density * squared
    sound_speed = jnp.sqrt(ADIABATIC * pressure / density)
    conserved = [density, density * state[1], density * state[2], density * state[3], energy]
    flux_list = [plain_term * normal_speed for plain_term in conserved]
    flux_list[normal] = flux_list[normal] + pressure
    flux_list[4] = flux_list[4] + pressure * normal_speed
    return (density, pressure, normal_speed, energy, sound_speed, conserved, flux_list)


def star_flux(state, parts, wave_speed, contact, normal):
    density, pressure, normal_speed, energy, sound_speed, conserved, flux_list = parts
    factor = density * (wave_speed - normal_speed) / (wave_speed - contact)
    star_energy = factor * (
        energy / density
        + (contact - normal_speed) * (contact + pressure / (density * (wave_speed - normal_speed)))
    )
    star_state = [factor, factor * state[1], factor * state[2], factor * state[3], star_energy]
    star_state[normal] = factor * contact
    return [
        flux_term + wave_speed * (star_term - plain_term)
        for flux_term, star_term, plain_term in zip(flux_list, star_state, conserved)
    ]


def riemann_flux(left_state, right_state, normal):
    left_parts = primitive_parts(left_state, normal)
    right_parts = primitive_parts(right_state, normal)
    slow_wave = jnp.minimum(left_parts[2] - left_parts[4], right_parts[2] - right_parts[4])
    fast_wave = jnp.maximum(left_parts[2] + left_parts[4], right_parts[2] + right_parts[4])
    mass_left = left_parts[0] * (left_parts[2] - slow_wave)
    mass_right = right_parts[0] * (fast_wave - right_parts[2])
    contact = (
        mass_left * left_parts[2] + mass_right * right_parts[2] + left_parts[1] - right_parts[1]
    ) / (mass_left + mass_right)
    star_left = star_flux(left_state, left_parts, slow_wave, contact, normal)
    star_right = star_flux(right_state, right_parts, fast_wave, contact, normal)
    merged = []
    for flux_left, inner_left, inner_right, flux_right in zip(
        left_parts[6], star_left, star_right, right_parts[6]
    ):
        merged.append(
            jnp.where(
                slow_wave >= 0.0,
                flux_left,
                jnp.where(
                    contact >= 0.0, inner_left, jnp.where(fast_wave > 0.0, inner_right, flux_right)
                ),
            )
        )
    return jnp.stack(merged)


def flux_difference(window, along, normal):
    left_edge, right_edge = edge_states(window, along)
    cell_total = left_edge.shape[along]
    from_left = cut_along(right_edge, 0, cell_total - 1, along)
    from_right = cut_along(left_edge, 1, cell_total, along)
    flux_all = riemann_flux(from_left, from_right, normal)
    faces = flux_all.shape[along]
    return cut_along(flux_all, 1, faces, along) - cut_along(flux_all, 0, faces - 1, along)


def tendency(window, courant_rows):
    padded = jnp.pad(window, ((0, 0), (0, 0), (3, 3), (0, 0)), mode="edge")
    radial_term = flux_difference(padded[:, :, 3:-3, 3:-3], 1, 1)
    polar_term = flux_difference(padded[:, 3:-3, :, 3:-3], 2, 2)
    azimuth_term = flux_difference(padded[:, 3:-3, 3:-3, :], 3, 3)
    return -(
        COURANT_RADIAL * radial_term
        + COURANT_POLAR * polar_term
        + courant_rows[None, :, None, None] * azimuth_term
    )


def courant_profile(row_index, total_rows):
    return COURANT_AZIMUTH / (1.0 + (row_index + 0.5) / total_rows)


def to_conserved(primitive):
    density = primitive[0]
    squared = (
        primitive[1] * primitive[1] + primitive[2] * primitive[2] + primitive[3] * primitive[3]
    )
    energy = primitive[4] / (ADIABATIC - 1.0) + 0.5 * density * squared
    return jnp.stack(
        [density, density * primitive[1], density * primitive[2], density * primitive[3], energy]
    )


def to_primitive(conserved):
    density = conserved[0]
    velocity = conserved[1:4] / density
    squared = velocity[0] * velocity[0] + velocity[1] * velocity[1] + velocity[2] * velocity[2]
    pressure = (ADIABATIC - 1.0) * (conserved[4] - 0.5 * density * squared)
    return jnp.concatenate([density[None], velocity, pressure[None]])


def fix_edges(extended, inner, depth):
    rad_index = lax.axis_index("rad")
    last_index = lax.axis_size("rad") - 1
    lower_rim = jnp.where(
        rad_index == 0,
        jnp.broadcast_to(inner[:, :1], extended[:, :depth].shape),
        extended[:, :depth],
    )
    upper_rim = jnp.where(
        rad_index == last_index,
        jnp.broadcast_to(inner[:, -1:], extended[:, -depth:].shape),
        extended[:, -depth:],
    )
    return jnp.concatenate([lower_rim, extended[:, depth:-depth], upper_rim], axis=1)


def extend_thin(primitive):
    widened = padded_2(primitive, (("rad", 1),), 3, False)
    widened = fix_edges(widened, primitive, 3)
    return padded_2(widened, (("az", 3),), 3, True)


def pick_rows(blocks, quotient):
    chosen = blocks[0]
    for distance in range(1, len(blocks)):
        chosen = jnp.where((quotient == distance)[None, :, None, None], blocks[distance], chosen)
    return chosen


def roll_rows(farther, current, remainder):
    joined = jnp.concatenate([farther, current], axis=3)
    cell_count = current.shape[3]

    def slice_row(one_row, amount):
        return lax.dynamic_slice_in_dim(one_row, cell_count - amount, cell_count, axis=2)

    return jax.vmap(slice_row, in_axes=(1, 0), out_axes=1)(joined, remainder)


def shift_rows(primitive, quotient, remainder):
    blocks = [primitive]
    for distance in range(1, 4):
        blocks.append(shifted(primitive, "az", distance))
    current = pick_rows(blocks, quotient)
    farther = pick_rows(blocks[1:] + [jnp.zeros_like(primitive)], quotient)
    return roll_rows(farther, current, remainder)


def on_device(fields, shifts):
    row_count = fields.shape[1]
    cell_count = fields.shape[3]
    rad_index = lax.axis_index("rad")
    total_rows = row_count * lax.axis_size("rad")
    inner_rows = (rad_index * row_count + jnp.arange(row_count, dtype=jnp.int32)).astype(
        jnp.float32
    )
    courant_inner = courant_profile(inner_rows, total_rows)
    quotient = shifts // cell_count
    remainder = shifts - quotient * cell_count
    current = fields
    initial = to_conserved(current)
    section_one = initial + tendency(extend_thin(current), courant_inner)
    section_one_prim = to_primitive(section_one)
    section_two = 0.5 * initial + 0.5 * (
        section_one + tendency(extend_thin(section_one_prim), courant_inner)
    )
    current = shift_rows(to_primitive(section_two), quotient, remainder)
    return current


def solution(mesh):
    in_specs = (P(None, "rad", None, "az"), P("rad"))
    out_specs = P(None, "rad", None, "az")
    return jax.shard_map(
        on_device, mesh=mesh, in_specs=in_specs, out_specs=out_specs, check_vma=False
    )
```

profile of v0, /device:TPU:81, one launch (start us, length us, event | category | flops | bytes accessed | tf_op | source)
XLA Modules:
  0.0 136.9 jit_solution(1160854875500198312)
XLA Ops:
  0.0 1.0 fusion.211
  1.0 3.8 %collective-permute-start = (f32[5,3,8,256]{3,2,1,0:T(8,128)S(1)}, f32[5,3,8,256]{3,2,1,0:T(8,128)S(1)}, u32[]{:S(2)}, u32[]{:S(2)}) collective-permute-start(f32[5,3,8,256]{3,2,1,0:T(8,128)S(1)} %get-tuple-element.39), channel_id=1, source_target_pairs={{0,24},{24,48},{48,72},{72,96},{96,120},{120,144},{144,168},{168,1... | collective-permute-start | bytes 368648 | tf_op jit(solution)/shard_map/ppermute | solution.py:19
  4.8 1.9 %collective-permute-start.1 = (f32[5,3,8,256]{3,2,1,0:T(8,128)S(1)}, f32[5,3,8,256]{3,2,1,0:T(8,128)S(1)}, u32[]{:S(2)}, u32[]{:S(2)}) collective-permute-start(f32[5,3,8,256]{3,2,1,0:T(8,128)S(1)} %get-tuple-element.40), channel_id=1, source_target_pairs={{24,0},{48,24},{72,48},{96,72},{120,96},{144,120},{168,144},{192,1... | collective-permute-start | bytes 368648 | tf_op jit(solution)/shard_map/ppermute | solution.py:20
  10.8 0.9 constant_dynamic-update-slice_fusion
  12.4 4.0 %collective-permute-start.2 = (f32[5,12,8,3]{3,2,1,0:T(8,128)S(1)}, f32[5,12,8,3]{3,2,1,0:T(8,128)S(1)}, u32[]{:S(2)}, u32[]{:S(2)}) collective-permute-start(f32[5,12,8,3]{3,2,1,0:T(8,128)S(1)} %get-tuple-element.27), channel_id=1, source_target_pairs={{0,1},{1,2},{2,3},{3,4},{4,5},{5,6},{6,7},{7,8},{8,9},{9,10},{10,1... | collective-permute-start | bytes 17288 | tf_op jit(solution)/shard_map/ppermute | solution.py:19
  16.4 1.9 %collective-permute-start.3 = (f32[5,12,8,3]{3,2,1,0:T(8,128)S(1)}, f32[5,12,8,3]{3,2,1,0:T(8,128)S(1)}, u32[]{:S(2)}, u32[]{:S(2)}) collective-permute-start(f32[5,12,8,3]{3,2,1,0:T(8,128)S(1)} %get-tuple-element.28), channel_id=1, source_target_pairs={{1,0},{2,1},{3,2},{4,3},{5,4},{6,5},{7,6},{8,7},{9,8},{10,9},{11,1... | collective-permute-start | bytes 17288 | tf_op jit(solution)/shard_map/ppermute | solution.py:20
  19.1 2.1 %collective-permute-done.2 = f32[5,12,8,3]{3,2,1,0:T(8,128)S(1)} collective-permute-done((f32[5,12,8,3]{3,2,1,0:T(8,128)S(1)}, f32[5,12,8,3]{3,2,1,0:T(8,128)S(1)}, u32[]{:S(2)}, u32[]{:S(2)}) %collective-permute-start.2) | collective-permute-done | bytes 5792 | tf_op jit(solution)/shard_map/ppermute | solution.py:19
  21.3 4.6 %collective-permute-done.3 = f32[5,12,8,3]{3,2,1,0:T(8,128)S(1)} collective-permute-done((f32[5,12,8,3]{3,2,1,0:T(8,128)S(1)}, f32[5,12,8,3]{3,2,1,0:T(8,128)S(1)}, u32[]{:S(2)}, u32[]{:S(2)}) %collective-permute-start.3) | collective-permute-done | bytes 5792 | tf_op jit(solution)/shard_map/ppermute | solution.py:20
  32.4 4.9 %collective-permute-start.4 = (f32[5,3,8,256]{3,2,1,0:T(8,128)S(1)}, f32[5,3,8,256]{3,2,1,0:T(8,128)S(1)}, u32[]{:S(2)}, u32[]{:S(2)}) collective-permute-start(f32[5,3,8,256]{3,2,1,0:T(8,128)S(1)} %get-tuple-element.33), channel_id=1, source_target_pairs={{0,24},{24,48},{48,72},{72,96},{96,120},{120,144},{144,168},{168,1... | collective-permute-start | bytes 368648 | tf_op jit(solution)/shard_map/ppermute | solution.py:19
  37.4 1.9 %collective-permute-start.5 = (f32[5,3,8,256]{3,2,1,0:T(8,128)S(1)}, f32[5,3,8,256]{3,2,1,0:T(8,128)S(1)}, u32[]{:S(2)}, u32[]{:S(2)}) collective-permute-start(f32[5,3,8,256]{3,2,1,0:T(8,128)S(1)} %get-tuple-element.34), channel_id=1, source_target_pairs={{24,0},{48,24},{72,48},{96,72},{120,96},{144,120},{168,144},{192,1... | collective-permute-start | bytes 368648 | tf_op jit(solution)/shard_map/ppermute | solution.py:20
  39.3 4.2 %collective-permute-done.5 = f32[5,3,8,256]{3,2,1,0:T(8,128)S(1)} collective-permute-done((f32[5,3,8,256]{3,2,1,0:T(8,128)S(1)}, f32[5,3,8,256]{3,2,1,0:T(8,128)S(1)}, u32[]{:S(2)}, u32[]{:S(2)}) %collective-permute-start.5) | collective-permute-done | bytes 122912 | tf_op jit(solution)/shard_map/ppermute | solution.py:20
  44.1 5.2 %collective-permute-start.6 = (f32[5,12,8,3]{3,2,1,0:T(8,128)S(1)}, f32[5,12,8,3]{3,2,1,0:T(8,128)S(1)}, u32[]{:S(2)}, u32[]{:S(2)}) collective-permute-start(f32[5,12,8,3]{3,2,1,0:T(8,128)S(1)} %get-tuple-element.25), channel_id=1, source_target_pairs={{0,1},{1,2},{2,3},{3,4},{4,5},{5,6},{6,7},{7,8},{8,9},{9,10},{10,1... | collective-permute-start | bytes 17288 | tf_op jit(solution)/shard_map/ppermute | solution.py:19
  49.4 8.1 %collective-permute-start.7 = (f32[5,12,8,3]{3,2,1,0:T(8,128)S(1)}, f32[5,12,8,3]{3,2,1,0:T(8,128)S(1)}, u32[]{:S(2)}, u32[]{:S(2)}) collective-permute-start(f32[5,12,8,3]{3,2,1,0:T(8,128)S(1)} %get-tuple-element.26), channel_id=1, source_target_pairs={{1,0},{2,1},{3,2},{4,3},{5,4},{6,5},{7,6},{8,7},{9,8},{10,9},{11,1... | collective-permute-start | bytes 17288 | tf_op jit(solution)/shard_map/ppermute | solution.py:20
  58.3 1.8 %collective-permute-done.6 = f32[5,12,8,3]{3,2,1,0:T(8,128)S(1)} collective-permute-done((f32[5,12,8,3]{3,2,1,0:T(8,128)S(1)}, f32[5,12,8,3]{3,2,1,0:T(8,128)S(1)}, u32[]{:S(2)}, u32[]{:S(2)}) %collective-permute-start.6) | collective-permute-done | bytes 5792 | tf_op jit(solution)/shard_map/ppermute | solution.py:19
  60.1 1.8 %collective-permute-done.7 = f32[5,12,8,3]{3,2,1,0:T(8,128)S(1)} collective-permute-done((f32[5,12,8,3]{3,2,1,0:T(8,128)S(1)}, f32[5,12,8,3]{3,2,1,0:T(8,128)S(1)}, u32[]{:S(2)}, u32[]{:S(2)}) %collective-permute-start.7) | collective-permute-done | bytes 5792 | tf_op jit(solution)/shard_map/ppermute | solution.py:20
  68.3 1.9 %collective-permute-start.10 = (f32[5,6,8,256]{3,2,1,0:T(8,128)S(1)}, f32[5,6,8,256]{3,2,1,0:T(8,128)S(1)}, u32[]{:S(2)}, u32[]{:S(2)}) collective-permute-start(f32[5,6,8,256]{3,2,1,0:T(8,128)S(1)} %pad_maximum_fusion.34), channel_id=1, source_target_pairs={{23,0},{0,1},{1,2},{2,3},{3,4},{4,5},{5,6},{6,7},{7,8},{8,9},{9,10... | collective-permute-start | bytes 737288 | tf_op jit(solution)/shard_map/ppermute | solution.py:28
  70.3 3.8 %collective-permute-start.9 = (f32[5,6,8,256]{3,2,1,0:T(8,128)S(1)}, f32[5,6,8,256]{3,2,1,0:T(8,128)S(1)}, u32[]{:S(2)}, u32[]{:S(2)}) collective-permute-start(f32[5,6,8,256]{3,2,1,0:T(8,128)S(1)} %pad_maximum_fusion.34), channel_id=1, source_target_pairs={{22,0},{23,1},{0,2},{1,3},{2,4},{3,5},{4,6},{5,7},{6,8},{7,9},{8,1... | collective-permute-start | bytes 737288 | tf_op jit(solution)/shard_map/ppermute | solution.py:28
  74.0 6.4 %collective-permute-start.8 = (f32[5,6,8,256]{3,2,1,0:T(8,128)S(1)}, f32[5,6,8,256]{3,2,1,0:T(8,128)S(1)}, u32[]{:S(2)}, u32[]{:S(2)}) collective-permute-start(f32[5,6,8,256]{3,2,1,0:T(8,128)S(1)} %pad_maximum_fusion.34), channel_id=1, source_target_pairs={{21,0},{22,1},{23,2},{0,3},{1,4},{2,5},{3,6},{4,7},{5,8},{6,9},{7,... | collective-permute-start | bytes 737288 | tf_op jit(solution)/shard_map/ppermute | solution.py:28
  80.5 1.8 %collective-permute-done.10 = f32[5,6,8,256]{3,2,1,0:T(8,128)S(1)} collective-permute-done((f32[5,6,8,256]{3,2,1,0:T(8,128)S(1)}, f32[5,6,8,256]{3,2,1,0:T(8,128)S(1)}, u32[]{:S(2)}, u32[]{:S(2)}) %collective-permute-start.10) | collective-permute-done | bytes 245792 | tf_op jit(solution)/shard_map/ppermute | solution.py:28
  82.3 10.7 %collective-permute-done.9 = f32[5,6,8,256]{3,2,1,0:T(8,128)S(1)} collective-permute-done((f32[5,6,8,256]{3,2,1,0:T(8,128)S(1)}, f32[5,6,8,256]{3,2,1,0:T(8,128)S(1)}, u32[]{:S(2)}, u32[]{:S(2)}) %collective-permute-start.9) | collective-permute-done | bytes 245792 | tf_op jit(solution)/shard_map/ppermute | solution.py:28
  92.9 22.2 %collective-permute-done.8 = f32[5,6,8,256]{3,2,1,0:T(8,128)S(1)} collective-permute-done((f32[5,6,8,256]{3,2,1,0:T(8,128)S(1)}, f32[5,6,8,256]{3,2,1,0:T(8,128)S(1)}, u32[]{:S(2)}, u32[]{:S(2)}) %collective-permute-start.8) | collective-permute-done | bytes 245792 | tf_op jit(solution)/shard_map/ppermute | solution.py:28
  115.4 8.6 %copy.87 = f32[5,6,8,512]{2,0,1,3:T(8,128)} copy(f32[5,6,8,512]{3,2,1,0:T(8,128)S(1)} %pad_maximum_fusion.16) | data formatting | bytes 983040 | tf_op jit(solution)/shard_map/concatenate | solution.py:193
  123.9 8.3 %gather_fusion = f32[6,5,8,256]{2,1,3,0:T(8,128)} fusion(f32[6,5,8,512]{2,1,0,3:T(8,128)} %bitcast.30, s32[6]{0:T(128)S(1)} %get-tuple-element.5), kind=kCustom, calls=%fused_computation | custom fusion | bytes 491616 | tf_op jit(solution)/shard_map/vmap()/gather | solution.py:197
  132.2 4.7 %copy.88 = f32[5,6,8,256]{3,2,1,0:T(8,128)} copy(f32[5,6,8,256]{2,0,3,1:T(8,128)} %bitcast.31) | data formatting | bytes 491520 | tf_op jit(solution)/shard_map/vmap()/transpose | solution.py:199
  (92 shorter events, 19.8 us)
Async XLA Ops:
  0.0 11.8 %copy-start = (f32[5,6,8,256]{3,2,1,0:T(8,128)S(1)}, f32[5,6,8,256]{3,2,1,0:T(8,128)}, u32[]{:S(2)}) copy-start(f32[5,6,8,256]{3,2,1,0:T(8,128)} %param.2) | copy-start | bytes 737284
  1.0 10.7 %collective-permute-start = (f32[5,3,8,256]{3,2,1,0:T(8,128)S(1)}, f32[5,3,8,256]{3,2,1,0:T(8,128)S(1)}, u32[]{:S(2)}, u32[]{:S(2)}) collective-permute-start(f32[5,3,8,256]{3,2,1,0:T(8,128)S(1)} %get-tuple-element.39), channel_id=1, source_target_pairs={{0,24},{24,48},{48,72},{72,96},{96,120},{120,144},{144,168},{168,1... | collective-permute-start | bytes 368648 | tf_op jit(solution)/shard_map/ppermute | solution.py:19
  4.8 7.0 %collective-permute-start.1 = (f32[5,3,8,256]{3,2,1,0:T(8,128)S(1)}, f32[5,3,8,256]{3,2,1,0:T(8,128)S(1)}, u32[]{:S(2)}, u32[]{:S(2)}) collective-permute-start(f32[5,3,8,256]{3,2,1,0:T(8,128)S(1)} %get-tuple-element.40), channel_id=1, source_target_pairs={{24,0},{48,24},{72,48},{96,72},{120,96},{144,120},{168,144},{192,1... | collective-permute-start | bytes 368648 | tf_op jit(solution)/shard_map/ppermute | solution.py:20
  12.4 8.9 %collective-permute-start.2 = (f32[5,12,8,3]{3,2,1,0:T(8,128)S(1)}, f32[5,12,8,3]{3,2,1,0:T(8,128)S(1)}, u32[]{:S(2)}, u32[]{:S(2)}) collective-permute-start(f32[5,12,8,3]{3,2,1,0:T(8,128)S(1)} %get-tuple-element.27), channel_id=1, source_target_pairs={{0,1},{1,2},{2,3},{3,4},{4,5},{5,6},{6,7},{7,8},{8,9},{9,10},{10,1... | collective-permute-start | bytes 17288 | tf_op jit(solution)/shard_map/ppermute | solution.py:19
  16.4 9.5 %collective-permute-start.3 = (f32[5,12,8,3]{3,2,1,0:T(8,128)S(1)}, f32[5,12,8,3]{3,2,1,0:T(8,128)S(1)}, u32[]{:S(2)}, u32[]{:S(2)}) collective-permute-start(f32[5,12,8,3]{3,2,1,0:T(8,128)S(1)} %get-tuple-element.28), channel_id=1, source_target_pairs={{1,0},{2,1},{3,2},{4,3},{5,4},{6,5},{7,6},{8,7},{9,8},{10,9},{11,1... | collective-permute-start | bytes 17288 | tf_op jit(solution)/shard_map/ppermute | solution.py:20
  32.4 6.9 %collective-permute-start.4 = (f32[5,3,8,256]{3,2,1,0:T(8,128)S(1)}, f32[5,3,8,256]{3,2,1,0:T(8,128)S(1)}, u32[]{:S(2)}, u32[]{:S(2)}) collective-permute-start(f32[5,3,8,256]{3,2,1,0:T(8,128)S(1)} %get-tuple-element.33), channel_id=1, source_target_pairs={{0,24},{24,48},{48,72},{72,96},{96,120},{120,144},{144,168},{168,1... | collective-permute-start | bytes 368648 | tf_op jit(solution)/shard_map/ppermute | solution.py:19
  37.4 6.2 %collective-permute-start.5 = (f32[5,3,8,256]{3,2,1,0:T(8,128)S(1)}, f32[5,3,8,256]{3,2,1,0:T(8,128)S(1)}, u32[]{:S(2)}, u32[]{:S(2)}) collective-permute-start(f32[5,3,8,256]{3,2,1,0:T(8,128)S(1)} %get-tuple-element.34), channel_id=1, source_target_pairs={{24,0},{48,24},{72,48},{96,72},{120,96},{144,120},{168,144},{192,1... | collective-permute-start | bytes 368648 | tf_op jit(solution)/shard_map/ppermute | solution.py:20
  44.1 15.9 %collective-permute-start.6 = (f32[5,12,8,3]{3,2,1,0:T(8,128)S(1)}, f32[5,12,8,3]{3,2,1,0:T(8,128)S(1)}, u32[]{:S(2)}, u32[]{:S(2)}) collective-permute-start(f32[5,12,8,3]{3,2,1,0:T(8,128)S(1)} %get-tuple-element.25), channel_id=1, source_target_pairs={{0,1},{1,2},{2,3},{3,4},{4,5},{5,6},{6,7},{7,8},{8,9},{9,10},{10,1... | collective-permute-start | bytes 17288 | tf_op jit(solution)/shard_map/ppermute | solution.py:19
  49.4 12.4 %collective-permute-start.7 = (f32[5,12,8,3]{3,2,1,0:T(8,128)S(1)}, f32[5,12,8,3]{3,2,1,0:T(8,128)S(1)}, u32[]{:S(2)}, u32[]{:S(2)}) collective-permute-start(f32[5,12,8,3]{3,2,1,0:T(8,128)S(1)} %get-tuple-element.26), channel_id=1, source_target_pairs={{1,0},{2,1},{3,2},{4,3},{5,4},{6,5},{7,6},{8,7},{9,8},{10,9},{11,1... | collective-permute-start | bytes 17288 | tf_op jit(solution)/shard_map/ppermute | solution.py:20
  68.1 12.4 %copy-start.1 = (s32[6]{0:T(128)S(1)}, s32[6]{0:T(128)}, u32[]{:S(2)}) copy-start(s32[6]{0:T(128)} %param.3) | copy-start | bytes 76
  68.3 13.9 %collective-permute-start.10 = (f32[5,6,8,256]{3,2,1,0:T(8,128)S(1)}, f32[5,6,8,256]{3,2,1,0:T(8,128)S(1)}, u32[]{:S(2)}, u32[]{:S(2)}) collective-permute-start(f32[5,6,8,256]{3,2,1,0:T(8,128)S(1)} %pad_maximum_fusion.34), channel_id=1, source_target_pairs={{23,0},{0,1},{1,2},{2,3},{3,4},{4,5},{5,6},{6,7},{7,8},{8,9},{9,10... | collective-permute-start | bytes 737288 | tf_op jit(solution)/shard_map/ppermute | solution.py:28
  70.3 22.7 %collective-permute-start.9 = (f32[5,6,8,256]{3,2,1,0:T(8,128)S(1)}, f32[5,6,8,256]{3,2,1,0:T(8,128)S(1)}, u32[]{:S(2)}, u32[]{:S(2)}) collective-permute-start(f32[5,6,8,256]{3,2,1,0:T(8,128)S(1)} %pad_maximum_fusion.34), channel_id=1, source_target_pairs={{22,0},{23,1},{0,2},{1,3},{2,4},{3,5},{4,6},{5,7},{6,8},{7,9},{8,1... | collective-permute-start | bytes 737288 | tf_op jit(solution)/shard_map/ppermute | solution.py:28
  74.0 41.1 %collective-permute-start.8 = (f32[5,6,8,256]{3,2,1,0:T(8,128)S(1)}, f32[5,6,8,256]{3,2,1,0:T(8,128)S(1)}, u32[]{:S(2)}, u32[]{:S(2)}) collective-permute-start(f32[5,6,8,256]{3,2,1,0:T(8,128)S(1)} %pad_maximum_fusion.34), channel_id=1, source_target_pairs={{21,0},{22,1},{23,2},{0,3},{1,4},{2,5},{3,6},{4,7},{5,8},{6,9},{7,... | collective-permute-start | bytes 737288 | tf_op jit(solution)/shard_map/ppermute | solution.py:28
where the time goes:
time: 138 us; the launch traced here: 137 us
  waiting for transfers between devices  49.2 us (36%)
  starting transfers between devices  43.8 us (32%)
  local copies, waits for them, and re-layouts  24.8 us (18%)
  other arithmetic  18.5 us (13%)
    ppermute x3, waiting for transfers between devices, shifted(): return lax.ppermute(block, axis, route)  34.6 us
    ppermute x4, starting transfers between devices, padded_2(): before = lax.ppermute(last, axis, up)  17.9 us
    ppermute x4, starting transfers between devices, padded_2(): after = lax.ppermute(initial, axis, down)  13.9 us
    ppermute x3, starting transfers between devices, shifted(): return lax.ppermute(block, axis, route)  12.1 us
    ppermute x4, waiting for transfers between devices, padded_2(): after = lax.ppermute(initial, axis, down)  10.6 us
    concatenate x1, local copies, waits for them, and re-layouts, roll_rows(): joined = jnp.concatenate([farther, current], axis=3)  8.55 us
    gather x1, local copies, waits for them, and re-layouts, slice_row(): lax.dynamic_slice_in_dim(one_row, cell_count - amount, cell_count, axis=2)  8.27 us
    unnamed x27, other arithmetic  7.41 us
  transfers between devices with their start and end apart: 11, of which 8 were waited for; matrix products, arithmetic and copies ran while one was open for 5% of the time, Pallas kernels for 0%

commit v1 on v0

--- a/solution.py
+++ b/solution.py
@@ -7,19 +7,6 @@
 COURANT_RADIAL = 0.09
 COURANT_POLAR = 0.08
 COURANT_AZIMUTH = 0.18
-
-
-def padded_2(shard, sides, width, wrap):
-    for axis, dim in sides:
-        count, length = (lax.axis_size(axis), shard.shape[dim])
-        up = [(i, (i + 1) % count) for i in range(count if wrap else count - 1)]
-        down = [(j, i) for i, j in up]
-        last = lax.slice_in_dim(shard, length - width, length, axis=dim)
-        initial = lax.slice_in_dim(shard, 0, width, axis=dim)
-        before = lax.ppermute(last, axis, up)
-        after = lax.ppermute(initial, axis, down)
-        shard = jnp.concatenate([before, shard, after], axis=dim)
-    return shard
 
 
 def shifted(block, axis, distance):
@@ -160,52 +147,81 @@
     return jnp.concatenate([density[None], velocity, pressure[None]])
 
 
-def fix_edges(extended, inner, depth):
+MAX_SHIFT = 768
+HALO = 6
+
+
+def ring_pairs(count, step, wrap):
+    if wrap:
+        return [(i, (i + step) % count) for i in range(count)]
+    return [(i, i + step) for i in range(count) if 0 <= i + step < count]
+
+
+def diagonal_pairs(n_rad, n_az, rad_step, az_step):
+    pairs = []
+    for r in range(n_rad):
+        if not 0 <= r + rad_step < n_rad:
+            continue
+        for a in range(n_az):
+            pairs.append((r * n_az + a, (r + rad_step) * n_az + (a + az_step) % n_az))
+    return pairs
+
+
+def clamp_rows(block, depth):
     rad_index = lax.axis_index("rad")
     last_index = lax.axis_size("rad") - 1
-    lower_rim = jnp.where(
+    rows = block.shape[1]
+    lower = jnp.where(
         rad_index == 0,
-        jnp.broadcast_to(inner[:, :1], extended[:, :depth].shape),
-        extended[:, :depth],
-    )
-    upper_rim = jnp.where(
+        jnp.broadcast_to(block[:, depth : depth + 1], block[:, :depth].shape),
+        block[:, :depth],
+    )
+    upper = jnp.where(
         rad_index == last_index,
-        jnp.broadcast_to(inner[:, -1:], extended[:, -depth:].shape),
-        extended[:, -depth:],
-    )
-    return jnp.concatenate([lower_rim, extended[:, depth:-depth], upper_rim], axis=1)
-
-
-def extend_thin(primitive):
-    widened = padded_2(primitive, (("rad", 1),), 3, False)
-    widened = fix_edges(widened, primitive, 3)
-    return padded_2(widened, (("az", 3),), 3, True)
-
-
-def pick_rows(blocks, quotient):
-    chosen = blocks[0]
-    for distance in range(1, len(blocks)):
-        chosen = jnp.where((quotient == distance)[None, :, None, None], blocks[distance], chosen)
-    return chosen
-
-
-def roll_rows(farther, current, remainder):
-    joined = jnp.concatenate([farther, current], axis=3)
-    cell_count = current.shape[3]
-
-    def slice_row(one_row, amount):
-        return lax.dynamic_slice_in_dim(one_row, cell_count - amount, cell_count, axis=2)
-
-    return jax.vmap(slice_row, in_axes=(1, 0), out_axes=1)(joined, remainder)
-
-
-def shift_rows(primitive, quotient, remainder):
+        jnp.broadcast_to(block[:, rows - depth - 1 : rows - depth], block[:, rows - depth :].shape),
+        block[:, rows - depth :],
+    )
+    return jnp.concatenate([lower, block[:, depth : rows - depth], upper], axis=1)
+
+
+def extend_wide(x, width):
+    n_rad, n_az = lax.axis_size("rad"), lax.axis_size("az")
+    top = x[:, -width:]
+    bottom = x[:, :width]
+    from_below = lax.ppermute(top, "rad", ring_pairs(n_rad, 1, False))
+    from_above = lax.ppermute(bottom, "rad", ring_pairs(n_rad, -1, False))
+    from_left = lax.ppermute(x[..., -width:], "az", ring_pairs(n_az, 1, True))
+    from_right = lax.ppermute(x[..., :width], "az", ring_pairs(n_az, -1, True))
+    both = ("rad", "az")
+    low_left = lax.ppermute(top[..., -width:], both, diagonal_pairs(n_rad, n_az, 1, 1))
+    low_right = lax.ppermute(top[..., :width], both, diagonal_pairs(n_rad, n_az, 1, -1))
+    up_left = lax.ppermute(bottom[..., -width:], both, diagonal_pairs(n_rad, n_az, -1, 1))
+    up_right = lax.ppermute(bottom[..., :width], both, diagonal_pairs(n_rad, n_az, -1, -1))
+    lower = jnp.concatenate([low_left, from_below, low_right], axis=3)
+    middle = jnp.concatenate([from_left, x, from_right], axis=3)
+    upper = jnp.concatenate([up_left, from_above, up_right], axis=3)
+    return clamp_rows(jnp.concatenate([lower, middle, upper], axis=1), width)
+
+
+def shift_rows(primitive, shifts):
+    cell_count = primitive.shape[3]
+    far = -(-MAX_SHIFT // cell_count)
     blocks = [primitive]
-    for distance in range(1, 4):
+    for distance in range(1, far + 1):
         blocks.append(shifted(primitive, "az", distance))
-    current = pick_rows(blocks, quotient)
-    farther = pick_rows(blocks[1:] + [jnp.zeros_like(primitive)], quotient)
-    return roll_rows(farther, current, remainder)
+    joined = jnp.concatenate(blocks[::-1], axis=3)
+    width = joined.shape[3]
+    source = lax.broadcasted_iota(jnp.int32, (1, width, cell_count), 1)
+    target = lax.broadcasted_iota(jnp.int32, (1, width, cell_count), 2)
+    start = far * cell_count - shifts
+    pick = (source == target + start[:, None, None]).astype(jnp.float32)
+    return jnp.einsum(
+        "fitk,ikc->fitc",
+        joined,
+        pick,
+        precision=lax.Precision.HIGHEST,
+        preferred_element_type=jnp.float32,
+    )
 
 
 def on_device(fields, shifts):
@@ -213,21 +229,22 @@
     cell_count = fields.shape[3]
     rad_index = lax.axis_index("rad")
     total_rows = row_count * lax.axis_size("rad")
-    inner_rows = (rad_index * row_count + jnp.arange(row_count, dtype=jnp.int32)).astype(
-        jnp.float32
-    )
-    courant_inner = courant_profile(inner_rows, total_rows)
-    quotient = shifts // cell_count
-    remainder = shifts - quotient * cell_count
-    current = fields
-    initial = to_conserved(current)
-    section_one = initial + tendency(extend_thin(current), courant_inner)
-    section_one_prim = to_primitive(section_one)
+    half = HALO // 2
+    wide_rows = (
+        rad_index * row_count - half + jnp.arange(row_count + HALO, dtype=jnp.int32)
+    ).astype(jnp.float32)
+    courant_wide = courant_profile(wide_rows, total_rows)
+    courant_inner = courant_wide[half : half + row_count]
+    wide = extend_wide(fields, HALO)
+    initial_wide = to_conserved(wide[:, half:-half, :, half:-half])
+    section_one = initial_wide + tendency(wide, courant_wide)
+    section_one_prim = clamp_rows(to_primitive(section_one), half)
+    initial = initial_wide[:, half:-half, :, half:-half]
+    section_one_inner = section_one[:, half:-half, :, half:-half]
     section_two = 0.5 * initial + 0.5 * (
-        section_one + tendency(extend_thin(section_one_prim), courant_inner)
-    )
-    current = shift_rows(to_primitive(section_two), quotient, remainder)
-    return current
+        section_one_inner + tendency(section_one_prim, courant_inner)
+    )
+    return shift_rows(to_primitive(section_two), shifts)
 
 
 def solution(mesh):

time: 138 us -> 120 us (0.87)
  the two profiles are of different devices: /device:TPU:81 before, /device:TPU:25 now
where the time goes in v1:
time: 120 us
  starting transfers between devices  48.5 us (40%)
  waiting for transfers between devices  37.3 us (31%)
  other arithmetic  27.2 us (23%)
  local copies, waits for them, and re-layouts  3.55 us (3%)
  matrix products  2.46 us (2%)
    ppermute x3, waiting for transfers between devices, shifted(): return lax.ppermute(block, axis, route)  35.1 us
    ppermute x1, starting transfers between devices, extend_wide(): from_right = lax.ppermute(x[..., :width], 'az', ring_pairs(n_az, -1, True))  9.67 us
    unnamed x27, other arithmetic  8.63 us
    ppermute x1, starting transfers between devices, extend_wide(): lax.ppermute(bottom[..., :width], both, diagonal_pairs(n_rad, n_az, -1, -1))  7.66 us
    min x6, other arithmetic, edge_states(): jnp.clip(interface, jnp.minimum(centre, follow), jnp.maximum(centre, foll...  7.34 us
    ppermute x3, starting transfers between devices, shifted(): return lax.ppermute(block, axis, route)  7.16 us
    ppermute x1, starting transfers between devices, extend_wide(): lax.ppermute(top[..., -width:], both, diagonal_pairs(n_rad, n_az, 1, 1))  7.06 us
    ppermute x1, starting transfers between devices, extend_wide(): lax.ppermute(top[..., :width], both, diagonal_pairs(n_rad, n_az, 1, -1))  6.71 us
  transfers between devices with their start and end apart: 11, of which 3 were waited for; matrix products, arithmetic and copies ran while one was open for 2% of the time, Pallas kernels for 0%

profile of v1, /device:TPU:25, one launch (start us, length us, event | category | flops | bytes accessed | tf_op | source)
XLA Modules:
  0.0 119.8 jit_solution(9317680871611074128)
XLA Ops:
  0.0 1.0 fusion.224
  1.1 4.0 %collective-permute-start = (f32[5,6,8,6]{3,2,0,1:T(8,128)S(1)}, f32[5,6,8,6]{3,2,0,1:T(8,128)S(1)}, u32[]{:S(2)}, u32[]{:S(2)}) collective-permute-start(f32[5,6,8,6]{3,2,0,1:T(8,128)S(1)} %get-tuple-element.31), channel_id=1, source_target_pairs={{0,1},{1,2},{2,3},{3,4},{4,5},{5,6},{6,7},{7,8},{8,9},{9,10},{10,1... | collective-permute-start | bytes 17288 | tf_op jit(solution)/shard_map/ppermute | solution.py:193
  5.1 7.1 %collective-permute-start.2 = (f32[5,6,8,6]{3,2,0,1:T(8,128)S(1)}, f32[5,6,8,6]{3,2,0,1:T(8,128)S(1)}, u32[]{:S(2)}, u32[]{:S(2)}) collective-permute-start(f32[5,6,8,6]{3,2,0,1:T(8,128)S(1)} %get-tuple-element.31), channel_id=1, source_target_pairs={{0,25},{1,26},{2,27},{3,28},{4,29},{5,30},{6,31},{7,32},{8,33},{9,... | collective-permute-start | bytes 17288 | tf_op jit(solution)/shard_map/ppermute | solution.py:196
  12.1 9.7 %collective-permute-start.1 = (f32[5,6,8,6]{3,2,0,1:T(8,128)S(1)}, f32[5,6,8,6]{3,2,0,1:T(8,128)S(1)}, u32[]{:S(2)}, u32[]{:S(2)}) collective-permute-start(f32[5,6,8,6]{3,2,0,1:T(8,128)S(1)} %get-tuple-element.32), channel_id=1, source_target_pairs={{0,23},{1,0},{2,1},{3,2},{4,3},{5,4},{6,5},{7,6},{8,7},{9,8},{10,9... | collective-permute-start | bytes 17288 | tf_op jit(solution)/shard_map/ppermute | solution.py:194
  21.8 6.7 %collective-permute-start.4 = (f32[5,6,8,6]{3,2,0,1:T(8,128)S(1)}, f32[5,6,8,6]{3,2,0,1:T(8,128)S(1)}, u32[]{:S(2)}, u32[]{:S(2)}) collective-permute-start(f32[5,6,8,6]{3,2,0,1:T(8,128)S(1)} %get-tuple-element.32), channel_id=1, source_target_pairs={{0,47},{1,24},{2,25},{3,26},{4,27},{5,28},{6,29},{7,30},{8,31},{9,... | collective-permute-start | bytes 17288 | tf_op jit(solution)/shard_map/ppermute | solution.py:197
  28.5 1.0 copy.9
  29.5 2.0 %collective-permute-start.3 = (f32[5,6,8,256]{3,2,0,1:T(8,128)S(1)}, f32[5,6,8,256]{3,2,0,1:T(8,128)S(1)}, u32[]{:S(2)}, u32[]{:S(2)}) collective-permute-start(f32[5,6,8,256]{3,2,0,1:T(8,128)S(1)} %copy.9), channel_id=1, source_target_pairs={{0,24},{24,48},{48,72},{72,96},{96,120},{120,144},{144,168},{168,1... | collective-permute-start | bytes 737288 | tf_op jit(solution)/shard_map/ppermute | solution.py:191
  31.6 1.9 %collective-permute-start.5 = (f32[5,6,8,6]{3,2,0,1:T(8,128)S(1)}, f32[5,6,8,6]{3,2,0,1:T(8,128)S(1)}, u32[]{:S(2)}, u32[]{:S(2)}) collective-permute-start(f32[5,6,8,6]{3,2,0,1:T(8,128)S(1)} %get-tuple-element.31), channel_id=1, source_target_pairs={{24,1},{25,2},{26,3},{27,4},{28,5},{29,6},{30,7},{31,8},{32,9},{33... | collective-permute-start | bytes 17288 | tf_op jit(solution)/shard_map/ppermute | solution.py:198
  33.6 2.3 %collective-permute-start.6 = (f32[5,6,8,256]{3,2,0,1:T(8,128)S(1)}, f32[5,6,8,256]{3,2,0,1:T(8,128)S(1)}, u32[]{:S(2)}, u32[]{:S(2)}) collective-permute-start(f32[5,6,8,256]{3,2,0,1:T(8,128)S(1)} %copy.9), channel_id=1, source_target_pairs={{24,0},{48,24},{72,48},{96,72},{120,96},{144,120},{168,144},{192,1... | collective-permute-start | bytes 737288 | tf_op jit(solution)/shard_map/ppermute | solution.py:192
  35.9 0.9 maximum_bitcast_fusion.2
  36.8 7.7 %collective-permute-start.7 = (f32[5,6,8,6]{3,2,0,1:T(8,128)S(1)}, f32[5,6,8,6]{3,2,0,1:T(8,128)S(1)}, u32[]{:S(2)}, u32[]{:S(2)}) collective-permute-start(f32[5,6,8,6]{3,2,0,1:T(8,128)S(1)} %get-tuple-element.32), channel_id=1, source_target_pairs={{24,23},{25,0},{26,1},{27,2},{28,3},{29,4},{30,5},{31,6},{32,7},{3... | collective-permute-start | bytes 17288 | tf_op jit(solution)/shard_map/ppermute | solution.py:199
  44.7 2.2 %collective-permute-done.7 = f32[5,6,8,6]{3,2,0,1:T(8,128)S(1)} collective-permute-done((f32[5,6,8,6]{3,2,0,1:T(8,128)S(1)}, f32[5,6,8,6]{3,2,0,1:T(8,128)S(1)}, u32[]{:S(2)}, u32[]{:S(2)}) %collective-permute-start.7) | collective-permute-done | bytes 5792 | tf_op jit(solution)/shard_map/ppermute | solution.py:199
  47.4 1.0 fusion.30
  49.3 0.8 subtract_select_fusion.2
  52.9 4.2 %fusion.10 = f32[5,12,11,262]{3,2,0,1:T(8,128)S(1)} fusion(f32[5,18,3,268]{3,2,0,1:T(4,128)S(1)} %reshape.32, f32[5,6,8,268]{3,2,0,1:T(8,128)S(1)} %maximum_select_fusion.1, f32[5,6,8,268]{3,2,0,1:T(8,128)S(1)} %maximum_select_fusion, f32[5,6,8,6]{3,2,0,1:T(8,128)S(1)} %collective-permute-done.1, f32[5,6,8,6]{3,2,0,1:T(8,128)S(1)} %collective-permute-done, ...), kind=kLoop, calls=%fused_computation.13 | loop fusion | flops 3285480 | bytes 3425760 | tf_op jit(solution)/shard_map/jit(clip)/min | solution.py:29
  57.1 1.5 %subtract_select_fusion = (f32[5,12,10,262]{3,2,0,1:T(8,128)S(1)}, f32[5,12,10,262]{3,2,0,1:T(8,128)S(1)}) fusion(f32[5,18,14,268]{3,2,0,1:T(8,128)S(1)} %pad_maximum_fusion, f32[5,12,11,262]{3,2,0,1:T(8,128)S(1)} %fusion.10), kind=kLoop, calls=%fused_computation.24 | loop fusion | flops 3930000 | bytes 3144000 | tf_op jit(solution)/shard_map/jit(_where)/select_n | solution.py:39
  61.4 1.0 fusion.90
  62.5 0.7 subtract_select_fusion.4
  74.3 1.9 %collective-permute-start.10 = (f32[5,6,8,256]{3,2,0,1:T(8,128)S(1)}, f32[5,6,8,256]{3,2,0,1:T(8,128)S(1)}, u32[]{:S(2)}, u32[]{:S(2)}) collective-permute-start(f32[5,6,8,256]{3,2,0,1:T(8,128)S(1)} %pad_maximum_fusion.23), channel_id=1, source_target_pairs={{23,0},{0,1},{1,2},{2,3},{3,4},{4,5},{5,6},{6,7},{7,8},{8,9},{9,10... | collective-permute-start | bytes 737288 | tf_op jit(solution)/shard_map/ppermute | solution.py:15
  76.2 1.9 %collective-permute-start.8 = (f32[5,6,8,256]{3,2,0,1:T(8,128)S(1)}, f32[5,6,8,256]{3,2,0,1:T(8,128)S(1)}, u32[]{:S(2)}, u32[]{:S(2)}) collective-permute-start(f32[5,6,8,256]{3,2,0,1:T(8,128)S(1)} %pad_maximum_fusion.23), channel_id=1, source_target_pairs={{21,0},{22,1},{23,2},{0,3},{1,4},{2,5},{3,6},{4,7},{5,8},{6,9},{7,... | collective-permute-start | bytes 737288 | tf_op jit(solution)/shard_map/ppermute | solution.py:15
  78.2 3.3 %collective-permute-start.9 = (f32[5,6,8,256]{3,2,0,1:T(8,128)S(1)}, f32[5,6,8,256]{3,2,0,1:T(8,128)S(1)}, u32[]{:S(2)}, u32[]{:S(2)}) collective-permute-start(f32[5,6,8,256]{3,2,0,1:T(8,128)S(1)} %pad_maximum_fusion.23), channel_id=1, source_target_pairs={{22,0},{23,1},{0,2},{1,3},{2,4},{3,5},{4,6},{5,7},{6,8},{7,9},{8,1... | collective-permute-start | bytes 737288 | tf_op jit(solution)/shard_map/ppermute | solution.py:15
  81.5 14.2 %collective-permute-done.10 = f32[5,6,8,256]{3,2,0,1:T(8,128)S(1)} collective-permute-done((f32[5,6,8,256]{3,2,0,1:T(8,128)S(1)}, f32[5,6,8,256]{3,2,0,1:T(8,128)S(1)}, u32[]{:S(2)}, u32[]{:S(2)}) %collective-permute-start.10) | collective-permute-done | bytes 245792 | tf_op jit(solution)/shard_map/ppermute | solution.py:15
  95.7 20.9 %collective-permute-done.9 = f32[5,6,8,256]{3,2,0,1:T(8,128)S(1)} collective-permute-done((f32[5,6,8,256]{3,2,0,1:T(8,128)S(1)}, f32[5,6,8,256]{3,2,0,1:T(8,128)S(1)}, u32[]{:S(2)}, u32[]{:S(2)}) %collective-permute-start.9) | collective-permute-done | bytes 245792 | tf_op jit(solution)/shard_map/ppermute | solution.py:15
  116.6 2.5 %fusion.13 = f32[5,6,8,256]{3,2,0,1:T(8,128)S(1)} fusion(s32[6]{0:T(128)S(1)} %broadcast_subtract_fusion, f32[1,6,8,256]{3,2,0,1:T(8,128)S(1)} %fusion.218, f32[3,6,8,256]{3,2,0,1:T(8,128)S(1)} %slice_divide_fusion.1, f32[1,6,8,256]{3,2,0,1:T(8,128)S(1)} %get-tuple-element.29, f32[5,6,8,256]{3,2,0,1:T(8,128)S(1)} %collective-permute-done.10, ...), kind=kOutput, calls=%fused_computation.32 | convolution fusion | flops 759349248 | bytes 1228824 | tf_op jit(solution)/shard_map/fitk,ikc->fitc/dot_general | solution.py:218
  (85 shorter events, 18.6 us)
Async XLA Ops:
  1.1 30.6 %collective-permute-start = (f32[5,6,8,6]{3,2,0,1:T(8,128)S(1)}, f32[5,6,8,6]{3,2,0,1:T(8,128)S(1)}, u32[]{:S(2)}, u32[]{:S(2)}) collective-permute-start(f32[5,6,8,6]{3,2,0,1:T(8,128)S(1)} %get-tuple-element.31), channel_id=1, source_target_pairs={{0,1},{1,2},{2,3},{3,4},{4,5},{5,6},{6,7},{7,8},{8,9},{9,10},{10,1... | collective-permute-start | bytes 17288 | tf_op jit(solution)/shard_map/ppermute | solution.py:193
  5.1 31.7 %collective-permute-start.2 = (f32[5,6,8,6]{3,2,0,1:T(8,128)S(1)}, f32[5,6,8,6]{3,2,0,1:T(8,128)S(1)}, u32[]{:S(2)}, u32[]{:S(2)}) collective-permute-start(f32[5,6,8,6]{3,2,0,1:T(8,128)S(1)} %get-tuple-element.31), channel_id=1, source_target_pairs={{0,25},{1,26},{2,27},{3,28},{4,29},{5,30},{6,31},{7,32},{8,33},{9,... | collective-permute-start | bytes 17288 | tf_op jit(solution)/shard_map/ppermute | solution.py:196
  12.1 35.0 %copy-start = (f32[5,6,8,256]{3,2,1,0:T(8,128)S(1)}, f32[5,6,8,256]{3,2,1,0:T(8,128)}, u32[]{:S(2)}) copy-start(f32[5,6,8,256]{3,2,1,0:T(8,128)} %param.2) | copy-start | bytes 737284
  12.1 21.4 %collective-permute-start.1 = (f32[5,6,8,6]{3,2,0,1:T(8,128)S(1)}, f32[5,6,8,6]{3,2,0,1:T(8,128)S(1)}, u32[]{:S(2)}, u32[]{:S(2)}) collective-permute-start(f32[5,6,8,6]{3,2,0,1:T(8,128)S(1)} %get-tuple-element.32), channel_id=1, source_target_pairs={{0,23},{1,0},{2,1},{3,2},{4,3},{5,4},{6,5},{7,6},{8,7},{9,8},{10,9... | collective-permute-start | bytes 17288 | tf_op jit(solution)/shard_map/ppermute | solution.py:194
  21.8 22.6 %collective-permute-start.4 = (f32[5,6,8,6]{3,2,0,1:T(8,128)S(1)}, f32[5,6,8,6]{3,2,0,1:T(8,128)S(1)}, u32[]{:S(2)}, u32[]{:S(2)}) collective-permute-start(f32[5,6,8,6]{3,2,0,1:T(8,128)S(1)} %get-tuple-element.32), channel_id=1, source_target_pairs={{0,47},{1,24},{2,25},{3,26},{4,27},{5,28},{6,29},{7,30},{8,31},{9,... | collective-permute-start | bytes 17288 | tf_op jit(solution)/shard_map/ppermute | solution.py:197
  29.5 15.0 %collective-permute-start.3 = (f32[5,6,8,256]{3,2,0,1:T(8,128)S(1)}, f32[5,6,8,256]{3,2,0,1:T(8,128)S(1)}, u32[]{:S(2)}, u32[]{:S(2)}) collective-permute-start(f32[5,6,8,256]{3,2,0,1:T(8,128)S(1)} %copy.9), channel_id=1, source_target_pairs={{0,24},{24,48},{48,72},{72,96},{96,120},{120,144},{144,168},{168,1... | collective-permute-start | bytes 737288 | tf_op jit(solution)/shard_map/ppermute | solution.py:191
  31.6 13.1 %collective-permute-start.5 = (f32[5,6,8,6]{3,2,0,1:T(8,128)S(1)}, f32[5,6,8,6]{3,2,0,1:T(8,128)S(1)}, u32[]{:S(2)}, u32[]{:S(2)}) collective-permute-start(f32[5,6,8,6]{3,2,0,1:T(8,128)S(1)} %get-tuple-element.31), channel_id=1, source_target_pairs={{24,1},{25,2},{26,3},{27,4},{28,5},{29,6},{30,7},{31,8},{32,9},{33... | collective-permute-start | bytes 17288 | tf_op jit(solution)/shard_map/ppermute | solution.py:198
  33.6 13.4 %collective-permute-start.6 = (f32[5,6,8,256]{3,2,0,1:T(8,128)S(1)}, f32[5,6,8,256]{3,2,0,1:T(8,128)S(1)}, u32[]{:S(2)}, u32[]{:S(2)}) collective-permute-start(f32[5,6,8,256]{3,2,0,1:T(8,128)S(1)} %copy.9), channel_id=1, source_target_pairs={{24,0},{48,24},{72,48},{96,72},{120,96},{144,120},{168,144},{192,1... | collective-permute-start | bytes 737288 | tf_op jit(solution)/shard_map/ppermute | solution.py:192
  36.8 10.1 %collective-permute-start.7 = (f32[5,6,8,6]{3,2,0,1:T(8,128)S(1)}, f32[5,6,8,6]{3,2,0,1:T(8,128)S(1)}, u32[]{:S(2)}, u32[]{:S(2)}) collective-permute-start(f32[5,6,8,6]{3,2,0,1:T(8,128)S(1)} %get-tuple-element.32), channel_id=1, source_target_pairs={{24,23},{25,0},{26,1},{27,2},{28,3},{29,4},{30,5},{31,6},{32,7},{3... | collective-permute-start | bytes 17288 | tf_op jit(solution)/shard_map/ppermute | solution.py:199
  73.9 7.6 %copy-start.1 = (s32[6]{0:T(128)S(1)}, s32[6]{0:T(128)}, u32[]{:S(2)}) copy-start(s32[6]{0:T(128)} %param.3) | copy-start | bytes 76
  74.3 21.4 %collective-permute-start.10 = (f32[5,6,8,256]{3,2,0,1:T(8,128)S(1)}, f32[5,6,8,256]{3,2,0,1:T(8,128)S(1)}, u32[]{:S(2)}, u32[]{:S(2)}) collective-permute-start(f32[5,6,8,256]{3,2,0,1:T(8,128)S(1)} %pad_maximum_fusion.23), channel_id=1, source_target_pairs={{23,0},{0,1},{1,2},{2,3},{3,4},{4,5},{5,6},{6,7},{7,8},{8,9},{9,10... | collective-permute-start | bytes 737288 | tf_op jit(solution)/shard_map/ppermute | solution.py:15
  76.2 19.5 %collective-permute-start.8 = (f32[5,6,8,256]{3,2,0,1:T(8,128)S(1)}, f32[5,6,8,256]{3,2,0,1:T(8,128)S(1)}, u32[]{:S(2)}, u32[]{:S(2)}) collective-permute-start(f32[5,6,8,256]{3,2,0,1:T(8,128)S(1)} %pad_maximum_fusion.23), channel_id=1, source_target_pairs={{21,0},{22,1},{23,2},{0,3},{1,4},{2,5},{3,6},{4,7},{5,8},{6,9},{7,... | collective-permute-start | bytes 737288 | tf_op jit(solution)/shard_map/ppermute | solution.py:15
  78.2 38.4 %collective-permute-start.9 = (f32[5,6,8,256]{3,2,0,1:T(8,128)S(1)}, f32[5,6,8,256]{3,2,0,1:T(8,128)S(1)}, u32[]{:S(2)}, u32[]{:S(2)}) collective-permute-start(f32[5,6,8,256]{3,2,0,1:T(8,128)S(1)} %pad_maximum_fusion.23), channel_id=1, source_target_pairs={{22,0},{23,1},{0,2},{1,3},{2,4},{3,5},{4,6},{5,7},{6,8},{7,9},{8,1... | collective-permute-start | bytes 737288 | tf_op jit(solution)/shard_map/ppermute | solution.py:15

commit v2 on v1

--- a/solution.py
+++ b/solution.py
@@ -112,11 +112,10 @@
     return cut_along(flux_all, 1, faces, along) - cut_along(flux_all, 0, faces - 1, along)
 
 
-def tendency(window, courant_rows):
-    padded = jnp.pad(window, ((0, 0), (0, 0), (3, 3), (0, 0)), mode="edge")
-    radial_term = flux_difference(padded[:, :, 3:-3, 3:-3], 1, 1)
-    polar_term = flux_difference(padded[:, 3:-3, :, 3:-3], 2, 2)
-    azimuth_term = flux_difference(padded[:, 3:-3, 3:-3, :], 3, 3)
+def tendency(along_rad, along_az, inner, courant_rows):
+    radial_term = flux_difference(along_rad, 1, 1)
+    polar_term = flux_difference(jnp.pad(inner, ((0, 0), (0, 0), (3, 3), (0, 0)), mode="edge"), 2, 2)
+    azimuth_term = flux_difference(along_az, 3, 3)
     return -(
         COURANT_RADIAL * radial_term
         + COURANT_POLAR * polar_term
@@ -148,23 +147,13 @@
 
 
 MAX_SHIFT = 768
-HALO = 6
+HALO = 3
 
 
 def ring_pairs(count, step, wrap):
     if wrap:
         return [(i, (i + step) % count) for i in range(count)]
     return [(i, i + step) for i in range(count) if 0 <= i + step < count]
-
-
-def diagonal_pairs(n_rad, n_az, rad_step, az_step):
-    pairs = []
-    for r in range(n_rad):
-        if not 0 <= r + rad_step < n_rad:
-            continue
-        for a in range(n_az):
-            pairs.append((r * n_az + a, (r + rad_step) * n_az + (a + az_step) % n_az))
-    return pairs
 
 
 def clamp_rows(block, depth):
@@ -184,23 +173,20 @@
     return jnp.concatenate([lower, block[:, depth : rows - depth], upper], axis=1)
 
 
-def extend_wide(x, width):
+def halos(x, width):
     n_rad, n_az = lax.axis_size("rad"), lax.axis_size("az")
-    top = x[:, -width:]
-    bottom = x[:, :width]
-    from_below = lax.ppermute(top, "rad", ring_pairs(n_rad, 1, False))
-    from_above = lax.ppermute(bottom, "rad", ring_pairs(n_rad, -1, False))
+    from_below = lax.ppermute(x[:, -width:], "rad", ring_pairs(n_rad, 1, False))
+    from_above = lax.ppermute(x[:, :width], "rad", ring_pairs(n_rad, -1, False))
     from_left = lax.ppermute(x[..., -width:], "az", ring_pairs(n_az, 1, True))
     from_right = lax.ppermute(x[..., :width], "az", ring_pairs(n_az, -1, True))
-    both = ("rad", "az")
-    low_left = lax.ppermute(top[..., -width:], both, diagonal_pairs(n_rad, n_az, 1, 1))
-    low_right = lax.ppermute(top[..., :width], both, diagonal_pairs(n_rad, n_az, 1, -1))
-    up_left = lax.ppermute(bottom[..., -width:], both, diagonal_pairs(n_rad, n_az, -1, 1))
-    up_right = lax.ppermute(bottom[..., :width], both, diagonal_pairs(n_rad, n_az, -1, -1))
-    lower = jnp.concatenate([low_left, from_below, low_right], axis=3)
-    middle = jnp.concatenate([from_left, x, from_right], axis=3)
-    upper = jnp.concatenate([up_left, from_above, up_right], axis=3)
-    return clamp_rows(jnp.concatenate([lower, middle, upper], axis=1), width)
+    along_rad = clamp_rows(jnp.concatenate([from_below, x, from_above], axis=1), width)
+    along_az = jnp.concatenate([from_left, x, from_right], axis=3)
+    return along_rad, along_az
+
+
+def change(x, courant_rows):
+    along_rad, along_az = halos(x, HALO)
+    return tendency(along_rad, along_az, x, courant_rows)
 
 
 def shift_rows(primitive, shifts):
@@ -208,7 +194,10 @@
     far = -(-MAX_SHIFT // cell_count)
     blocks = [primitive]
     for distance in range(1, far + 1):
-        blocks.append(shifted(primitive, "az", distance))
+        if distance <= 2:
+            blocks.append(shifted(primitive, "az", distance))
+        else:
+            blocks.append(shifted(blocks[-1], "az", 1))
     joined = jnp.concatenate(blocks[::-1], axis=3)
     width = joined.shape[3]
     source = lax.broadcasted_iota(jnp.int32, (1, width, cell_count), 1)
@@ -226,24 +215,16 @@
 
 def on_device(fields, shifts):
     row_count = fields.shape[1]
-    cell_count = fields.shape[3]
     rad_index = lax.axis_index("rad")
     total_rows = row_count * lax.axis_size("rad")
-    half = HALO // 2
-    wide_rows = (
-        rad_index * row_count - half + jnp.arange(row_count + HALO, dtype=jnp.int32)
-    ).astype(jnp.float32)
-    courant_wide = courant_profile(wide_rows, total_rows)
-    courant_inner = courant_wide[half : half + row_count]
-    wide = extend_wide(fields, HALO)
-    initial_wide = to_conserved(wide[:, half:-half, :, half:-half])
-    section_one = initial_wide + tendency(wide, courant_wide)
-    section_one_prim = clamp_rows(to_primitive(section_one), half)
-    initial = initial_wide[:, half:-half, :, half:-half]
-    section_one_inner = section_one[:, half:-half, :, half:-half]
-    section_two = 0.5 * initial + 0.5 * (
-        section_one_inner + tendency(section_one_prim, courant_inner)
-    )
+    inner_rows = (rad_index * row_count + jnp.arange(row_count, dtype=jnp.int32)).astype(
+        jnp.float32
+    )
+    courant_inner = courant_profile(inner_rows, total_rows)
+    initial = to_conserved(fields)
+    section_one = initial + change(fields, courant_inner)
+    section_one_prim = to_primitive(section_one)
+    section_two = 0.5 * initial + 0.5 * (section_one + change(section_one_prim, courant_inner))
     return shift_rows(to_primitive(section_two), shifts)
 
 

time: 120 us -> 90.9 us (0.76)
  the two profiles are of different devices: /device:TPU:25 before, /device:TPU:56 now
where the time goes in v2:
time: 90.9 us; the launch traced here: 89.2 us
  starting transfers between devices  45.5 us (50%)
  waiting for transfers between devices  26.7 us (29%)
  other arithmetic  11.6 us (13%)
  matrix products  2.46 us (3%)
  local copies, waits for them, and re-layouts  2.18 us (2%)
    ppermute x3, waiting for transfers between devices, shifted(): return lax.ppermute(block, axis, route)  26.4 us
    ppermute x2, starting transfers between devices, halos(): from_right = lax.ppermute(x[..., :width], 'az', ring_pairs(n_az, -1, True))  22.4 us
    ppermute x2, starting transfers between devices, halos(): from_above = lax.ppermute(x[:, :width], 'rad', ring_pairs(n_rad, -1, False))  7.28 us
    ppermute x2, starting transfers between devices, halos(): from_left = lax.ppermute(x[..., -width:], 'az', ring_pairs(n_az, 1, True))  6.2 us
    ppermute x3, starting transfers between devices, shifted(): return lax.ppermute(block, axis, route)  5.75 us
    unnamed x27, other arithmetic  4.96 us
    ppermute x2, starting transfers between devices, halos(): from_below = lax.ppermute(x[:, -width:], 'rad', ring_pairs(n_rad, 1, False))  3.84 us
    dot_general x1, matrix products, shift_rows(): jnp.einsum('fitk,ikc->fitc', joined, pick, precision=lax.Precision.HIGHES...  2.46 us
  transfers between devices with their start and end apart: 11, of which 4 were waited for; matrix products, arithmetic and copies ran while one was open for 10% of the time, Pallas kernels for 0%

profile of v2, /device:TPU:56, one launch (start us, length us, event | category | flops | bytes accessed | tf_op | source)
XLA Modules:
  0.0 89.2 jit_solution(14779601256108328507)
XLA Ops:
  0.0 1.1 %fusion.213 = (f32[5,6,8,3]{3,2,0,1:T(8,128)S(1)}, f32[5,6,8,3]{3,2,0,1:T(8,128)S(1)}) fusion(f32[5,6,8,256]{3,2,1,0:T(8,128)} %param.2), kind=kLoop, calls=%fused_computation.413 | loop fusion | bytes 251520 | tf_op jit(solution)/shard_map/slice | solution.py:180
  1.1 4.3 %collective-permute-start.2 = (f32[5,6,8,3]{3,2,0,1:T(8,128)S(1)}, f32[5,6,8,3]{3,2,0,1:T(8,128)S(1)}, u32[]{:S(2)}, u32[]{:S(2)}) collective-permute-start(f32[5,6,8,3]{3,2,0,1:T(8,128)S(1)} %get-tuple-element.35), channel_id=1, source_target_pairs={{0,1},{1,2},{2,3},{3,4},{4,5},{5,6},{6,7},{7,8},{8,9},{9,10},{10,1... | collective-permute-start | bytes 8648 | tf_op jit(solution)/shard_map/ppermute | solution.py:180
  5.4 14.7 %collective-permute-start.3 = (f32[5,6,8,3]{3,2,0,1:T(8,128)S(1)}, f32[5,6,8,3]{3,2,0,1:T(8,128)S(1)}, u32[]{:S(2)}, u32[]{:S(2)}) collective-permute-start(f32[5,6,8,3]{3,2,0,1:T(8,128)S(1)} %get-tuple-element.36), channel_id=1, source_target_pairs={{0,23},{1,0},{2,1},{3,2},{4,3},{5,4},{6,5},{7,6},{8,7},{9,8},{10,9... | collective-permute-start | bytes 8648 | tf_op jit(solution)/shard_map/ppermute | solution.py:181
  20.1 1.9 %collective-permute-start = (f32[5,3,8,256]{3,2,0,1:T(8,128)S(1)}, f32[5,3,8,256]{3,2,0,1:T(8,128)S(1)}, u32[]{:S(2)}, u32[]{:S(2)}) collective-permute-start(f32[5,3,8,256]{3,2,0,1:T(8,128)S(1)} %get-tuple-element.31), channel_id=1, source_target_pairs={{0,24},{24,48},{48,72},{72,96},{96,120},{120,144},{144,168},{168,1... | collective-permute-start | bytes 368648 | tf_op jit(solution)/shard_map/ppermute | solution.py:178
  22.0 3.6 %collective-permute-start.1 = (f32[5,3,8,256]{3,2,0,1:T(8,128)S(1)}, f32[5,3,8,256]{3,2,0,1:T(8,128)S(1)}, u32[]{:S(2)}, u32[]{:S(2)}) collective-permute-start(f32[5,3,8,256]{3,2,0,1:T(8,128)S(1)} %get-tuple-element.32), channel_id=1, source_target_pairs={{24,0},{48,24},{72,48},{96,72},{120,96},{144,120},{168,144},{192,1... | collective-permute-start | bytes 368648 | tf_op jit(solution)/shard_map/ppermute | solution.py:179
  26.3 0.5 subtract_select_fusion.2
  27.8 0.4 fusion.96
  28.4 0.4 fusion.45
  28.8 0.4 subtract_select_fusion.6
  32.2 1.9 %collective-permute-start.4 = (f32[5,3,8,256]{3,2,0,1:T(8,128)S(1)}, f32[5,3,8,256]{3,2,0,1:T(8,128)S(1)}, u32[]{:S(2)}, u32[]{:S(2)}) collective-permute-start(f32[5,3,8,256]{3,2,0,1:T(8,128)S(1)} %get-tuple-element.21), channel_id=1, source_target_pairs={{0,24},{24,48},{48,72},{72,96},{96,120},{120,144},{144,168},{168,1... | collective-permute-start | bytes 368648 | tf_op jit(solution)/shard_map/ppermute | solution.py:178
  34.1 3.6 %collective-permute-start.5 = (f32[5,3,8,256]{3,2,0,1:T(8,128)S(1)}, f32[5,3,8,256]{3,2,0,1:T(8,128)S(1)}, u32[]{:S(2)}, u32[]{:S(2)}) collective-permute-start(f32[5,3,8,256]{3,2,0,1:T(8,128)S(1)} %get-tuple-element.22), channel_id=1, source_target_pairs={{24,0},{48,24},{72,48},{96,72},{120,96},{144,120},{168,144},{192,1... | collective-permute-start | bytes 368648 | tf_op jit(solution)/shard_map/ppermute | solution.py:179
  37.8 1.9 %collective-permute-start.6 = (f32[5,6,8,3]{3,2,0,1:T(8,128)S(1)}, f32[5,6,8,3]{3,2,0,1:T(8,128)S(1)}, u32[]{:S(2)}, u32[]{:S(2)}) collective-permute-start(f32[5,6,8,3]{3,2,0,1:T(8,128)S(1)} %get-tuple-element.25), channel_id=1, source_target_pairs={{0,1},{1,2},{2,3},{3,4},{4,5},{5,6},{6,7},{7,8},{8,9},{9,10},{10,1... | collective-permute-start | bytes 8648 | tf_op jit(solution)/shard_map/ppermute | solution.py:180
  39.7 7.7 %collective-permute-start.7 = (f32[5,6,8,3]{3,2,0,1:T(8,128)S(1)}, f32[5,6,8,3]{3,2,0,1:T(8,128)S(1)}, u32[]{:S(2)}, u32[]{:S(2)}) collective-permute-start(f32[5,6,8,3]{3,2,0,1:T(8,128)S(1)} %get-tuple-element.26), channel_id=1, source_target_pairs={{0,23},{1,0},{2,1},{3,2},{4,3},{5,4},{6,5},{7,6},{8,7},{9,8},{10,9... | collective-permute-start | bytes 8648 | tf_op jit(solution)/shard_map/ppermute | solution.py:181
  47.8 0.5 subtract_select_fusion
  50.2 0.4 fusion.53
  50.5 0.4 subtract_select_fusion.4
  53.8 1.9 %collective-permute-start.8 = (f32[5,6,8,256]{3,2,0,1:T(8,128)S(1)}, f32[5,6,8,256]{3,2,0,1:T(8,128)S(1)}, u32[]{:S(2)}, u32[]{:S(2)}) collective-permute-start(f32[5,6,8,256]{3,2,0,1:T(8,128)S(1)} %pad_maximum_fusion.7), channel_id=1, source_target_pairs={{22,0},{23,1},{0,2},{1,3},{2,4},{3,5},{4,6},{5,7},{6,8},{7,9},{8,1... | collective-permute-start | bytes 737288 | tf_op jit(solution)/shard_map/ppermute | solution.py:15
  55.7 1.9 %collective-permute-start.10 = (f32[5,6,8,256]{3,2,0,1:T(8,128)S(1)}, f32[5,6,8,256]{3,2,0,1:T(8,128)S(1)}, u32[]{:S(2)}, u32[]{:S(2)}) collective-permute-start(f32[5,6,8,256]{3,2,0,1:T(8,128)S(1)} %pad_maximum_fusion.7), channel_id=1, source_target_pairs={{23,0},{0,1},{1,2},{2,3},{3,4},{4,5},{5,6},{6,7},{7,8},{8,9},{9,10... | collective-permute-start | bytes 737288 | tf_op jit(solution)/shard_map/ppermute | solution.py:15
  57.6 16.7 %collective-permute-done.8 = f32[5,6,8,256]{3,2,0,1:T(8,128)S(1)} collective-permute-done((f32[5,6,8,256]{3,2,0,1:T(8,128)S(1)}, f32[5,6,8,256]{3,2,0,1:T(8,128)S(1)}, u32[]{:S(2)}, u32[]{:S(2)}) %collective-permute-start.8) | collective-permute-done | bytes 245792 | tf_op jit(solution)/shard_map/ppermute | solution.py:15
  74.3 1.9 %collective-permute-start.9 = (f32[5,6,8,256]{3,2,0,1:T(8,128)S(1)}, f32[5,6,8,256]{3,2,0,1:T(8,128)S(1)}, u32[]{:S(2)}, u32[]{:S(2)}) collective-permute-start(f32[5,6,8,256]{3,2,0,1:T(8,128)S(1)} %collective-permute-done.8), channel_id=1, source_target_pairs={{23,0},{0,1},{1,2},{2,3},{3,4},{4,5},{5,6},{6,7},{7,8},{8,9},{9,10... | collective-permute-start | bytes 737288 | tf_op jit(solution)/shard_map/ppermute | solution.py:15
  76.2 1.3 %collective-permute-done.10 = f32[5,6,8,256]{3,2,0,1:T(8,128)S(1)} collective-permute-done((f32[5,6,8,256]{3,2,0,1:T(8,128)S(1)}, f32[5,6,8,256]{3,2,0,1:T(8,128)S(1)}, u32[]{:S(2)}, u32[]{:S(2)}) %collective-permute-start.10) | collective-permute-done | bytes 245792 | tf_op jit(solution)/shard_map/ppermute | solution.py:15
  77.6 8.4 %collective-permute-done.9 = f32[5,6,8,256]{3,2,0,1:T(8,128)S(1)} collective-permute-done((f32[5,6,8,256]{3,2,0,1:T(8,128)S(1)}, f32[5,6,8,256]{3,2,0,1:T(8,128)S(1)}, u32[]{:S(2)}, u32[]{:S(2)}) %collective-permute-start.9) | collective-permute-done | bytes 245792 | tf_op jit(solution)/shard_map/ppermute | solution.py:15
  86.0 2.5 %fusion.4 = f32[5,6,8,256]{3,2,0,1:T(8,128)S(1)} fusion(s32[6]{0:T(128)S(1)} %broadcast_subtract_fusion, f32[1,6,8,256]{3,2,0,1:T(8,128)S(1)} %fusion.197, f32[3,6,8,256]{3,2,0,1:T(8,128)S(1)} %slice_divide_fusion, f32[1,6,8,256]{3,2,0,1:T(8,128)S(1)} %get-tuple-element.17, f32[5,6,8,256]{3,2,0,1:T(8,128)S(1)} %collective-permute-done.10, ...), kind=kOutput, calls=%fused_computation.4 | convolution fusion | flops 759349248 | bytes 1228824 | tf_op jit(solution)/shard_map/fitk,ikc->fitc/dot_general | solution.py:207
  88.5 0.7 copy.50
  (88 shorter events, 9.5 us)
Async XLA Ops:
  0.0 20.1 %copy-start = (f32[5,6,8,256]{3,2,1,0:T(8,128)S(1)}, f32[5,6,8,256]{3,2,1,0:T(8,128)}, u32[]{:S(2)}) copy-start(f32[5,6,8,256]{3,2,1,0:T(8,128)} %param.2) | copy-start | bytes 737284
  1.1 27.1 %collective-permute-start.2 = (f32[5,6,8,3]{3,2,0,1:T(8,128)S(1)}, f32[5,6,8,3]{3,2,0,1:T(8,128)S(1)}, u32[]{:S(2)}, u32[]{:S(2)}) collective-permute-start(f32[5,6,8,3]{3,2,0,1:T(8,128)S(1)} %get-tuple-element.35), channel_id=1, source_target_pairs={{0,1},{1,2},{2,3},{3,4},{4,5},{5,6},{6,7},{7,8},{8,9},{9,10},{10,1... | collective-permute-start | bytes 8648 | tf_op jit(solution)/shard_map/ppermute | solution.py:180
  5.4 22.8 %collective-permute-start.3 = (f32[5,6,8,3]{3,2,0,1:T(8,128)S(1)}, f32[5,6,8,3]{3,2,0,1:T(8,128)S(1)}, u32[]{:S(2)}, u32[]{:S(2)}) collective-permute-start(f32[5,6,8,3]{3,2,0,1:T(8,128)S(1)} %get-tuple-element.36), channel_id=1, source_target_pairs={{0,23},{1,0},{2,1},{3,2},{4,3},{5,4},{6,5},{7,6},{8,7},{9,8},{10,9... | collective-permute-start | bytes 8648 | tf_op jit(solution)/shard_map/ppermute | solution.py:181
  20.1 10.3 %collective-permute-start = (f32[5,3,8,256]{3,2,0,1:T(8,128)S(1)}, f32[5,3,8,256]{3,2,0,1:T(8,128)S(1)}, u32[]{:S(2)}, u32[]{:S(2)}) collective-permute-start(f32[5,3,8,256]{3,2,0,1:T(8,128)S(1)} %get-tuple-element.31), channel_id=1, source_target_pairs={{0,24},{24,48},{48,72},{72,96},{96,120},{120,144},{144,168},{168,1... | collective-permute-start | bytes 368648 | tf_op jit(solution)/shard_map/ppermute | solution.py:178
  22.0 8.4 %collective-permute-start.1 = (f32[5,3,8,256]{3,2,0,1:T(8,128)S(1)}, f32[5,3,8,256]{3,2,0,1:T(8,128)S(1)}, u32[]{:S(2)}, u32[]{:S(2)}) collective-permute-start(f32[5,3,8,256]{3,2,0,1:T(8,128)S(1)} %get-tuple-element.32), channel_id=1, source_target_pairs={{24,0},{48,24},{72,48},{96,72},{120,96},{144,120},{168,144},{192,1... | collective-permute-start | bytes 368648 | tf_op jit(solution)/shard_map/ppermute | solution.py:179
  32.2 20.0 %collective-permute-start.4 = (f32[5,3,8,256]{3,2,0,1:T(8,128)S(1)}, f32[5,3,8,256]{3,2,0,1:T(8,128)S(1)}, u32[]{:S(2)}, u32[]{:S(2)}) collective-permute-start(f32[5,3,8,256]{3,2,0,1:T(8,128)S(1)} %get-tuple-element.21), channel_id=1, source_target_pairs={{0,24},{24,48},{48,72},{72,96},{96,120},{120,144},{144,168},{168,1... | collective-permute-start | bytes 368648 | tf_op jit(solution)/shard_map/ppermute | solution.py:178
  34.1 18.1 %collective-permute-start.5 = (f32[5,3,8,256]{3,2,0,1:T(8,128)S(1)}, f32[5,3,8,256]{3,2,0,1:T(8,128)S(1)}, u32[]{:S(2)}, u32[]{:S(2)}) collective-permute-start(f32[5,3,8,256]{3,2,0,1:T(8,128)S(1)} %get-tuple-element.22), channel_id=1, source_target_pairs={{24,0},{48,24},{72,48},{96,72},{120,96},{144,120},{168,144},{192,1... | collective-permute-start | bytes 368648 | tf_op jit(solution)/shard_map/ppermute | solution.py:179
  37.8 11.9 %collective-permute-start.6 = (f32[5,6,8,3]{3,2,0,1:T(8,128)S(1)}, f32[5,6,8,3]{3,2,0,1:T(8,128)S(1)}, u32[]{:S(2)}, u32[]{:S(2)}) collective-permute-start(f32[5,6,8,3]{3,2,0,1:T(8,128)S(1)} %get-tuple-element.25), channel_id=1, source_target_pairs={{0,1},{1,2},{2,3},{3,4},{4,5},{5,6},{6,7},{7,8},{8,9},{9,10},{10,1... | collective-permute-start | bytes 8648 | tf_op jit(solution)/shard_map/ppermute | solution.py:180
  39.7 10.3 %collective-permute-start.7 = (f32[5,6,8,3]{3,2,0,1:T(8,128)S(1)}, f32[5,6,8,3]{3,2,0,1:T(8,128)S(1)}, u32[]{:S(2)}, u32[]{:S(2)}) collective-permute-start(f32[5,6,8,3]{3,2,0,1:T(8,128)S(1)} %get-tuple-element.26), channel_id=1, source_target_pairs={{0,23},{1,0},{2,1},{3,2},{4,3},{5,4},{6,5},{7,6},{8,7},{9,8},{10,9... | collective-permute-start | bytes 8648 | tf_op jit(solution)/shard_map/ppermute | solution.py:181
  53.7 22.6 %copy-start.1 = (s32[6]{0:T(128)S(1)}, s32[6]{0:T(128)}, u32[]{:S(2)}) copy-start(s32[6]{0:T(128)} %param.3) | copy-start | bytes 76
  53.8 20.5 %collective-permute-start.8 = (f32[5,6,8,256]{3,2,0,1:T(8,128)S(1)}, f32[5,6,8,256]{3,2,0,1:T(8,128)S(1)}, u32[]{:S(2)}, u32[]{:S(2)}) collective-permute-start(f32[5,6,8,256]{3,2,0,1:T(8,128)S(1)} %pad_maximum_fusion.7), channel_id=1, source_target_pairs={{22,0},{23,1},{0,2},{1,3},{2,4},{3,5},{4,6},{5,7},{6,8},{7,9},{8,1... | collective-permute-start | bytes 737288 | tf_op jit(solution)/shard_map/ppermute | solution.py:15
  55.7 21.9 %collective-permute-start.10 = (f32[5,6,8,256]{3,2,0,1:T(8,128)S(1)}, f32[5,6,8,256]{3,2,0,1:T(8,128)S(1)}, u32[]{:S(2)}, u32[]{:S(2)}) collective-permute-start(f32[5,6,8,256]{3,2,0,1:T(8,128)S(1)} %pad_maximum_fusion.7), channel_id=1, source_target_pairs={{23,0},{0,1},{1,2},{2,3},{3,4},{4,5},{5,6},{6,7},{7,8},{8,9},{9,10... | collective-permute-start | bytes 737288 | tf_op jit(solution)/shard_map/ppermute | solution.py:15
  74.3 11.7 %collective-permute-start.9 = (f32[5,6,8,256]{3,2,0,1:T(8,128)S(1)}, f32[5,6,8,256]{3,2,0,1:T(8,128)S(1)}, u32[]{:S(2)}, u32[]{:S(2)}) collective-permute-start(f32[5,6,8,256]{3,2,0,1:T(8,128)S(1)} %collective-permute-done.8), channel_id=1, source_target_pairs={{23,0},{0,1},{1,2},{2,3},{3,4},{4,5},{5,6},{6,7},{7,8},{8,9},{9,10... | collective-permute-start | bytes 737288 | tf_op jit(solution)/shard_map/ppermute | solution.py:15

commit v3 on v2

--- a/solution.py
+++ b/solution.py
@@ -213,18 +213,43 @@
     )
 
 
+def extend_wide(x, width):
+    n_rad, n_az = lax.axis_size("rad"), lax.axis_size("az")
+    from_below = lax.ppermute(x[:, -width:], "rad", ring_pairs(n_rad, 1, False))
+    from_above = lax.ppermute(x[:, :width], "rad", ring_pairs(n_rad, -1, False))
+    rows = clamp_rows(jnp.concatenate([from_below, x, from_above], axis=1), width)
+    from_left = lax.ppermute(rows[..., -width:], "az", ring_pairs(n_az, 1, True))
+    from_right = lax.ppermute(rows[..., :width], "az", ring_pairs(n_az, -1, True))
+    return jnp.concatenate([from_left, rows, from_right], axis=3)
+
+
+def local_change(window, courant_rows):
+    depth = HALO
+    along_rad = window[..., depth:-depth]
+    along_az = window[:, depth:-depth]
+    inner = window[:, depth:-depth, :, depth:-depth]
+    return tendency(along_rad, along_az, inner, courant_rows)
+
+
 def on_device(fields, shifts):
     row_count = fields.shape[1]
     rad_index = lax.axis_index("rad")
     total_rows = row_count * lax.axis_size("rad")
-    inner_rows = (rad_index * row_count + jnp.arange(row_count, dtype=jnp.int32)).astype(
-        jnp.float32
-    )
-    courant_inner = courant_profile(inner_rows, total_rows)
-    initial = to_conserved(fields)
-    section_one = initial + change(fields, courant_inner)
-    section_one_prim = to_primitive(section_one)
-    section_two = 0.5 * initial + 0.5 * (section_one + change(section_one_prim, courant_inner))
+    depth = HALO
+    wide_rows = (
+        rad_index * row_count - depth + jnp.arange(row_count + 2 * depth, dtype=jnp.int32)
+    ).astype(jnp.float32)
+    courant_wide = courant_profile(wide_rows, total_rows)
+    courant_inner = courant_wide[depth : depth + row_count]
+    wide = extend_wide(fields, 2 * depth)
+    initial_wide = to_conserved(wide[:, depth:-depth, :, depth:-depth])
+    section_one = initial_wide + local_change(wide, courant_wide)
+    section_one_prim = clamp_rows(to_primitive(section_one), depth)
+    initial = initial_wide[:, depth:-depth, :, depth:-depth]
+    section_one_inner = section_one[:, depth:-depth, :, depth:-depth]
+    section_two = 0.5 * initial + 0.5 * (
+        section_one_inner + local_change(section_one_prim, courant_inner)
+    )
     return shift_rows(to_primitive(section_two), shifts)
 
 

time: 90.9 us -> 98.1 us (1.079); the launches traced: 89.2 us -> 97.7 us
  starting transfers between devices: 45.5 us -> 29.3 us
  waiting for transfers between devices: 26.7 us -> 39.5 us
  other arithmetic: 11.6 us -> 21.9 us
  local copies, waits for them, and re-layouts: 2.18 us -> 4.01 us
    ppermute x8 -> x4, starting transfers between devices: 39.7 us -> 23.6 us  [the longest x1 14.7 us: extend_wide(): lax.ppermute(rows[..., :width], 'az', ring_pairs(n_az, -1, True))]
    ppermute x8 -> x4, waiting for transfers between devices: 0.27 us -> 13.1 us  [the longest x1 7.14 us: extend_wide(): lax.ppermute(rows[..., -width:], 'az', ring_pairs(n_az, 1, True))]
    unnamed x27, other arithmetic: 4.96 us -> 8.63 us
    min x6, other arithmetic: 1.5 us -> 3.61 us  [edge_states(): jnp.clip(interface, jnp.minimum(centre, follow), jnp.maximum(centre, foll...]
    select_n x6, other arithmetic: 2.26 us -> 4.08 us  [edge_states(): jnp.where(spread * middle > spread * spread / 6.0, 3.0 * middle_cell - 2....]
    another operation x6, other arithmetic: 1.7 us -> 3.13 us  [riemann_flux(): return jnp.stack(merged)]
    unnamed x5 -> x6, local copies, waits for them, and re-layouts: 0.02 us -> 1.14 us
  transfers between devices with their start and end apart: 11 -> 7, of which waited for: 4 -> 7; matrix products, arithmetic and copies ran while one was open for 10% -> 1% of each run, Pallas kernels for 0% -> 0%
where the time goes in v3:
time: 98.1 us; the launch traced here: 97.7 us
  waiting for transfers between devices  39.5 us (40%)
  starting transfers between devices  29.3 us (30%)
  other arithmetic  21.9 us (22%)
  local copies, waits for them, and re-layouts  4.01 us (4%)
  matrix products  2.47 us (3%)
    ppermute x3, waiting for transfers between devices, shifted(): return lax.ppermute(block, axis, route)  26.4 us
    ppermute x1, starting transfers between devices, extend_wide(): lax.ppermute(rows[..., :width], 'az', ring_pairs(n_az, -1, True))  14.7 us
    unnamed x27, other arithmetic  8.63 us
    ppermute x1, waiting for transfers between devices, extend_wide(): lax.ppermute(rows[..., -width:], 'az', ring_pairs(n_az, 1, True))  7.14 us
    ppermute x3, starting transfers between devices, shifted(): return lax.ppermute(block, axis, route)  5.75 us
    ppermute x1, starting transfers between devices, extend_wide(): lax.ppermute(rows[..., -width:], 'az', ring_pairs(n_az, 1, True))  4.28 us
    select_n x6, other arithmetic, edge_states(): jnp.where(spread * middle > spread * spread / 6.0, 3.0 * middle_cell - 2....  4.08 us
    ppermute x1, waiting for transfers between devices, extend_wide(): from_below = lax.ppermute(x[:, -width:], 'rad', ring_pairs(n_rad, 1, False))  3.8 us
  transfers between devices with their start and end apart: 7, of which 7 were waited for; matrix products, arithmetic and copies ran while one was open for 1% of the time, Pallas kernels for 0%

profile of v3, /device:TPU:56, one launch (start us, length us, event | category | flops | bytes accessed | tf_op | source)
XLA Modules:
  0.0 97.7 jit_solution(12084413559073682022)
XLA Ops:
  0.0 1.0 %copy.7 = f32[5,6,8,256]{3,2,0,1:T(8,128)S(1)} copy(f32[5,6,8,256]{3,2,1,0:T(8,128)} %param.2) | data formatting | bytes 491520 | tf_op args[0]
  1.0 2.7 %collective-permute-start.1 = (f32[5,6,8,256]{3,2,0,1:T(8,128)S(1)}, f32[5,6,8,256]{3,2,0,1:T(8,128)S(1)}, u32[]{:S(2)}, u32[]{:S(2)}) collective-permute-start(f32[5,6,8,256]{3,2,0,1:T(8,128)S(1)} %copy.7), channel_id=1, source_target_pairs={{24,0},{48,24},{72,48},{96,72},{120,96},{144,120},{168,144},{192,1... | collective-permute-start | bytes 737288 | tf_op jit(solution)/shard_map/ppermute | solution.py:219
  3.7 1.9 %collective-permute-start = (f32[5,6,8,256]{3,2,0,1:T(8,128)S(1)}, f32[5,6,8,256]{3,2,0,1:T(8,128)S(1)}, u32[]{:S(2)}, u32[]{:S(2)}) collective-permute-start(f32[5,6,8,256]{3,2,0,1:T(8,128)S(1)} %copy.7), channel_id=1, source_target_pairs={{0,24},{24,48},{48,72},{72,96},{96,120},{120,144},{144,168},{168,1... | collective-permute-start | bytes 737288 | tf_op jit(solution)/shard_map/ppermute | solution.py:218
  5.7 0.8 slice_bitcast_fusion.3
  6.5 1.0 collective-permute-done.1
  7.5 3.8 %collective-permute-done = f32[5,6,8,256]{3,2,0,1:T(8,128)S(1)} collective-permute-done((f32[5,6,8,256]{3,2,0,1:T(8,128)S(1)}, f32[5,6,8,256]{3,2,0,1:T(8,128)S(1)}, u32[]{:S(2)}, u32[]{:S(2)}) %collective-permute-start) | collective-permute-done | bytes 245792 | tf_op jit(solution)/shard_map/ppermute | solution.py:218
  11.5 4.3 %collective-permute-start.2 = (f32[5,18,8,6]{3,2,0,1:T(8,128)S(1)}, f32[5,18,8,6]{3,2,0,1:T(8,128)S(1)}, u32[]{:S(2)}, u32[]{:S(2)}) collective-permute-start(f32[5,18,8,6]{3,2,0,1:T(8,128)S(1)} %get-tuple-element.27), channel_id=1, source_target_pairs={{0,1},{1,2},{2,3},{3,4},{4,5},{5,6},{6,7},{7,8},{8,9},{9,10},{10,1... | collective-permute-start | bytes 51848 | tf_op jit(solution)/shard_map/ppermute | solution.py:221
  15.8 14.7 %collective-permute-start.3 = (f32[5,18,8,6]{3,2,0,1:T(8,128)S(1)}, f32[5,18,8,6]{3,2,0,1:T(8,128)S(1)}, u32[]{:S(2)}, u32[]{:S(2)}) collective-permute-start(f32[5,18,8,6]{3,2,0,1:T(8,128)S(1)} %get-tuple-element.28), channel_id=1, source_target_pairs={{0,23},{1,0},{2,1},{3,2},{4,3},{5,4},{6,5},{7,6},{8,7},{9,8},{10,9... | collective-permute-start | bytes 51848 | tf_op jit(solution)/shard_map/ppermute | solution.py:222
  30.6 7.1 %collective-permute-done.2 = f32[5,18,8,6]{3,2,0,1:T(8,128)S(1)} collective-permute-done((f32[5,18,8,6]{3,2,0,1:T(8,128)S(1)}, f32[5,18,8,6]{3,2,0,1:T(8,128)S(1)}, u32[]{:S(2)}, u32[]{:S(2)}) %collective-permute-start.2) | collective-permute-done | bytes 17312 | tf_op jit(solution)/shard_map/ppermute | solution.py:221
  37.7 1.2 %collective-permute-done.3 = f32[5,18,8,6]{3,2,0,1:T(8,128)S(1)} collective-permute-done((f32[5,18,8,6]{3,2,0,1:T(8,128)S(1)}, f32[5,18,8,6]{3,2,0,1:T(8,128)S(1)}, u32[]{:S(2)}, u32[]{:S(2)}) %collective-permute-start.3) | collective-permute-done | bytes 17312 | tf_op jit(solution)/shard_map/ppermute | solution.py:222
  39.4 1.0 %fusion.29 = f32[5,15,8,262]{3,2,0,1:T(8,128)S(1)} fusion(f32[5,18,8,268]{3,2,0,1:T(8,128)S(1)} %pad_maximum_fusion.1), kind=kLoop, calls=%fused_computation.39 | loop fusion | flops 1414800 | bytes 3144000 | tf_op jit(solution)/shard_map/jit(clip)/min | solution.py:29
  41.8 0.8 subtract_select_fusion.2
  45.1 0.8 fusion.9
  45.9 1.4 %subtract_select_fusion = (f32[5,12,10,262]{3,2,0,1:T(8,128)S(1)}, f32[5,12,10,262]{3,2,0,1:T(8,128)S(1)}) fusion(f32[5,12,14,262]{3,2,0,1:T(8,128)S(1)} %pad_maximum_fusion, f32[5,12,11,262]{3,2,0,1:T(8,128)S(1)} %fusion.9), kind=kLoop, calls=%fused_computation.13 | loop fusion | flops 3930000 | bytes 3144000 | tf_op jit(solution)/shard_map/jit(_where)/select_n | solution.py:39
  50.1 1.2 %fusion.88 = f32[5,12,9,262]{3,2,0,1:T(8,128)S(1)} fusion(f32[5,12,9,262]{3,2,0,1:T(8,128)S(1)} %fusion.85, f32[5,12,10,262]{3,2,0,1:T(8,128)S(1)} %get-tuple-element.5, f32[5,12,10,262]{3,2,0,1:T(8,128)S(1)} %get-tuple-element.6), kind=kLoop, calls=%fused_computation.144 | loop fusion | flops 2122200 | bytes 3244032 | tf_op jit(solution)/shard_map/stack | solution.py:102
  51.3 0.7 subtract_select_fusion.4
  62.4 1.9 %collective-permute-start.4 = (f32[5,6,8,256]{3,2,0,1:T(8,128)S(1)}, f32[5,6,8,256]{3,2,0,1:T(8,128)S(1)}, u32[]{:S(2)}, u32[]{:S(2)}) collective-permute-start(f32[5,6,8,256]{3,2,0,1:T(8,128)S(1)} %pad_maximum_fusion.8), channel_id=1, source_target_pairs={{22,0},{23,1},{0,2},{1,3},{2,4},{3,5},{4,6},{5,7},{6,8},{7,9},{8,1... | collective-permute-start | bytes 737288 | tf_op jit(solution)/shard_map/ppermute | solution.py:15
  64.3 1.9 %collective-permute-start.6 = (f32[5,6,8,256]{3,2,0,1:T(8,128)S(1)}, f32[5,6,8,256]{3,2,0,1:T(8,128)S(1)}, u32[]{:S(2)}, u32[]{:S(2)}) collective-permute-start(f32[5,6,8,256]{3,2,0,1:T(8,128)S(1)} %pad_maximum_fusion.8), channel_id=1, source_target_pairs={{23,0},{0,1},{1,2},{2,3},{3,4},{4,5},{5,6},{6,7},{7,8},{8,9},{9,10... | collective-permute-start | bytes 737288 | tf_op jit(solution)/shard_map/ppermute | solution.py:15
  66.2 16.6 %collective-permute-done.4 = f32[5,6,8,256]{3,2,0,1:T(8,128)S(1)} collective-permute-done((f32[5,6,8,256]{3,2,0,1:T(8,128)S(1)}, f32[5,6,8,256]{3,2,0,1:T(8,128)S(1)}, u32[]{:S(2)}, u32[]{:S(2)}) %collective-permute-start.4) | collective-permute-done | bytes 245792 | tf_op jit(solution)/shard_map/ppermute | solution.py:15
  82.9 1.9 %collective-permute-start.5 = (f32[5,6,8,256]{3,2,0,1:T(8,128)S(1)}, f32[5,6,8,256]{3,2,0,1:T(8,128)S(1)}, u32[]{:S(2)}, u32[]{:S(2)}) collective-permute-start(f32[5,6,8,256]{3,2,0,1:T(8,128)S(1)} %collective-permute-done.4), channel_id=1, source_target_pairs={{23,0},{0,1},{1,2},{2,3},{3,4},{4,5},{5,6},{6,7},{7,8},{8,9},{9,10... | collective-permute-start | bytes 737288 | tf_op jit(solution)/shard_map/ppermute | solution.py:15
  84.8 2.0 %collective-permute-done.6 = f32[5,6,8,256]{3,2,0,1:T(8,128)S(1)} collective-permute-done((f32[5,6,8,256]{3,2,0,1:T(8,128)S(1)}, f32[5,6,8,256]{3,2,0,1:T(8,128)S(1)}, u32[]{:S(2)}, u32[]{:S(2)}) %collective-permute-start.6) | collective-permute-done | bytes 245792 | tf_op jit(solution)/shard_map/ppermute | solution.py:15
  86.8 7.7 %collective-permute-done.5 = f32[5,6,8,256]{3,2,0,1:T(8,128)S(1)} collective-permute-done((f32[5,6,8,256]{3,2,0,1:T(8,128)S(1)}, f32[5,6,8,256]{3,2,0,1:T(8,128)S(1)}, u32[]{:S(2)}, u32[]{:S(2)}) %collective-permute-start.5) | collective-permute-done | bytes 245792 | tf_op jit(solution)/shard_map/ppermute | solution.py:15
  94.6 2.5 %fusion.12 = f32[5,6,8,256]{3,2,0,1:T(8,128)S(1)} fusion(s32[6]{0:T(128)S(1)} %broadcast_subtract_fusion, f32[1,6,8,256]{3,2,0,1:T(8,128)S(1)} %fusion.215, f32[3,6,8,256]{3,2,0,1:T(8,128)S(1)} %slice_divide_fusion.1, f32[1,6,8,256]{3,2,0,1:T(8,128)S(1)} %get-tuple-element.29, f32[5,6,8,256]{3,2,0,1:T(8,128)S(1)} %collective-permute-done.6, ...), kind=kOutput, calls=%fused_computation.21 | convolution fusion | flops 759349248 | bytes 1228824 | tf_op jit(solution)/shard_map/fitk,ikc->fitc/dot_general | solution.py:207
  97.0 0.7 copy.18
  (80 shorter events, 17.4 us)
Async XLA Ops:
  0.0 11.3 %copy-start = (f32[5,6,8,256]{3,2,1,0:T(8,128)S(1)}, f32[5,6,8,256]{3,2,1,0:T(8,128)}, u32[]{:S(2)}) copy-start(f32[5,6,8,256]{3,2,1,0:T(8,128)} %param.2) | copy-start | bytes 737284
  1.0 6.4 %collective-permute-start.1 = (f32[5,6,8,256]{3,2,0,1:T(8,128)S(1)}, f32[5,6,8,256]{3,2,0,1:T(8,128)S(1)}, u32[]{:S(2)}, u32[]{:S(2)}) collective-permute-start(f32[5,6,8,256]{3,2,0,1:T(8,128)S(1)} %copy.7), channel_id=1, source_target_pairs={{24,0},{48,24},{72,48},{96,72},{120,96},{144,120},{168,144},{192,1... | collective-permute-start | bytes 737288 | tf_op jit(solution)/shard_map/ppermute | solution.py:219
  3.7 7.5 %collective-permute-start = (f32[5,6,8,256]{3,2,0,1:T(8,128)S(1)}, f32[5,6,8,256]{3,2,0,1:T(8,128)S(1)}, u32[]{:S(2)}, u32[]{:S(2)}) collective-permute-start(f32[5,6,8,256]{3,2,0,1:T(8,128)S(1)} %copy.7), channel_id=1, source_target_pairs={{0,24},{24,48},{48,72},{72,96},{96,120},{120,144},{144,168},{168,1... | collective-permute-start | bytes 737288 | tf_op jit(solution)/shard_map/ppermute | solution.py:218
  11.5 26.2 %collective-permute-start.2 = (f32[5,18,8,6]{3,2,0,1:T(8,128)S(1)}, f32[5,18,8,6]{3,2,0,1:T(8,128)S(1)}, u32[]{:S(2)}, u32[]{:S(2)}) collective-permute-start(f32[5,18,8,6]{3,2,0,1:T(8,128)S(1)} %get-tuple-element.27), channel_id=1, source_target_pairs={{0,1},{1,2},{2,3},{3,4},{4,5},{5,6},{6,7},{7,8},{8,9},{9,10},{10,1... | collective-permute-start | bytes 51848 | tf_op jit(solution)/shard_map/ppermute | solution.py:221
  15.8 23.1 %collective-permute-start.3 = (f32[5,18,8,6]{3,2,0,1:T(8,128)S(1)}, f32[5,18,8,6]{3,2,0,1:T(8,128)S(1)}, u32[]{:S(2)}, u32[]{:S(2)}) collective-permute-start(f32[5,18,8,6]{3,2,0,1:T(8,128)S(1)} %get-tuple-element.28), channel_id=1, source_target_pairs={{0,23},{1,0},{2,1},{3,2},{4,3},{5,4},{6,5},{7,6},{8,7},{9,8},{10,9... | collective-permute-start | bytes 51848 | tf_op jit(solution)/shard_map/ppermute | solution.py:222
  61.9 22.8 %copy-start.1 = (s32[6]{0:T(128)S(1)}, s32[6]{0:T(128)}, u32[]{:S(2)}) copy-start(s32[6]{0:T(128)} %param.3) | copy-start | bytes 76
  62.4 20.5 %collective-permute-start.4 = (f32[5,6,8,256]{3,2,0,1:T(8,128)S(1)}, f32[5,6,8,256]{3,2,0,1:T(8,128)S(1)}, u32[]{:S(2)}, u32[]{:S(2)}) collective-permute-start(f32[5,6,8,256]{3,2,0,1:T(8,128)S(1)} %pad_maximum_fusion.8), channel_id=1, source_target_pairs={{22,0},{23,1},{0,2},{1,3},{2,4},{3,5},{4,6},{5,7},{6,8},{7,9},{8,1... | collective-permute-start | bytes 737288 | tf_op jit(solution)/shard_map/ppermute | solution.py:15
  64.3 22.5 %collective-permute-start.6 = (f32[5,6,8,256]{3,2,0,1:T(8,128)S(1)}, f32[5,6,8,256]{3,2,0,1:T(8,128)S(1)}, u32[]{:S(2)}, u32[]{:S(2)}) collective-permute-start(f32[5,6,8,256]{3,2,0,1:T(8,128)S(1)} %pad_maximum_fusion.8), channel_id=1, source_target_pairs={{23,0},{0,1},{1,2},{2,3},{3,4},{4,5},{5,6},{6,7},{7,8},{8,9},{9,10... | collective-permute-start | bytes 737288 | tf_op jit(solution)/shard_map/ppermute | solution.py:15
  82.9 11.7 %collective-permute-start.5 = (f32[5,6,8,256]{3,2,0,1:T(8,128)S(1)}, f32[5,6,8,256]{3,2,0,1:T(8,128)S(1)}, u32[]{:S(2)}, u32[]{:S(2)}) collective-permute-start(f32[5,6,8,256]{3,2,0,1:T(8,128)S(1)} %collective-permute-done.4), channel_id=1, source_target_pairs={{23,0},{0,1},{1,2},{2,3},{3,4},{4,5},{5,6},{6,7},{7,8},{8,9},{9,10... | collective-permute-start | bytes 737288 | tf_op jit(solution)/shard_map/ppermute | solution.py:15

commit v4 on v2

--- a/solution.py
+++ b/solution.py
@@ -198,19 +198,21 @@
             blocks.append(shifted(primitive, "az", distance))
         else:
             blocks.append(shifted(blocks[-1], "az", 1))
-    joined = jnp.concatenate(blocks[::-1], axis=3)
-    width = joined.shape[3]
-    source = lax.broadcasted_iota(jnp.int32, (1, width, cell_count), 1)
-    target = lax.broadcasted_iota(jnp.int32, (1, width, cell_count), 2)
-    start = far * cell_count - shifts
-    pick = (source == target + start[:, None, None]).astype(jnp.float32)
-    return jnp.einsum(
-        "fitk,ikc->fitc",
-        joined,
-        pick,
-        precision=lax.Precision.HIGHEST,
-        preferred_element_type=jnp.float32,
-    )
+    source = lax.broadcasted_iota(jnp.int32, (1, cell_count, cell_count), 1)
+    target = lax.broadcasted_iota(jnp.int32, (1, cell_count, cell_count), 2)
+    offset = source - target + shifts[:, None, None]
+    total = None
+    for distance, block in enumerate(blocks):
+        pick = (offset == distance * cell_count).astype(jnp.float32)
+        part = jnp.einsum(
+            "fitk,ikc->fitc",
+            block,
+            pick,
+            precision=lax.Precision.HIGHEST,
+            preferred_element_type=jnp.float32,
+        )
+        total = part if total is None else total + part
+    return total
 
 
 def on_device(fields, shifts):

time: 90.9 us -> 96.8 us (1.065)
  waiting for transfers between devices: 26.7 us -> 32.9 us
    ppermute x3, waiting for transfers between devices: 26.4 us -> 29.8 us  [shifted(): return lax.ppermute(block, axis, route)]
    ppermute x2, starting transfers between devices: 7.28 us -> 4.62 us  [halos(): from_above = lax.ppermute(x[:, :width], 'rad', ring_pairs(n_rad, -1, False))]
    ppermute x2, starting transfers between devices: 3.84 us -> 6.44 us  [halos(): from_below = lax.ppermute(x[:, -width:], 'rad', ring_pairs(n_rad, 1, False))]
    ppermute x2, waiting for transfers between devices: 0.01 us -> 1.98 us  [halos(): from_left = lax.ppermute(x[..., -width:], 'az', ring_pairs(n_az, 1, True))]
    slice x2, local copies, waits for them, and re-layouts: 0.04 us -> 1.04 us  [halos(): from_below = lax.ppermute(x[:, -width:], 'rad', ring_pairs(n_rad, 1, False))]
    slice x2, local copies, waits for them, and re-layouts: 1.18 us -> 0.18 us  [halos(): from_left = lax.ppermute(x[..., -width:], 'az', ring_pairs(n_az, 1, True))]
    dot_general x1 -> x4, matrix products: 2.46 us -> 3 us  [shift_rows(): jnp.einsum('fitk,ikc->fitc', block, pick, precision=lax.Precision.HIGHEST...]
  transfers between devices with their start and end apart: 11 -> 11, of which waited for: 4 -> 4; matrix products, arithmetic and copies ran while one was open for 10% -> 12% of each run, Pallas kernels for 0% -> 0%
where the time goes in v4:
time: 96.8 us; the launch traced here: 95.9 us
  starting transfers between devices  45.4 us (47%)
  waiting for transfers between devices  32.9 us (34%)
  other arithmetic  11.6 us (12%)
  matrix products  3 us (3%)
  local copies, waits for them, and re-layouts  2.19 us (2%)
    ppermute x3, waiting for transfers between devices, shifted(): return lax.ppermute(block, axis, route)  29.8 us
    ppermute x2, starting transfers between devices, halos(): from_right = lax.ppermute(x[..., :width], 'az', ring_pairs(n_az, -1, True))  22.4 us
    ppermute x2, starting transfers between devices, halos(): from_below = lax.ppermute(x[:, -width:], 'rad', ring_pairs(n_rad, 1, False))  6.44 us
    ppermute x2, starting transfers between devices, halos(): from_left = lax.ppermute(x[..., -width:], 'az', ring_pairs(n_az, 1, True))  6.2 us
    ppermute x3, starting transfers between devices, shifted(): return lax.ppermute(block, axis, route)  5.75 us
    unnamed x27, other arithmetic  4.96 us
    ppermute x2, starting transfers between devices, halos(): from_above = lax.ppermute(x[:, :width], 'rad', ring_pairs(n_rad, -1, False))  4.62 us
    dot_general x4, matrix products, shift_rows(): jnp.einsum('fitk,ikc->fitc', block, pick, precision=lax.Precision.HIGHEST...  3 us
  transfers between devices with their start and end apart: 11, of which 4 were waited for; matrix products, arithmetic and copies ran while one was open for 12% of the time, Pallas kernels for 0%

profile of v4, /device:TPU:56, one launch (start us, length us, event | category | flops | bytes accessed | tf_op | source)
XLA Modules:
  0.0 95.9 jit_solution(392766151678688734)
XLA Ops:
  0.0 1.0 %fusion.232 = (f32[5,3,8,256]{3,2,0,1:T(8,128)S(1)}, f32[5,3,8,256]{3,2,0,1:T(8,128)S(1)}) fusion(f32[5,6,8,256]{3,2,1,0:T(8,128)} %param.2), kind=kLoop, calls=%fused_computation.426 | loop fusion | bytes 491520 | tf_op jit(solution)/shard_map/slice | solution.py:178
  1.0 2.7 %collective-permute-start.1 = (f32[5,3,8,256]{3,2,0,1:T(8,128)S(1)}, f32[5,3,8,256]{3,2,0,1:T(8,128)S(1)}, u32[]{:S(2)}, u32[]{:S(2)}) collective-permute-start(f32[5,3,8,256]{3,2,0,1:T(8,128)S(1)} %get-tuple-element.32), channel_id=1, source_target_pairs={{24,0},{48,24},{72,48},{96,72},{120,96},{144,120},{168,144},{192,1... | collective-permute-start | bytes 368648 | tf_op jit(solution)/shard_map/ppermute | solution.py:179
  3.7 1.9 %collective-permute-start = (f32[5,3,8,256]{3,2,0,1:T(8,128)S(1)}, f32[5,3,8,256]{3,2,0,1:T(8,128)S(1)}, u32[]{:S(2)}, u32[]{:S(2)}) collective-permute-start(f32[5,3,8,256]{3,2,0,1:T(8,128)S(1)} %get-tuple-element.31), channel_id=1, source_target_pairs={{0,24},{24,48},{48,72},{72,96},{96,120},{120,144},{144,168},{168,1... | collective-permute-start | bytes 368648 | tf_op jit(solution)/shard_map/ppermute | solution.py:178
  5.8 4.3 %collective-permute-start.2 = (f32[5,6,8,3]{3,2,0,1:T(8,128)S(1)}, f32[5,6,8,3]{3,2,0,1:T(8,128)S(1)}, u32[]{:S(2)}, u32[]{:S(2)}) collective-permute-start(f32[5,6,8,3]{3,2,0,1:T(8,128)S(1)} %get-tuple-element.35), channel_id=1, source_target_pairs={{0,1},{1,2},{2,3},{3,4},{4,5},{5,6},{6,7},{7,8},{8,9},{9,10},{10,1... | collective-permute-start | bytes 8648 | tf_op jit(solution)/shard_map/ppermute | solution.py:180
  10.1 14.7 %collective-permute-start.3 = (f32[5,6,8,3]{3,2,0,1:T(8,128)S(1)}, f32[5,6,8,3]{3,2,0,1:T(8,128)S(1)}, u32[]{:S(2)}, u32[]{:S(2)}) collective-permute-start(f32[5,6,8,3]{3,2,0,1:T(8,128)S(1)} %get-tuple-element.36), channel_id=1, source_target_pairs={{0,23},{1,0},{2,1},{3,2},{4,3},{5,4},{6,5},{7,6},{8,7},{9,8},{10,9... | collective-permute-start | bytes 8648 | tf_op jit(solution)/shard_map/ppermute | solution.py:181
  25.3 0.5 subtract_select_fusion.2
  27.8 0.4 subtract_select_fusion.6
  31.2 4.5 %collective-permute-start.4 = (f32[5,3,8,256]{3,2,0,1:T(8,128)S(1)}, f32[5,3,8,256]{3,2,0,1:T(8,128)S(1)}, u32[]{:S(2)}, u32[]{:S(2)}) collective-permute-start(f32[5,3,8,256]{3,2,0,1:T(8,128)S(1)} %get-tuple-element.21), channel_id=1, source_target_pairs={{0,24},{24,48},{48,72},{72,96},{96,120},{120,144},{144,168},{168,1... | collective-permute-start | bytes 368648 | tf_op jit(solution)/shard_map/ppermute | solution.py:178
  35.7 1.9 %collective-permute-start.5 = (f32[5,3,8,256]{3,2,0,1:T(8,128)S(1)}, f32[5,3,8,256]{3,2,0,1:T(8,128)S(1)}, u32[]{:S(2)}, u32[]{:S(2)}) collective-permute-start(f32[5,3,8,256]{3,2,0,1:T(8,128)S(1)} %get-tuple-element.22), channel_id=1, source_target_pairs={{24,0},{48,24},{72,48},{96,72},{120,96},{144,120},{168,144},{192,1... | collective-permute-start | bytes 368648 | tf_op jit(solution)/shard_map/ppermute | solution.py:179
  38.1 0.5 subtract_select_fusion
  40.0 1.9 %collective-permute-start.6 = (f32[5,6,8,3]{3,2,0,1:T(8,128)S(1)}, f32[5,6,8,3]{3,2,0,1:T(8,128)S(1)}, u32[]{:S(2)}, u32[]{:S(2)}) collective-permute-start(f32[5,6,8,3]{3,2,0,1:T(8,128)S(1)} %get-tuple-element.25), channel_id=1, source_target_pairs={{0,1},{1,2},{2,3},{3,4},{4,5},{5,6},{6,7},{7,8},{8,9},{9,10},{10,1... | collective-permute-start | bytes 8648 | tf_op jit(solution)/shard_map/ppermute | solution.py:180
  41.9 7.7 %collective-permute-start.7 = (f32[5,6,8,3]{3,2,0,1:T(8,128)S(1)}, f32[5,6,8,3]{3,2,0,1:T(8,128)S(1)}, u32[]{:S(2)}, u32[]{:S(2)}) collective-permute-start(f32[5,6,8,3]{3,2,0,1:T(8,128)S(1)} %get-tuple-element.26), channel_id=1, source_target_pairs={{0,23},{1,0},{2,1},{3,2},{4,3},{5,4},{6,5},{7,6},{8,7},{9,8},{10,9... | collective-permute-start | bytes 8648 | tf_op jit(solution)/shard_map/ppermute | solution.py:181
  49.6 2.0 %collective-permute-done.6 = f32[5,6,8,3]{3,2,0,1:T(8,128)S(1)} collective-permute-done((f32[5,6,8,3]{3,2,0,1:T(8,128)S(1)}, f32[5,6,8,3]{3,2,0,1:T(8,128)S(1)}, u32[]{:S(2)}, u32[]{:S(2)}) %collective-permute-start.6) | collective-permute-done | bytes 2912 | tf_op jit(solution)/shard_map/ppermute | solution.py:180
  51.6 1.2 %collective-permute-done.7 = f32[5,6,8,3]{3,2,0,1:T(8,128)S(1)} collective-permute-done((f32[5,6,8,3]{3,2,0,1:T(8,128)S(1)}, f32[5,6,8,3]{3,2,0,1:T(8,128)S(1)}, u32[]{:S(2)}, u32[]{:S(2)}) %collective-permute-start.7) | collective-permute-done | bytes 2912 | tf_op jit(solution)/shard_map/ppermute | solution.py:181
  56.6 1.9 %collective-permute-start.8 = (f32[5,6,8,256]{3,2,0,1:T(8,128)S(1)}, f32[5,6,8,256]{3,2,0,1:T(8,128)S(1)}, u32[]{:S(2)}, u32[]{:S(2)}) collective-permute-start(f32[5,6,8,256]{3,2,0,1:T(8,128)S(1)} %pad_maximum_fusion.7), channel_id=1, source_target_pairs={{23,0},{0,1},{1,2},{2,3},{3,4},{4,5},{5,6},{6,7},{7,8},{8,9},{9,10... | collective-permute-start | bytes 737288 | tf_op jit(solution)/shard_map/ppermute | solution.py:15
  58.5 1.9 %collective-permute-start.9 = (f32[5,6,8,256]{3,2,0,1:T(8,128)S(1)}, f32[5,6,8,256]{3,2,0,1:T(8,128)S(1)}, u32[]{:S(2)}, u32[]{:S(2)}) collective-permute-start(f32[5,6,8,256]{3,2,0,1:T(8,128)S(1)} %pad_maximum_fusion.7), channel_id=1, source_target_pairs={{22,0},{23,1},{0,2},{1,3},{2,4},{3,5},{4,6},{5,7},{6,8},{7,9},{8,1... | collective-permute-start | bytes 737288 | tf_op jit(solution)/shard_map/ppermute | solution.py:15
  60.5 0.8 fusion.1
  61.2 20.9 %collective-permute-done.9 = f32[5,6,8,256]{3,2,0,1:T(8,128)S(1)} collective-permute-done((f32[5,6,8,256]{3,2,0,1:T(8,128)S(1)}, f32[5,6,8,256]{3,2,0,1:T(8,128)S(1)}, u32[]{:S(2)}, u32[]{:S(2)}) %collective-permute-start.9) | collective-permute-done | bytes 245792 | tf_op jit(solution)/shard_map/ppermute | solution.py:15
  82.2 1.9 %collective-permute-start.10 = (f32[5,6,8,256]{3,2,0,1:T(8,128)S(1)}, f32[5,6,8,256]{3,2,0,1:T(8,128)S(1)}, u32[]{:S(2)}, u32[]{:S(2)}) collective-permute-start(f32[5,6,8,256]{3,2,0,1:T(8,128)S(1)} %collective-permute-done.9), channel_id=1, source_target_pairs={{23,0},{0,1},{1,2},{2,3},{3,4},{4,5},{5,6},{6,7},{7,8},{8,9},{9,10... | collective-permute-start | bytes 737288 | tf_op jit(solution)/shard_map/ppermute | solution.py:15
  84.1 0.8 fusion.21
  84.9 0.8 fusion.18
  85.6 8.8 %collective-permute-done.10 = f32[5,6,8,256]{3,2,0,1:T(8,128)S(1)} collective-permute-done((f32[5,6,8,256]{3,2,0,1:T(8,128)S(1)}, f32[5,6,8,256]{3,2,0,1:T(8,128)S(1)}, u32[]{:S(2)}, u32[]{:S(2)}) %collective-permute-start.10) | collective-permute-done | bytes 245792 | tf_op jit(solution)/shard_map/ppermute | solution.py:15
  94.5 0.8 fusion.15
  95.2 0.7 copy.50
  (91 shorter events, 10.7 us)
Async XLA Ops:
  0.0 5.7 %copy-start = (f32[5,6,8,256]{3,2,1,0:T(8,128)S(1)}, f32[5,6,8,256]{3,2,1,0:T(8,128)}, u32[]{:S(2)}) copy-start(f32[5,6,8,256]{3,2,1,0:T(8,128)} %param.2) | copy-start | bytes 737284
  1.0 28.5 %collective-permute-start.1 = (f32[5,3,8,256]{3,2,0,1:T(8,128)S(1)}, f32[5,3,8,256]{3,2,0,1:T(8,128)S(1)}, u32[]{:S(2)}, u32[]{:S(2)}) collective-permute-start(f32[5,3,8,256]{3,2,0,1:T(8,128)S(1)} %get-tuple-element.32), channel_id=1, source_target_pairs={{24,0},{48,24},{72,48},{96,72},{120,96},{144,120},{168,144},{192,1... | collective-permute-start | bytes 368648 | tf_op jit(solution)/shard_map/ppermute | solution.py:179
  3.7 25.8 %collective-permute-start = (f32[5,3,8,256]{3,2,0,1:T(8,128)S(1)}, f32[5,3,8,256]{3,2,0,1:T(8,128)S(1)}, u32[]{:S(2)}, u32[]{:S(2)}) collective-permute-start(f32[5,3,8,256]{3,2,0,1:T(8,128)S(1)} %get-tuple-element.31), channel_id=1, source_target_pairs={{0,24},{24,48},{48,72},{72,96},{96,120},{120,144},{144,168},{168,1... | collective-permute-start | bytes 368648 | tf_op jit(solution)/shard_map/ppermute | solution.py:178
  5.8 21.5 %collective-permute-start.2 = (f32[5,6,8,3]{3,2,0,1:T(8,128)S(1)}, f32[5,6,8,3]{3,2,0,1:T(8,128)S(1)}, u32[]{:S(2)}, u32[]{:S(2)}) collective-permute-start(f32[5,6,8,3]{3,2,0,1:T(8,128)S(1)} %get-tuple-element.35), channel_id=1, source_target_pairs={{0,1},{1,2},{2,3},{3,4},{4,5},{5,6},{6,7},{7,8},{8,9},{9,10},{10,1... | collective-permute-start | bytes 8648 | tf_op jit(solution)/shard_map/ppermute | solution.py:180
  10.1 17.2 %collective-permute-start.3 = (f32[5,6,8,3]{3,2,0,1:T(8,128)S(1)}, f32[5,6,8,3]{3,2,0,1:T(8,128)S(1)}, u32[]{:S(2)}, u32[]{:S(2)}) collective-permute-start(f32[5,6,8,3]{3,2,0,1:T(8,128)S(1)} %get-tuple-element.36), channel_id=1, source_target_pairs={{0,23},{1,0},{2,1},{3,2},{4,3},{5,4},{6,5},{7,6},{8,7},{9,8},{10,9... | collective-permute-start | bytes 8648 | tf_op jit(solution)/shard_map/ppermute | solution.py:181
  31.2 23.8 %collective-permute-start.4 = (f32[5,3,8,256]{3,2,0,1:T(8,128)S(1)}, f32[5,3,8,256]{3,2,0,1:T(8,128)S(1)}, u32[]{:S(2)}, u32[]{:S(2)}) collective-permute-start(f32[5,3,8,256]{3,2,0,1:T(8,128)S(1)} %get-tuple-element.21), channel_id=1, source_target_pairs={{0,24},{24,48},{48,72},{72,96},{96,120},{120,144},{144,168},{168,1... | collective-permute-start | bytes 368648 | tf_op jit(solution)/shard_map/ppermute | solution.py:178
  35.7 19.3 %collective-permute-start.5 = (f32[5,3,8,256]{3,2,0,1:T(8,128)S(1)}, f32[5,3,8,256]{3,2,0,1:T(8,128)S(1)}, u32[]{:S(2)}, u32[]{:S(2)}) collective-permute-start(f32[5,3,8,256]{3,2,0,1:T(8,128)S(1)} %get-tuple-element.22), channel_id=1, source_target_pairs={{24,0},{48,24},{72,48},{96,72},{120,96},{144,120},{168,144},{192,1... | collective-permute-start | bytes 368648 | tf_op jit(solution)/shard_map/ppermute | solution.py:179
  40.0 11.6 %collective-permute-start.6 = (f32[5,6,8,3]{3,2,0,1:T(8,128)S(1)}, f32[5,6,8,3]{3,2,0,1:T(8,128)S(1)}, u32[]{:S(2)}, u32[]{:S(2)}) collective-permute-start(f32[5,6,8,3]{3,2,0,1:T(8,128)S(1)} %get-tuple-element.25), channel_id=1, source_target_pairs={{0,1},{1,2},{2,3},{3,4},{4,5},{5,6},{6,7},{7,8},{8,9},{9,10},{10,1... | collective-permute-start | bytes 8648 | tf_op jit(solution)/shard_map/ppermute | solution.py:180
  41.9 10.9 %collective-permute-start.7 = (f32[5,6,8,3]{3,2,0,1:T(8,128)S(1)}, f32[5,6,8,3]{3,2,0,1:T(8,128)S(1)}, u32[]{:S(2)}, u32[]{:S(2)}) collective-permute-start(f32[5,6,8,3]{3,2,0,1:T(8,128)S(1)} %get-tuple-element.26), channel_id=1, source_target_pairs={{0,23},{1,0},{2,1},{3,2},{4,3},{5,4},{6,5},{7,6},{8,7},{9,8},{10,9... | collective-permute-start | bytes 8648 | tf_op jit(solution)/shard_map/ppermute | solution.py:181
  56.5 4.0 %copy-start.1 = (s32[6]{0:T(128)S(1)}, s32[6]{0:T(128)}, u32[]{:S(2)}) copy-start(s32[6]{0:T(128)} %param.3) | copy-start | bytes 76
  56.6 27.5 %collective-permute-start.8 = (f32[5,6,8,256]{3,2,0,1:T(8,128)S(1)}, f32[5,6,8,256]{3,2,0,1:T(8,128)S(1)}, u32[]{:S(2)}, u32[]{:S(2)}) collective-permute-start(f32[5,6,8,256]{3,2,0,1:T(8,128)S(1)} %pad_maximum_fusion.7), channel_id=1, source_target_pairs={{23,0},{0,1},{1,2},{2,3},{3,4},{4,5},{5,6},{6,7},{7,8},{8,9},{9,10... | collective-permute-start | bytes 737288 | tf_op jit(solution)/shard_map/ppermute | solution.py:15
  58.5 23.7 %collective-permute-start.9 = (f32[5,6,8,256]{3,2,0,1:T(8,128)S(1)}, f32[5,6,8,256]{3,2,0,1:T(8,128)S(1)}, u32[]{:S(2)}, u32[]{:S(2)}) collective-permute-start(f32[5,6,8,256]{3,2,0,1:T(8,128)S(1)} %pad_maximum_fusion.7), channel_id=1, source_target_pairs={{22,0},{23,1},{0,2},{1,3},{2,4},{3,5},{4,6},{5,7},{6,8},{7,9},{8,1... | collective-permute-start | bytes 737288 | tf_op jit(solution)/shard_map/ppermute | solution.py:15
  82.2 12.3 %collective-permute-start.10 = (f32[5,6,8,256]{3,2,0,1:T(8,128)S(1)}, f32[5,6,8,256]{3,2,0,1:T(8,128)S(1)}, u32[]{:S(2)}, u32[]{:S(2)}) collective-permute-start(f32[5,6,8,256]{3,2,0,1:T(8,128)S(1)} %collective-permute-done.9), channel_id=1, source_target_pairs={{23,0},{0,1},{1,2},{2,3},{3,4},{4,5},{5,6},{6,7},{7,8},{8,9},{9,10... | collective-permute-start | bytes 737288 | tf_op jit(solution)/shard_map/ppermute | solution.py:15

commit v5 on v4

--- a/solution.py
+++ b/solution.py
@@ -2,6 +2,7 @@
 import jax.numpy as jnp
 from jax import lax
 from jax.sharding import PartitionSpec as P
+
 
 ADIABATIC = 1.4
 COURANT_RADIAL = 0.09
@@ -60,7 +61,7 @@
 
 
 def star_flux(state, parts, wave_speed, contact, normal):
-    density, pressure, normal_speed, energy, sound_speed, conserved, flux_list = parts
+    density, pressure, normal_speed, energy, _, conserved, flux_list = parts
     factor = density * (wave_speed - normal_speed) / (wave_speed - contact)
     star_energy = factor * (
         energy / density
@@ -173,12 +174,16 @@
     return jnp.concatenate([lower, block[:, depth : rows - depth], upper], axis=1)
 
 
+def flat_ppermute(block, axis, pairs):
+    return lax.ppermute(block.reshape(-1), axis, pairs).reshape(block.shape)
+
+
 def halos(x, width):
     n_rad, n_az = lax.axis_size("rad"), lax.axis_size("az")
     from_below = lax.ppermute(x[:, -width:], "rad", ring_pairs(n_rad, 1, False))
     from_above = lax.ppermute(x[:, :width], "rad", ring_pairs(n_rad, -1, False))
-    from_left = lax.ppermute(x[..., -width:], "az", ring_pairs(n_az, 1, True))
-    from_right = lax.ppermute(x[..., :width], "az", ring_pairs(n_az, -1, True))
+    from_left = flat_ppermute(x[..., -width:], "az", ring_pairs(n_az, 1, True))
+    from_right = flat_ppermute(x[..., :width], "az", ring_pairs(n_az, -1, True))
     along_rad = clamp_rows(jnp.concatenate([from_below, x, from_above], axis=1), width)
     along_az = jnp.concatenate([from_left, x, from_right], axis=3)
     return along_rad, along_az

time: 96.8 us -> 94.4 us (0.975)
  waiting for transfers between devices: 32.9 us -> 29.2 us
  local copies, waits for them, and re-layouts: 2.19 us -> 3.79 us
    ppermute x4, waiting for transfers between devices: 3.17 us -> 0.9 us  [flat_ppermute(): return lax.ppermute(block.reshape(-1), axis, pairs).reshape(block.shape)]
    reshape x0 -> x8, local copies, waits for them, and re-layouts: none -> 1.59 us  [flat_ppermute(): return lax.ppermute(block.reshape(-1), axis, pairs).reshape(block.shape)]
    ppermute x3, waiting for transfers between devices: 29.8 us -> 28.3 us  [shifted(): return lax.ppermute(block, axis, route)]
  transfers between devices with their start and end apart: 11 -> 11, of which waited for: 4 -> 3; matrix products, arithmetic and copies ran while one was open for 12% -> 14% of each run, Pallas kernels for 0% -> 0%
where the time goes in v5:
time: 94.4 us; the launch traced here: 94 us
  starting transfers between devices  45.4 us (48%)
  waiting for transfers between devices  29.2 us (31%)
  other arithmetic  11.7 us (12%)
  local copies, waits for them, and re-layouts  3.79 us (4%)
  matrix products  3 us (3%)
    ppermute x4, starting transfers between devices, flat_ppermute(): return lax.ppermute(block.reshape(-1), axis, pairs).reshape(block.shape)  28.6 us
    ppermute x3, waiting for transfers between devices, shifted(): return lax.ppermute(block, axis, route)  28.3 us
    ppermute x2, starting transfers between devices, halos(): from_below = lax.ppermute(x[:, -width:], 'rad', ring_pairs(n_rad, 1, False))  6.44 us
    ppermute x3, starting transfers between devices, shifted(): return lax.ppermute(block, axis, route)  5.75 us
    unnamed x27, other arithmetic  4.96 us
    ppermute x2, starting transfers between devices, halos(): from_above = lax.ppermute(x[:, :width], 'rad', ring_pairs(n_rad, -1, False))  4.62 us
    dot_general x4, matrix products, shift_rows(): jnp.einsum('fitk,ikc->fitc', block, pick, precision=lax.Precision.HIGHEST...  3 us
    select_n x6, other arithmetic, edge_states(): jnp.where(spread * middle > spread * spread / 6.0, 3.0 * middle_cell - 2....  2.25 us
  transfers between devices with their start and end apart: 11, of which 3 were waited for; matrix products, arithmetic and copies ran while one was open for 14% of the time, Pallas kernels for 0%

profile of v5, /device:TPU:56, one launch (start us, length us, event | category | flops | bytes accessed | tf_op | source)
XLA Modules:
  0.0 94.0 jit_solution(5696492788352362579)
XLA Ops:
  0.0 1.0 %fusion.233 = (f32[5,3,8,256]{3,2,0,1:T(8,128)S(1)}, f32[5,3,8,256]{3,2,0,1:T(8,128)S(1)}) fusion(f32[5,6,8,256]{3,2,1,0:T(8,128)} %param.2), kind=kLoop, calls=%fused_computation.429 | loop fusion | bytes 491520 | tf_op jit(solution)/shard_map/slice | solution.py:183
  1.0 2.7 %collective-permute-start.1 = (f32[5,3,8,256]{3,2,0,1:T(8,128)S(1)}, f32[5,3,8,256]{3,2,0,1:T(8,128)S(1)}, u32[]{:S(2)}, u32[]{:S(2)}) collective-permute-start(f32[5,3,8,256]{3,2,0,1:T(8,128)S(1)} %get-tuple-element.34), channel_id=1, source_target_pairs={{24,0},{48,24},{72,48},{96,72},{120,96},{144,120},{168,144},{192,1... | collective-permute-start | bytes 368648 | tf_op jit(solution)/shard_map/ppermute | solution.py:184
  3.7 1.9 %collective-permute-start = (f32[5,3,8,256]{3,2,0,1:T(8,128)S(1)}, f32[5,3,8,256]{3,2,0,1:T(8,128)S(1)}, u32[]{:S(2)}, u32[]{:S(2)}) collective-permute-start(f32[5,3,8,256]{3,2,0,1:T(8,128)S(1)} %get-tuple-element.33), channel_id=1, source_target_pairs={{0,24},{24,48},{48,72},{72,96},{96,120},{120,144},{144,168},{168,1... | collective-permute-start | bytes 368648 | tf_op jit(solution)/shard_map/ppermute | solution.py:183
  6.0 4.3 %collective-permute-start.2 = (f32[720]{0:T(1024)S(1)}, f32[720]{0:T(1024)S(1)}, u32[]{:S(2)}, u32[]{:S(2)}) collective-permute-start(f32[720]{0:T(1024)S(1)} %reshape.62), channel_id=1, source_target_pairs={{0,1},{1,2},{2,3},{3,4},{4,5},{5,6},{6,7},{7,8},{8,9},{9,10},{10,1... | collective-permute-start | bytes 8648 | tf_op jit(solution)/shard_map/ppermute | solution.py:178
  10.5 14.7 %collective-permute-start.3 = (f32[720]{0:T(1024)S(1)}, f32[720]{0:T(1024)S(1)}, u32[]{:S(2)}, u32[]{:S(2)}) collective-permute-start(f32[720]{0:T(1024)S(1)} %reshape.64), channel_id=1, source_target_pairs={{0,23},{1,0},{2,1},{3,2},{4,3},{5,4},{6,5},{7,6},{8,7},{9,8},{10,9... | collective-permute-start | bytes 8648 | tf_op jit(solution)/shard_map/ppermute | solution.py:178
  25.7 0.5 subtract_select_fusion.2
  28.8 0.4 subtract_select_fusion.6
  32.1 4.5 %collective-permute-start.4 = (f32[5,3,8,256]{3,2,0,1:T(8,128)S(1)}, f32[5,3,8,256]{3,2,0,1:T(8,128)S(1)}, u32[]{:S(2)}, u32[]{:S(2)}) collective-permute-start(f32[5,3,8,256]{3,2,0,1:T(8,128)S(1)} %get-tuple-element.23), channel_id=1, source_target_pairs={{0,24},{24,48},{48,72},{72,96},{96,120},{120,144},{144,168},{168,1... | collective-permute-start | bytes 368648 | tf_op jit(solution)/shard_map/ppermute | solution.py:183
  36.7 1.9 %collective-permute-start.5 = (f32[5,3,8,256]{3,2,0,1:T(8,128)S(1)}, f32[5,3,8,256]{3,2,0,1:T(8,128)S(1)}, u32[]{:S(2)}, u32[]{:S(2)}) collective-permute-start(f32[5,3,8,256]{3,2,0,1:T(8,128)S(1)} %get-tuple-element.24), channel_id=1, source_target_pairs={{24,0},{48,24},{72,48},{96,72},{120,96},{144,120},{168,144},{192,1... | collective-permute-start | bytes 368648 | tf_op jit(solution)/shard_map/ppermute | solution.py:184
  39.1 0.5 subtract_select_fusion
  41.1 1.9 %collective-permute-start.6 = (f32[720]{0:T(1024)S(1)}, f32[720]{0:T(1024)S(1)}, u32[]{:S(2)}, u32[]{:S(2)}) collective-permute-start(f32[720]{0:T(1024)S(1)} %reshape.68), channel_id=1, source_target_pairs={{0,1},{1,2},{2,3},{3,4},{4,5},{5,6},{6,7},{7,8},{8,9},{9,10},{10,1... | collective-permute-start | bytes 8648 | tf_op jit(solution)/shard_map/ppermute | solution.py:178
  43.3 7.7 %collective-permute-start.7 = (f32[720]{0:T(1024)S(1)}, f32[720]{0:T(1024)S(1)}, u32[]{:S(2)}, u32[]{:S(2)}) collective-permute-start(f32[720]{0:T(1024)S(1)} %reshape.70), channel_id=1, source_target_pairs={{0,23},{1,0},{2,1},{3,2},{4,3},{5,4},{6,5},{7,6},{8,7},{9,8},{10,9... | collective-permute-start | bytes 8648 | tf_op jit(solution)/shard_map/ppermute | solution.py:178
  51.2 0.9 collective-permute-done.7
  52.9 0.4 subtract_select_fusion.4
  56.1 1.9 %collective-permute-start.8 = (f32[5,6,8,256]{3,2,0,1:T(8,128)S(1)}, f32[5,6,8,256]{3,2,0,1:T(8,128)S(1)}, u32[]{:S(2)}, u32[]{:S(2)}) collective-permute-start(f32[5,6,8,256]{3,2,0,1:T(8,128)S(1)} %pad_maximum_fusion.9), channel_id=1, source_target_pairs={{23,0},{0,1},{1,2},{2,3},{3,4},{4,5},{5,6},{6,7},{7,8},{8,9},{9,10... | collective-permute-start | bytes 737288 | tf_op jit(solution)/shard_map/ppermute | solution.py:16
  58.0 1.9 %collective-permute-start.9 = (f32[5,6,8,256]{3,2,0,1:T(8,128)S(1)}, f32[5,6,8,256]{3,2,0,1:T(8,128)S(1)}, u32[]{:S(2)}, u32[]{:S(2)}) collective-permute-start(f32[5,6,8,256]{3,2,0,1:T(8,128)S(1)} %pad_maximum_fusion.9), channel_id=1, source_target_pairs={{22,0},{23,1},{0,2},{1,3},{2,4},{3,5},{4,6},{5,7},{6,8},{7,9},{8,1... | collective-permute-start | bytes 737288 | tf_op jit(solution)/shard_map/ppermute | solution.py:16
  60.0 0.8 fusion.1
  60.8 20.0 %collective-permute-done.9 = f32[5,6,8,256]{3,2,0,1:T(8,128)S(1)} collective-permute-done((f32[5,6,8,256]{3,2,0,1:T(8,128)S(1)}, f32[5,6,8,256]{3,2,0,1:T(8,128)S(1)}, u32[]{:S(2)}, u32[]{:S(2)}) %collective-permute-start.9) | collective-permute-done | bytes 245792 | tf_op jit(solution)/shard_map/ppermute | solution.py:16
  80.8 1.9 %collective-permute-start.10 = (f32[5,6,8,256]{3,2,0,1:T(8,128)S(1)}, f32[5,6,8,256]{3,2,0,1:T(8,128)S(1)}, u32[]{:S(2)}, u32[]{:S(2)}) collective-permute-start(f32[5,6,8,256]{3,2,0,1:T(8,128)S(1)} %collective-permute-done.9), channel_id=1, source_target_pairs={{23,0},{0,1},{1,2},{2,3},{3,4},{4,5},{5,6},{6,7},{7,8},{8,9},{9,10... | collective-permute-start | bytes 737288 | tf_op jit(solution)/shard_map/ppermute | solution.py:16
  82.7 0.8 fusion.21
  83.5 0.8 fusion.18
  84.3 8.2 %collective-permute-done.10 = f32[5,6,8,256]{3,2,0,1:T(8,128)S(1)} collective-permute-done((f32[5,6,8,256]{3,2,0,1:T(8,128)S(1)}, f32[5,6,8,256]{3,2,0,1:T(8,128)S(1)}, u32[]{:S(2)}, u32[]{:S(2)}) %collective-permute-start.10) | collective-permute-done | bytes 245792 | tf_op jit(solution)/shard_map/ppermute | solution.py:16
  92.5 0.7 fusion.15
  93.3 0.7 copy.56
  (102 shorter events, 12.1 us)
Async XLA Ops:
  0.0 5.7 %copy-start = (f32[5,6,8,256]{3,2,1,0:T(8,128)S(1)}, f32[5,6,8,256]{3,2,1,0:T(8,128)}, u32[]{:S(2)}) copy-start(f32[5,6,8,256]{3,2,1,0:T(8,128)} %param.2) | copy-start | bytes 737284
  1.0 29.4 %collective-permute-start.1 = (f32[5,3,8,256]{3,2,0,1:T(8,128)S(1)}, f32[5,3,8,256]{3,2,0,1:T(8,128)S(1)}, u32[]{:S(2)}, u32[]{:S(2)}) collective-permute-start(f32[5,3,8,256]{3,2,0,1:T(8,128)S(1)} %get-tuple-element.34), channel_id=1, source_target_pairs={{24,0},{48,24},{72,48},{96,72},{120,96},{144,120},{168,144},{192,1... | collective-permute-start | bytes 368648 | tf_op jit(solution)/shard_map/ppermute | solution.py:184
  3.7 26.7 %collective-permute-start = (f32[5,3,8,256]{3,2,0,1:T(8,128)S(1)}, f32[5,3,8,256]{3,2,0,1:T(8,128)S(1)}, u32[]{:S(2)}, u32[]{:S(2)}) collective-permute-start(f32[5,3,8,256]{3,2,0,1:T(8,128)S(1)} %get-tuple-element.33), channel_id=1, source_target_pairs={{0,24},{24,48},{48,72},{72,96},{96,120},{120,144},{144,168},{168,1... | collective-permute-start | bytes 368648 | tf_op jit(solution)/shard_map/ppermute | solution.py:183
  6.0 21.7 %collective-permute-start.2 = (f32[720]{0:T(1024)S(1)}, f32[720]{0:T(1024)S(1)}, u32[]{:S(2)}, u32[]{:S(2)}) collective-permute-start(f32[720]{0:T(1024)S(1)} %reshape.62), channel_id=1, source_target_pairs={{0,1},{1,2},{2,3},{3,4},{4,5},{5,6},{6,7},{7,8},{8,9},{9,10},{10,1... | collective-permute-start | bytes 8648 | tf_op jit(solution)/shard_map/ppermute | solution.py:178
  10.5 17.4 %collective-permute-start.3 = (f32[720]{0:T(1024)S(1)}, f32[720]{0:T(1024)S(1)}, u32[]{:S(2)}, u32[]{:S(2)}) collective-permute-start(f32[720]{0:T(1024)S(1)} %reshape.64), channel_id=1, source_target_pairs={{0,23},{1,0},{2,1},{3,2},{4,3},{5,4},{6,5},{7,6},{8,7},{9,8},{10,9... | collective-permute-start | bytes 8648 | tf_op jit(solution)/shard_map/ppermute | solution.py:178
  32.1 22.4 %collective-permute-start.4 = (f32[5,3,8,256]{3,2,0,1:T(8,128)S(1)}, f32[5,3,8,256]{3,2,0,1:T(8,128)S(1)}, u32[]{:S(2)}, u32[]{:S(2)}) collective-permute-start(f32[5,3,8,256]{3,2,0,1:T(8,128)S(1)} %get-tuple-element.23), channel_id=1, source_target_pairs={{0,24},{24,48},{48,72},{72,96},{96,120},{120,144},{144,168},{168,1... | collective-permute-start | bytes 368648 | tf_op jit(solution)/shard_map/ppermute | solution.py:183
  36.7 17.9 %collective-permute-start.5 = (f32[5,3,8,256]{3,2,0,1:T(8,128)S(1)}, f32[5,3,8,256]{3,2,0,1:T(8,128)S(1)}, u32[]{:S(2)}, u32[]{:S(2)}) collective-permute-start(f32[5,3,8,256]{3,2,0,1:T(8,128)S(1)} %get-tuple-element.24), channel_id=1, source_target_pairs={{24,0},{48,24},{72,48},{96,72},{120,96},{144,120},{168,144},{192,1... | collective-permute-start | bytes 368648 | tf_op jit(solution)/shard_map/ppermute | solution.py:184
  41.1 9.9 %collective-permute-start.6 = (f32[720]{0:T(1024)S(1)}, f32[720]{0:T(1024)S(1)}, u32[]{:S(2)}, u32[]{:S(2)}) collective-permute-start(f32[720]{0:T(1024)S(1)} %reshape.68), channel_id=1, source_target_pairs={{0,1},{1,2},{2,3},{3,4},{4,5},{5,6},{6,7},{7,8},{8,9},{9,10},{10,1... | collective-permute-start | bytes 8648 | tf_op jit(solution)/shard_map/ppermute | solution.py:178
  43.3 8.8 %collective-permute-start.7 = (f32[720]{0:T(1024)S(1)}, f32[720]{0:T(1024)S(1)}, u32[]{:S(2)}, u32[]{:S(2)}) collective-permute-start(f32[720]{0:T(1024)S(1)} %reshape.70), channel_id=1, source_target_pairs={{0,23},{1,0},{2,1},{3,2},{4,3},{5,4},{6,5},{7,6},{8,7},{9,8},{10,9... | collective-permute-start | bytes 8648 | tf_op jit(solution)/shard_map/ppermute | solution.py:178
  56.1 4.0 %copy-start.1 = (s32[6]{0:T(128)S(1)}, s32[6]{0:T(128)}, u32[]{:S(2)}) copy-start(s32[6]{0:T(128)} %param.3) | copy-start | bytes 76
  56.1 26.6 %collective-permute-start.8 = (f32[5,6,8,256]{3,2,0,1:T(8,128)S(1)}, f32[5,6,8,256]{3,2,0,1:T(8,128)S(1)}, u32[]{:S(2)}, u32[]{:S(2)}) collective-permute-start(f32[5,6,8,256]{3,2,0,1:T(8,128)S(1)} %pad_maximum_fusion.9), channel_id=1, source_target_pairs={{23,0},{0,1},{1,2},{2,3},{3,4},{4,5},{5,6},{6,7},{7,8},{8,9},{9,10... | collective-permute-start | bytes 737288 | tf_op jit(solution)/shard_map/ppermute | solution.py:16
  58.0 22.8 %collective-permute-start.9 = (f32[5,6,8,256]{3,2,0,1:T(8,128)S(1)}, f32[5,6,8,256]{3,2,0,1:T(8,128)S(1)}, u32[]{:S(2)}, u32[]{:S(2)}) collective-permute-start(f32[5,6,8,256]{3,2,0,1:T(8,128)S(1)} %pad_maximum_fusion.9), channel_id=1, source_target_pairs={{22,0},{23,1},{0,2},{1,3},{2,4},{3,5},{4,6},{5,7},{6,8},{7,9},{8,1... | collective-permute-start | bytes 737288 | tf_op jit(solution)/shard_map/ppermute | solution.py:16
  80.8 11.7 %collective-permute-start.10 = (f32[5,6,8,256]{3,2,0,1:T(8,128)S(1)}, f32[5,6,8,256]{3,2,0,1:T(8,128)S(1)}, u32[]{:S(2)}, u32[]{:S(2)}) collective-permute-start(f32[5,6,8,256]{3,2,0,1:T(8,128)S(1)} %collective-permute-done.9), channel_id=1, source_target_pairs={{23,0},{0,1},{1,2},{2,3},{3,4},{4,5},{5,6},{6,7},{7,8},{8,9},{9,10... | collective-permute-start | bytes 737288 | tf_op jit(solution)/shard_map/ppermute | solution.py:16

commit v6 on v5

--- a/solution.py
+++ b/solution.py
@@ -115,7 +115,9 @@
 
 def tendency(along_rad, along_az, inner, courant_rows):
     radial_term = flux_difference(along_rad, 1, 1)
-    polar_term = flux_difference(jnp.pad(inner, ((0, 0), (0, 0), (3, 3), (0, 0)), mode="edge"), 2, 2)
+    polar_term = flux_difference(
+        jnp.pad(inner, ((0, 0), (0, 0), (3, 3), (0, 0)), mode="edge"), 2, 2
+    )
     azimuth_term = flux_difference(along_az, 3, 3)
     return -(
         COURANT_RADIAL * radial_term
@@ -231,7 +233,9 @@
     initial = to_conserved(fields)
     section_one = initial + change(fields, courant_inner)
     section_one_prim = to_primitive(section_one)
-    section_two = 0.5 * initial + 0.5 * (section_one + change(section_one_prim, courant_inner))
+    section_two = 0.5 * initial + 0.5 * (
+        section_one + change(section_one_prim, courant_inner)
+    )
     return shift_rows(to_primitive(section_two), shifts)
 
 

time: 94.4 us -> 94.4 us (level)
  no operation moved by 1% of the time
where the time goes in v6:
time: 94.4 us; the launch traced here: 94 us
  starting transfers between devices  45.4 us (48%)
  waiting for transfers between devices  29.2 us (31%)
  other arithmetic  11.7 us (12%)
  local copies, waits for them, and re-layouts  3.79 us (4%)
  matrix products  3 us (3%)
    ppermute x4, starting transfers between devices, flat_ppermute(): return lax.ppermute(block.reshape(-1), axis, pairs).reshape(block.shape)  28.6 us
    ppermute x3, waiting for transfers between devices, shifted(): return lax.ppermute(block, axis, route)  28.3 us
    ppermute x2, starting transfers between devices, halos(): from_below = lax.ppermute(x[:, -width:], 'rad', ring_pairs(n_rad, 1, False))  6.44 us
    ppermute x3, starting transfers between devices, shifted(): return lax.ppermute(block, axis, route)  5.75 us
    unnamed x27, other arithmetic  4.96 us
    ppermute x2, starting transfers between devices, halos(): from_above = lax.ppermute(x[:, :width], 'rad', ring_pairs(n_rad, -1, False))  4.62 us
    dot_general x4, matrix products, shift_rows(): jnp.einsum('fitk,ikc->fitc', block, pick, precision=lax.Precision.HIGHEST...  3 us
    select_n x6, other arithmetic, edge_states(): jnp.where(spread * middle > spread * spread / 6.0, 3.0 * middle_cell - 2....  2.25 us
  transfers between devices with their start and end apart: 11, of which 3 were waited for; matrix products, arithmetic and copies ran while one was open for 14% of the time, Pallas kernels for 0%

profile of v6, /device:TPU:56, one launch (start us, length us, event | category | flops | bytes accessed | tf_op | source)
XLA Modules:
  0.0 94.0 jit_solution(5696492788352362579)
XLA Ops:
  0.0 1.0 %fusion.233 = (f32[5,3,8,256]{3,2,0,1:T(8,128)S(1)}, f32[5,3,8,256]{3,2,0,1:T(8,128)S(1)}) fusion(f32[5,6,8,256]{3,2,1,0:T(8,128)} %param.2), kind=kLoop, calls=%fused_computation.429 | loop fusion | bytes 491520 | tf_op jit(solution)/shard_map/slice | solution.py:185
  1.0 2.7 %collective-permute-start.1 = (f32[5,3,8,256]{3,2,0,1:T(8,128)S(1)}, f32[5,3,8,256]{3,2,0,1:T(8,128)S(1)}, u32[]{:S(2)}, u32[]{:S(2)}) collective-permute-start(f32[5,3,8,256]{3,2,0,1:T(8,128)S(1)} %get-tuple-element.34), channel_id=1, source_target_pairs={{24,0},{48,24},{72,48},{96,72},{120,96},{144,120},{168,144},{192,1... | collective-permute-start | bytes 368648 | tf_op jit(solution)/shard_map/ppermute | solution.py:186
  3.7 1.9 %collective-permute-start = (f32[5,3,8,256]{3,2,0,1:T(8,128)S(1)}, f32[5,3,8,256]{3,2,0,1:T(8,128)S(1)}, u32[]{:S(2)}, u32[]{:S(2)}) collective-permute-start(f32[5,3,8,256]{3,2,0,1:T(8,128)S(1)} %get-tuple-element.33), channel_id=1, source_target_pairs={{0,24},{24,48},{48,72},{72,96},{96,120},{120,144},{144,168},{168,1... | collective-permute-start | bytes 368648 | tf_op jit(solution)/shard_map/ppermute | solution.py:185
  6.0 4.3 %collective-permute-start.2 = (f32[720]{0:T(1024)S(1)}, f32[720]{0:T(1024)S(1)}, u32[]{:S(2)}, u32[]{:S(2)}) collective-permute-start(f32[720]{0:T(1024)S(1)} %reshape.62), channel_id=1, source_target_pairs={{0,1},{1,2},{2,3},{3,4},{4,5},{5,6},{6,7},{7,8},{8,9},{9,10},{10,1... | collective-permute-start | bytes 8648 | tf_op jit(solution)/shard_map/ppermute | solution.py:180
  10.5 14.7 %collective-permute-start.3 = (f32[720]{0:T(1024)S(1)}, f32[720]{0:T(1024)S(1)}, u32[]{:S(2)}, u32[]{:S(2)}) collective-permute-start(f32[720]{0:T(1024)S(1)} %reshape.64), channel_id=1, source_target_pairs={{0,23},{1,0},{2,1},{3,2},{4,3},{5,4},{6,5},{7,6},{8,7},{9,8},{10,9... | collective-permute-start | bytes 8648 | tf_op jit(solution)/shard_map/ppermute | solution.py:180
  25.7 0.5 subtract_select_fusion.2
  28.8 0.4 subtract_select_fusion.6
  32.1 4.5 %collective-permute-start.4 = (f32[5,3,8,256]{3,2,0,1:T(8,128)S(1)}, f32[5,3,8,256]{3,2,0,1:T(8,128)S(1)}, u32[]{:S(2)}, u32[]{:S(2)}) collective-permute-start(f32[5,3,8,256]{3,2,0,1:T(8,128)S(1)} %get-tuple-element.23), channel_id=1, source_target_pairs={{0,24},{24,48},{48,72},{72,96},{96,120},{120,144},{144,168},{168,1... | collective-permute-start | bytes 368648 | tf_op jit(solution)/shard_map/ppermute | solution.py:185
  36.7 1.9 %collective-permute-start.5 = (f32[5,3,8,256]{3,2,0,1:T(8,128)S(1)}, f32[5,3,8,256]{3,2,0,1:T(8,128)S(1)}, u32[]{:S(2)}, u32[]{:S(2)}) collective-permute-start(f32[5,3,8,256]{3,2,0,1:T(8,128)S(1)} %get-tuple-element.24), channel_id=1, source_target_pairs={{24,0},{48,24},{72,48},{96,72},{120,96},{144,120},{168,144},{192,1... | collective-permute-start | bytes 368648 | tf_op jit(solution)/shard_map/ppermute | solution.py:186
  39.1 0.5 subtract_select_fusion
  41.1 1.9 %collective-permute-start.6 = (f32[720]{0:T(1024)S(1)}, f32[720]{0:T(1024)S(1)}, u32[]{:S(2)}, u32[]{:S(2)}) collective-permute-start(f32[720]{0:T(1024)S(1)} %reshape.68), channel_id=1, source_target_pairs={{0,1},{1,2},{2,3},{3,4},{4,5},{5,6},{6,7},{7,8},{8,9},{9,10},{10,1... | collective-permute-start | bytes 8648 | tf_op jit(solution)/shard_map/ppermute | solution.py:180
  43.3 7.7 %collective-permute-start.7 = (f32[720]{0:T(1024)S(1)}, f32[720]{0:T(1024)S(1)}, u32[]{:S(2)}, u32[]{:S(2)}) collective-permute-start(f32[720]{0:T(1024)S(1)} %reshape.70), channel_id=1, source_target_pairs={{0,23},{1,0},{2,1},{3,2},{4,3},{5,4},{6,5},{7,6},{8,7},{9,8},{10,9... | collective-permute-start | bytes 8648 | tf_op jit(solution)/shard_map/ppermute | solution.py:180
  51.2 0.9 collective-permute-done.7
  52.9 0.4 subtract_select_fusion.4
  56.1 1.9 %collective-permute-start.8 = (f32[5,6,8,256]{3,2,0,1:T(8,128)S(1)}, f32[5,6,8,256]{3,2,0,1:T(8,128)S(1)}, u32[]{:S(2)}, u32[]{:S(2)}) collective-permute-start(f32[5,6,8,256]{3,2,0,1:T(8,128)S(1)} %pad_maximum_fusion.9), channel_id=1, source_target_pairs={{23,0},{0,1},{1,2},{2,3},{3,4},{4,5},{5,6},{6,7},{7,8},{8,9},{9,10... | collective-permute-start | bytes 737288 | tf_op jit(solution)/shard_map/ppermute | solution.py:16
  58.0 1.9 %collective-permute-start.9 = (f32[5,6,8,256]{3,2,0,1:T(8,128)S(1)}, f32[5,6,8,256]{3,2,0,1:T(8,128)S(1)}, u32[]{:S(2)}, u32[]{:S(2)}) collective-permute-start(f32[5,6,8,256]{3,2,0,1:T(8,128)S(1)} %pad_maximum_fusion.9), channel_id=1, source_target_pairs={{22,0},{23,1},{0,2},{1,3},{2,4},{3,5},{4,6},{5,7},{6,8},{7,9},{8,1... | collective-permute-start | bytes 737288 | tf_op jit(solution)/shard_map/ppermute | solution.py:16
  60.0 0.8 fusion.1
  60.8 20.0 %collective-permute-done.9 = f32[5,6,8,256]{3,2,0,1:T(8,128)S(1)} collective-permute-done((f32[5,6,8,256]{3,2,0,1:T(8,128)S(1)}, f32[5,6,8,256]{3,2,0,1:T(8,128)S(1)}, u32[]{:S(2)}, u32[]{:S(2)}) %collective-permute-start.9) | collective-permute-done | bytes 245792 | tf_op jit(solution)/shard_map/ppermute | solution.py:16
  80.8 1.9 %collective-permute-start.10 = (f32[5,6,8,256]{3,2,0,1:T(8,128)S(1)}, f32[5,6,8,256]{3,2,0,1:T(8,128)S(1)}, u32[]{:S(2)}, u32[]{:S(2)}) collective-permute-start(f32[5,6,8,256]{3,2,0,1:T(8,128)S(1)} %collective-permute-done.9), channel_id=1, source_target_pairs={{23,0},{0,1},{1,2},{2,3},{3,4},{4,5},{5,6},{6,7},{7,8},{8,9},{9,10... | collective-permute-start | bytes 737288 | tf_op jit(solution)/shard_map/ppermute | solution.py:16
  82.7 0.8 fusion.21
  83.5 0.8 fusion.18
  84.3 8.2 %collective-permute-done.10 = f32[5,6,8,256]{3,2,0,1:T(8,128)S(1)} collective-permute-done((f32[5,6,8,256]{3,2,0,1:T(8,128)S(1)}, f32[5,6,8,256]{3,2,0,1:T(8,128)S(1)}, u32[]{:S(2)}, u32[]{:S(2)}) %collective-permute-start.10) | collective-permute-done | bytes 245792 | tf_op jit(solution)/shard_map/ppermute | solution.py:16
  92.5 0.7 fusion.15
  93.3 0.7 copy.56
  (102 shorter events, 12.1 us)
Async XLA Ops:
  0.0 5.7 %copy-start = (f32[5,6,8,256]{3,2,1,0:T(8,128)S(1)}, f32[5,6,8,256]{3,2,1,0:T(8,128)}, u32[]{:S(2)}) copy-start(f32[5,6,8,256]{3,2,1,0:T(8,128)} %param.2) | copy-start | bytes 737284
  1.0 29.4 %collective-permute-start.1 = (f32[5,3,8,256]{3,2,0,1:T(8,128)S(1)}, f32[5,3,8,256]{3,2,0,1:T(8,128)S(1)}, u32[]{:S(2)}, u32[]{:S(2)}) collective-permute-start(f32[5,3,8,256]{3,2,0,1:T(8,128)S(1)} %get-tuple-element.34), channel_id=1, source_target_pairs={{24,0},{48,24},{72,48},{96,72},{120,96},{144,120},{168,144},{192,1... | collective-permute-start | bytes 368648 | tf_op jit(solution)/shard_map/ppermute | solution.py:186
  3.7 26.7 %collective-permute-start = (f32[5,3,8,256]{3,2,0,1:T(8,128)S(1)}, f32[5,3,8,256]{3,2,0,1:T(8,128)S(1)}, u32[]{:S(2)}, u32[]{:S(2)}) collective-permute-start(f32[5,3,8,256]{3,2,0,1:T(8,128)S(1)} %get-tuple-element.33), channel_id=1, source_target_pairs={{0,24},{24,48},{48,72},{72,96},{96,120},{120,144},{144,168},{168,1... | collective-permute-start | bytes 368648 | tf_op jit(solution)/shard_map/ppermute | solution.py:185
  6.0 21.7 %collective-permute-start.2 = (f32[720]{0:T(1024)S(1)}, f32[720]{0:T(1024)S(1)}, u32[]{:S(2)}, u32[]{:S(2)}) collective-permute-start(f32[720]{0:T(1024)S(1)} %reshape.62), channel_id=1, source_target_pairs={{0,1},{1,2},{2,3},{3,4},{4,5},{5,6},{6,7},{7,8},{8,9},{9,10},{10,1... | collective-permute-start | bytes 8648 | tf_op jit(solution)/shard_map/ppermute | solution.py:180
  10.5 17.4 %collective-permute-start.3 = (f32[720]{0:T(1024)S(1)}, f32[720]{0:T(1024)S(1)}, u32[]{:S(2)}, u32[]{:S(2)}) collective-permute-start(f32[720]{0:T(1024)S(1)} %reshape.64), channel_id=1, source_target_pairs={{0,23},{1,0},{2,1},{3,2},{4,3},{5,4},{6,5},{7,6},{8,7},{9,8},{10,9... | collective-permute-start | bytes 8648 | tf_op jit(solution)/shard_map/ppermute | solution.py:180
  32.1 22.4 %collective-permute-start.4 = (f32[5,3,8,256]{3,2,0,1:T(8,128)S(1)}, f32[5,3,8,256]{3,2,0,1:T(8,128)S(1)}, u32[]{:S(2)}, u32[]{:S(2)}) collective-permute-start(f32[5,3,8,256]{3,2,0,1:T(8,128)S(1)} %get-tuple-element.23), channel_id=1, source_target_pairs={{0,24},{24,48},{48,72},{72,96},{96,120},{120,144},{144,168},{168,1... | collective-permute-start | bytes 368648 | tf_op jit(solution)/shard_map/ppermute | solution.py:185
  36.7 17.9 %collective-permute-start.5 = (f32[5,3,8,256]{3,2,0,1:T(8,128)S(1)}, f32[5,3,8,256]{3,2,0,1:T(8,128)S(1)}, u32[]{:S(2)}, u32[]{:S(2)}) collective-permute-start(f32[5,3,8,256]{3,2,0,1:T(8,128)S(1)} %get-tuple-element.24), channel_id=1, source_target_pairs={{24,0},{48,24},{72,48},{96,72},{120,96},{144,120},{168,144},{192,1... | collective-permute-start | bytes 368648 | tf_op jit(solution)/shard_map/ppermute | solution.py:186
  41.1 9.9 %collective-permute-start.6 = (f32[720]{0:T(1024)S(1)}, f32[720]{0:T(1024)S(1)}, u32[]{:S(2)}, u32[]{:S(2)}) collective-permute-start(f32[720]{0:T(1024)S(1)} %reshape.68), channel_id=1, source_target_pairs={{0,1},{1,2},{2,3},{3,4},{4,5},{5,6},{6,7},{7,8},{8,9},{9,10},{10,1... | collective-permute-start | bytes 8648 | tf_op jit(solution)/shard_map/ppermute | solution.py:180
  43.3 8.8 %collective-permute-start.7 = (f32[720]{0:T(1024)S(1)}, f32[720]{0:T(1024)S(1)}, u32[]{:S(2)}, u32[]{:S(2)}) collective-permute-start(f32[720]{0:T(1024)S(1)} %reshape.70), channel_id=1, source_target_pairs={{0,23},{1,0},{2,1},{3,2},{4,3},{5,4},{6,5},{7,6},{8,7},{9,8},{10,9... | collective-permute-start | bytes 8648 | tf_op jit(solution)/shard_map/ppermute | solution.py:180
  56.1 4.0 %copy-start.1 = (s32[6]{0:T(128)S(1)}, s32[6]{0:T(128)}, u32[]{:S(2)}) copy-start(s32[6]{0:T(128)} %param.3) | copy-start | bytes 76
  56.1 26.6 %collective-permute-start.8 = (f32[5,6,8,256]{3,2,0,1:T(8,128)S(1)}, f32[5,6,8,256]{3,2,0,1:T(8,128)S(1)}, u32[]{:S(2)}, u32[]{:S(2)}) collective-permute-start(f32[5,6,8,256]{3,2,0,1:T(8,128)S(1)} %pad_maximum_fusion.9), channel_id=1, source_target_pairs={{23,0},{0,1},{1,2},{2,3},{3,4},{4,5},{5,6},{6,7},{7,8},{8,9},{9,10... | collective-permute-start | bytes 737288 | tf_op jit(solution)/shard_map/ppermute | solution.py:16
  58.0 22.8 %collective-permute-start.9 = (f32[5,6,8,256]{3,2,0,1:T(8,128)S(1)}, f32[5,6,8,256]{3,2,0,1:T(8,128)S(1)}, u32[]{:S(2)}, u32[]{:S(2)}) collective-permute-start(f32[5,6,8,256]{3,2,0,1:T(8,128)S(1)} %pad_maximum_fusion.9), channel_id=1, source_target_pairs={{22,0},{23,1},{0,2},{1,3},{2,4},{3,5},{4,6},{5,7},{6,8},{7,9},{8,1... | collective-permute-start | bytes 737288 | tf_op jit(solution)/shard_map/ppermute | solution.py:16
  80.8 11.7 %collective-permute-start.10 = (f32[5,6,8,256]{3,2,0,1:T(8,128)S(1)}, f32[5,6,8,256]{3,2,0,1:T(8,128)S(1)}, u32[]{:S(2)}, u32[]{:S(2)}) collective-permute-start(f32[5,6,8,256]{3,2,0,1:T(8,128)S(1)} %collective-permute-done.9), channel_id=1, source_target_pairs={{23,0},{0,1},{1,2},{2,3},{3,4},{4,5},{5,6},{6,7},{7,8},{8,9},{9,10... | collective-permute-start | bytes 737288 | tf_op jit(solution)/shard_map/ppermute | solution.py:16

commit v7 on v6

--- a/solution.py
+++ b/solution.py
@@ -176,16 +176,12 @@
     return jnp.concatenate([lower, block[:, depth : rows - depth], upper], axis=1)
 
 
-def flat_ppermute(block, axis, pairs):
-    return lax.ppermute(block.reshape(-1), axis, pairs).reshape(block.shape)
-
-
 def halos(x, width):
     n_rad, n_az = lax.axis_size("rad"), lax.axis_size("az")
     from_below = lax.ppermute(x[:, -width:], "rad", ring_pairs(n_rad, 1, False))
     from_above = lax.ppermute(x[:, :width], "rad", ring_pairs(n_rad, -1, False))
-    from_left = flat_ppermute(x[..., -width:], "az", ring_pairs(n_az, 1, True))
-    from_right = flat_ppermute(x[..., :width], "az", ring_pairs(n_az, -1, True))
+    from_left = lax.ppermute(x[..., -width:], "az", ring_pairs(n_az, 1, True))
+    from_right = lax.ppermute(x[..., :width], "az", ring_pairs(n_az, -1, True))
     along_rad = clamp_rows(jnp.concatenate([from_below, x, from_above], axis=1), width)
     along_az = jnp.concatenate([from_left, x, from_right], axis=3)
     return along_rad, along_az

time: 94.4 us -> 96.8 us (1.025)
  waiting for transfers between devices: 29.2 us -> 32.9 us
  local copies, waits for them, and re-layouts: 3.79 us -> 2.19 us
    ppermute x4, waiting for transfers between devices: 0.9 us -> 3.17 us  [the longest x2 1.98 us: halos(): from_left = lax.ppermute(x[..., -width:], 'az', ring_pairs(n_az, 1, True))]
    reshape x8 -> x0, local copies, waits for them, and re-layouts: 1.59 us -> none  [flat_ppermute(): return lax.ppermute(block.reshape(-1), axis, pairs).reshape(block.shape)]
    ppermute x3, waiting for transfers between devices: 28.3 us -> 29.8 us  [shifted(): return lax.ppermute(block, axis, route)]
  transfers between devices with their start and end apart: 11 -> 11, of which waited for: 3 -> 4; matrix products, arithmetic and copies ran while one was open for 14% -> 12% of each run, Pallas kernels for 0% -> 0%
where the time goes in v7:
time: 96.8 us; the launch traced here: 95.9 us
  starting transfers between devices  45.4 us (47%)
  waiting for transfers between devices  32.9 us (34%)
  other arithmetic  11.6 us (12%)
  matrix products  3 us (3%)
  local copies, waits for them, and re-layouts  2.19 us (2%)
    ppermute x3, waiting for transfers between devices, shifted(): return lax.ppermute(block, axis, route)  29.8 us
    ppermute x2, starting transfers between devices, halos(): from_right = lax.ppermute(x[..., :width], 'az', ring_pairs(n_az, -1, True))  22.4 us
    ppermute x2, starting transfers between devices, halos(): from_below = lax.ppermute(x[:, -width:], 'rad', ring_pairs(n_rad, 1, False))  6.44 us
    ppermute x2, starting transfers between devices, halos(): from_left = lax.ppermute(x[..., -width:], 'az', ring_pairs(n_az, 1, True))  6.2 us
    ppermute x3, starting transfers between devices, shifted(): return lax.ppermute(block, axis, route)  5.75 us
    unnamed x27, other arithmetic  4.96 us
    ppermute x2, starting transfers between devices, halos(): from_above = lax.ppermute(x[:, :width], 'rad', ring_pairs(n_rad, -1, False))  4.62 us
    dot_general x4, matrix products, shift_rows(): jnp.einsum('fitk,ikc->fitc', block, pick, precision=lax.Precision.HIGHEST...  3 us
  transfers between devices with their start and end apart: 11, of which 4 were waited for; matrix products, arithmetic and copies ran while one was open for 12% of the time, Pallas kernels for 0%

profile of v7, /device:TPU:56, one launch (start us, length us, event | category | flops | bytes accessed | tf_op | source)
XLA Modules:
  0.0 95.9 jit_solution(392766151678688734)
XLA Ops:
  0.0 1.0 %fusion.232 = (f32[5,3,8,256]{3,2,0,1:T(8,128)S(1)}, f32[5,3,8,256]{3,2,0,1:T(8,128)S(1)}) fusion(f32[5,6,8,256]{3,2,1,0:T(8,128)} %param.2), kind=kLoop, calls=%fused_computation.426 | loop fusion | bytes 491520 | tf_op jit(solution)/shard_map/slice | solution.py:181
  1.0 2.7 %collective-permute-start.1 = (f32[5,3,8,256]{3,2,0,1:T(8,128)S(1)}, f32[5,3,8,256]{3,2,0,1:T(8,128)S(1)}, u32[]{:S(2)}, u32[]{:S(2)}) collective-permute-start(f32[5,3,8,256]{3,2,0,1:T(8,128)S(1)} %get-tuple-element.32), channel_id=1, source_target_pairs={{24,0},{48,24},{72,48},{96,72},{120,96},{144,120},{168,144},{192,1... | collective-permute-start | bytes 368648 | tf_op jit(solution)/shard_map/ppermute | solution.py:182
  3.7 1.9 %collective-permute-start = (f32[5,3,8,256]{3,2,0,1:T(8,128)S(1)}, f32[5,3,8,256]{3,2,0,1:T(8,128)S(1)}, u32[]{:S(2)}, u32[]{:S(2)}) collective-permute-start(f32[5,3,8,256]{3,2,0,1:T(8,128)S(1)} %get-tuple-element.31), channel_id=1, source_target_pairs={{0,24},{24,48},{48,72},{72,96},{96,120},{120,144},{144,168},{168,1... | collective-permute-start | bytes 368648 | tf_op jit(solution)/shard_map/ppermute | solution.py:181
  5.8 4.3 %collective-permute-start.2 = (f32[5,6,8,3]{3,2,0,1:T(8,128)S(1)}, f32[5,6,8,3]{3,2,0,1:T(8,128)S(1)}, u32[]{:S(2)}, u32[]{:S(2)}) collective-permute-start(f32[5,6,8,3]{3,2,0,1:T(8,128)S(1)} %get-tuple-element.35), channel_id=1, source_target_pairs={{0,1},{1,2},{2,3},{3,4},{4,5},{5,6},{6,7},{7,8},{8,9},{9,10},{10,1... | collective-permute-start | bytes 8648 | tf_op jit(solution)/shard_map/ppermute | solution.py:183
  10.1 14.7 %collective-permute-start.3 = (f32[5,6,8,3]{3,2,0,1:T(8,128)S(1)}, f32[5,6,8,3]{3,2,0,1:T(8,128)S(1)}, u32[]{:S(2)}, u32[]{:S(2)}) collective-permute-start(f32[5,6,8,3]{3,2,0,1:T(8,128)S(1)} %get-tuple-element.36), channel_id=1, source_target_pairs={{0,23},{1,0},{2,1},{3,2},{4,3},{5,4},{6,5},{7,6},{8,7},{9,8},{10,9... | collective-permute-start | bytes 8648 | tf_op jit(solution)/shard_map/ppermute | solution.py:184
  25.3 0.5 subtract_select_fusion.2
  27.8 0.4 subtract_select_fusion.6
  31.2 4.5 %collective-permute-start.4 = (f32[5,3,8,256]{3,2,0,1:T(8,128)S(1)}, f32[5,3,8,256]{3,2,0,1:T(8,128)S(1)}, u32[]{:S(2)}, u32[]{:S(2)}) collective-permute-start(f32[5,3,8,256]{3,2,0,1:T(8,128)S(1)} %get-tuple-element.21), channel_id=1, source_target_pairs={{0,24},{24,48},{48,72},{72,96},{96,120},{120,144},{144,168},{168,1... | collective-permute-start | bytes 368648 | tf_op jit(solution)/shard_map/ppermute | solution.py:181
  35.7 1.9 %collective-permute-start.5 = (f32[5,3,8,256]{3,2,0,1:T(8,128)S(1)}, f32[5,3,8,256]{3,2,0,1:T(8,128)S(1)}, u32[]{:S(2)}, u32[]{:S(2)}) collective-permute-start(f32[5,3,8,256]{3,2,0,1:T(8,128)S(1)} %get-tuple-element.22), channel_id=1, source_target_pairs={{24,0},{48,24},{72,48},{96,72},{120,96},{144,120},{168,144},{192,1... | collective-permute-start | bytes 368648 | tf_op jit(solution)/shard_map/ppermute | solution.py:182
  38.1 0.5 subtract_select_fusion
  40.0 1.9 %collective-permute-start.6 = (f32[5,6,8,3]{3,2,0,1:T(8,128)S(1)}, f32[5,6,8,3]{3,2,0,1:T(8,128)S(1)}, u32[]{:S(2)}, u32[]{:S(2)}) collective-permute-start(f32[5,6,8,3]{3,2,0,1:T(8,128)S(1)} %get-tuple-element.25), channel_id=1, source_target_pairs={{0,1},{1,2},{2,3},{3,4},{4,5},{5,6},{6,7},{7,8},{8,9},{9,10},{10,1... | collective-permute-start | bytes 8648 | tf_op jit(solution)/shard_map/ppermute | solution.py:183
  41.9 7.7 %collective-permute-start.7 = (f32[5,6,8,3]{3,2,0,1:T(8,128)S(1)}, f32[5,6,8,3]{3,2,0,1:T(8,128)S(1)}, u32[]{:S(2)}, u32[]{:S(2)}) collective-permute-start(f32[5,6,8,3]{3,2,0,1:T(8,128)S(1)} %get-tuple-element.26), channel_id=1, source_target_pairs={{0,23},{1,0},{2,1},{3,2},{4,3},{5,4},{6,5},{7,6},{8,7},{9,8},{10,9... | collective-permute-start | bytes 8648 | tf_op jit(solution)/shard_map/ppermute | solution.py:184
  49.6 2.0 %collective-permute-done.6 = f32[5,6,8,3]{3,2,0,1:T(8,128)S(1)} collective-permute-done((f32[5,6,8,3]{3,2,0,1:T(8,128)S(1)}, f32[5,6,8,3]{3,2,0,1:T(8,128)S(1)}, u32[]{:S(2)}, u32[]{:S(2)}) %collective-permute-start.6) | collective-permute-done | bytes 2912 | tf_op jit(solution)/shard_map/ppermute | solution.py:183
  51.6 1.2 %collective-permute-done.7 = f32[5,6,8,3]{3,2,0,1:T(8,128)S(1)} collective-permute-done((f32[5,6,8,3]{3,2,0,1:T(8,128)S(1)}, f32[5,6,8,3]{3,2,0,1:T(8,128)S(1)}, u32[]{:S(2)}, u32[]{:S(2)}) %collective-permute-start.7) | collective-permute-done | bytes 2912 | tf_op jit(solution)/shard_map/ppermute | solution.py:184
  56.6 1.9 %collective-permute-start.8 = (f32[5,6,8,256]{3,2,0,1:T(8,128)S(1)}, f32[5,6,8,256]{3,2,0,1:T(8,128)S(1)}, u32[]{:S(2)}, u32[]{:S(2)}) collective-permute-start(f32[5,6,8,256]{3,2,0,1:T(8,128)S(1)} %pad_maximum_fusion.7), channel_id=1, source_target_pairs={{23,0},{0,1},{1,2},{2,3},{3,4},{4,5},{5,6},{6,7},{7,8},{8,9},{9,10... | collective-permute-start | bytes 737288 | tf_op jit(solution)/shard_map/ppermute | solution.py:16
  58.5 1.9 %collective-permute-start.9 = (f32[5,6,8,256]{3,2,0,1:T(8,128)S(1)}, f32[5,6,8,256]{3,2,0,1:T(8,128)S(1)}, u32[]{:S(2)}, u32[]{:S(2)}) collective-permute-start(f32[5,6,8,256]{3,2,0,1:T(8,128)S(1)} %pad_maximum_fusion.7), channel_id=1, source_target_pairs={{22,0},{23,1},{0,2},{1,3},{2,4},{3,5},{4,6},{5,7},{6,8},{7,9},{8,1... | collective-permute-start | bytes 737288 | tf_op jit(solution)/shard_map/ppermute | solution.py:16
  60.5 0.8 fusion.1
  61.2 20.9 %collective-permute-done.9 = f32[5,6,8,256]{3,2,0,1:T(8,128)S(1)} collective-permute-done((f32[5,6,8,256]{3,2,0,1:T(8,128)S(1)}, f32[5,6,8,256]{3,2,0,1:T(8,128)S(1)}, u32[]{:S(2)}, u32[]{:S(2)}) %collective-permute-start.9) | collective-permute-done | bytes 245792 | tf_op jit(solution)/shard_map/ppermute | solution.py:16
  82.2 1.9 %collective-permute-start.10 = (f32[5,6,8,256]{3,2,0,1:T(8,128)S(1)}, f32[5,6,8,256]{3,2,0,1:T(8,128)S(1)}, u32[]{:S(2)}, u32[]{:S(2)}) collective-permute-start(f32[5,6,8,256]{3,2,0,1:T(8,128)S(1)} %collective-permute-done.9), channel_id=1, source_target_pairs={{23,0},{0,1},{1,2},{2,3},{3,4},{4,5},{5,6},{6,7},{7,8},{8,9},{9,10... | collective-permute-start | bytes 737288 | tf_op jit(solution)/shard_map/ppermute | solution.py:16
  84.1 0.8 fusion.21
  84.9 0.8 fusion.18
  85.6 8.8 %collective-permute-done.10 = f32[5,6,8,256]{3,2,0,1:T(8,128)S(1)} collective-permute-done((f32[5,6,8,256]{3,2,0,1:T(8,128)S(1)}, f32[5,6,8,256]{3,2,0,1:T(8,128)S(1)}, u32[]{:S(2)}, u32[]{:S(2)}) %collective-permute-start.10) | collective-permute-done | bytes 245792 | tf_op jit(solution)/shard_map/ppermute | solution.py:16
  94.5 0.8 fusion.15
  95.2 0.7 copy.50
  (91 shorter events, 10.7 us)
Async XLA Ops:
  0.0 5.7 %copy-start = (f32[5,6,8,256]{3,2,1,0:T(8,128)S(1)}, f32[5,6,8,256]{3,2,1,0:T(8,128)}, u32[]{:S(2)}) copy-start(f32[5,6,8,256]{3,2,1,0:T(8,128)} %param.2) | copy-start | bytes 737284
  1.0 28.5 %collective-permute-start.1 = (f32[5,3,8,256]{3,2,0,1:T(8,128)S(1)}, f32[5,3,8,256]{3,2,0,1:T(8,128)S(1)}, u32[]{:S(2)}, u32[]{:S(2)}) collective-permute-start(f32[5,3,8,256]{3,2,0,1:T(8,128)S(1)} %get-tuple-element.32), channel_id=1, source_target_pairs={{24,0},{48,24},{72,48},{96,72},{120,96},{144,120},{168,144},{192,1... | collective-permute-start | bytes 368648 | tf_op jit(solution)/shard_map/ppermute | solution.py:182
  3.7 25.8 %collective-permute-start = (f32[5,3,8,256]{3,2,0,1:T(8,128)S(1)}, f32[5,3,8,256]{3,2,0,1:T(8,128)S(1)}, u32[]{:S(2)}, u32[]{:S(2)}) collective-permute-start(f32[5,3,8,256]{3,2,0,1:T(8,128)S(1)} %get-tuple-element.31), channel_id=1, source_target_pairs={{0,24},{24,48},{48,72},{72,96},{96,120},{120,144},{144,168},{168,1... | collective-permute-start | bytes 368648 | tf_op jit(solution)/shard_map/ppermute | solution.py:181
  5.8 21.5 %collective-permute-start.2 = (f32[5,6,8,3]{3,2,0,1:T(8,128)S(1)}, f32[5,6,8,3]{3,2,0,1:T(8,128)S(1)}, u32[]{:S(2)}, u32[]{:S(2)}) collective-permute-start(f32[5,6,8,3]{3,2,0,1:T(8,128)S(1)} %get-tuple-element.35), channel_id=1, source_target_pairs={{0,1},{1,2},{2,3},{3,4},{4,5},{5,6},{6,7},{7,8},{8,9},{9,10},{10,1... | collective-permute-start | bytes 8648 | tf_op jit(solution)/shard_map/ppermute | solution.py:183
  10.1 17.2 %collective-permute-start.3 = (f32[5,6,8,3]{3,2,0,1:T(8,128)S(1)}, f32[5,6,8,3]{3,2,0,1:T(8,128)S(1)}, u32[]{:S(2)}, u32[]{:S(2)}) collective-permute-start(f32[5,6,8,3]{3,2,0,1:T(8,128)S(1)} %get-tuple-element.36), channel_id=1, source_target_pairs={{0,23},{1,0},{2,1},{3,2},{4,3},{5,4},{6,5},{7,6},{8,7},{9,8},{10,9... | collective-permute-start | bytes 8648 | tf_op jit(solution)/shard_map/ppermute | solution.py:184
  31.2 23.8 %collective-permute-start.4 = (f32[5,3,8,256]{3,2,0,1:T(8,128)S(1)}, f32[5,3,8,256]{3,2,0,1:T(8,128)S(1)}, u32[]{:S(2)}, u32[]{:S(2)}) collective-permute-start(f32[5,3,8,256]{3,2,0,1:T(8,128)S(1)} %get-tuple-element.21), channel_id=1, source_target_pairs={{0,24},{24,48},{48,72},{72,96},{96,120},{120,144},{144,168},{168,1... | collective-permute-start | bytes 368648 | tf_op jit(solution)/shard_map/ppermute | solution.py:181
  35.7 19.3 %collective-permute-start.5 = (f32[5,3,8,256]{3,2,0,1:T(8,128)S(1)}, f32[5,3,8,256]{3,2,0,1:T(8,128)S(1)}, u32[]{:S(2)}, u32[]{:S(2)}) collective-permute-start(f32[5,3,8,256]{3,2,0,1:T(8,128)S(1)} %get-tuple-element.22), channel_id=1, source_target_pairs={{24,0},{48,24},{72,48},{96,72},{120,96},{144,120},{168,144},{192,1... | collective-permute-start | bytes 368648 | tf_op jit(solution)/shard_map/ppermute | solution.py:182
  40.0 11.6 %collective-permute-start.6 = (f32[5,6,8,3]{3,2,0,1:T(8,128)S(1)}, f32[5,6,8,3]{3,2,0,1:T(8,128)S(1)}, u32[]{:S(2)}, u32[]{:S(2)}) collective-permute-start(f32[5,6,8,3]{3,2,0,1:T(8,128)S(1)} %get-tuple-element.25), channel_id=1, source_target_pairs={{0,1},{1,2},{2,3},{3,4},{4,5},{5,6},{6,7},{7,8},{8,9},{9,10},{10,1... | collective-permute-start | bytes 8648 | tf_op jit(solution)/shard_map/ppermute | solution.py:183
  41.9 10.9 %collective-permute-start.7 = (f32[5,6,8,3]{3,2,0,1:T(8,128)S(1)}, f32[5,6,8,3]{3,2,0,1:T(8,128)S(1)}, u32[]{:S(2)}, u32[]{:S(2)}) collective-permute-start(f32[5,6,8,3]{3,2,0,1:T(8,128)S(1)} %get-tuple-element.26), channel_id=1, source_target_pairs={{0,23},{1,0},{2,1},{3,2},{4,3},{5,4},{6,5},{7,6},{8,7},{9,8},{10,9... | collective-permute-start | bytes 8648 | tf_op jit(solution)/shard_map/ppermute | solution.py:184
  56.5 4.0 %copy-start.1 = (s32[6]{0:T(128)S(1)}, s32[6]{0:T(128)}, u32[]{:S(2)}) copy-start(s32[6]{0:T(128)} %param.3) | copy-start | bytes 76
  56.6 27.5 %collective-permute-start.8 = (f32[5,6,8,256]{3,2,0,1:T(8,128)S(1)}, f32[5,6,8,256]{3,2,0,1:T(8,128)S(1)}, u32[]{:S(2)}, u32[]{:S(2)}) collective-permute-start(f32[5,6,8,256]{3,2,0,1:T(8,128)S(1)} %pad_maximum_fusion.7), channel_id=1, source_target_pairs={{23,0},{0,1},{1,2},{2,3},{3,4},{4,5},{5,6},{6,7},{7,8},{8,9},{9,10... | collective-permute-start | bytes 737288 | tf_op jit(solution)/shard_map/ppermute | solution.py:16
  58.5 23.7 %collective-permute-start.9 = (f32[5,6,8,256]{3,2,0,1:T(8,128)S(1)}, f32[5,6,8,256]{3,2,0,1:T(8,128)S(1)}, u32[]{:S(2)}, u32[]{:S(2)}) collective-permute-start(f32[5,6,8,256]{3,2,0,1:T(8,128)S(1)} %pad_maximum_fusion.7), channel_id=1, source_target_pairs={{22,0},{23,1},{0,2},{1,3},{2,4},{3,5},{4,6},{5,7},{6,8},{7,9},{8,1... | collective-permute-start | bytes 737288 | tf_op jit(solution)/shard_map/ppermute | solution.py:16
  82.2 12.3 %collective-permute-start.10 = (f32[5,6,8,256]{3,2,0,1:T(8,128)S(1)}, f32[5,6,8,256]{3,2,0,1:T(8,128)S(1)}, u32[]{:S(2)}, u32[]{:S(2)}) collective-permute-start(f32[5,6,8,256]{3,2,0,1:T(8,128)S(1)} %collective-permute-done.9), channel_id=1, source_target_pairs={{23,0},{0,1},{1,2},{2,3},{3,4},{4,5},{5,6},{6,7},{7,8},{8,9},{9,10... | collective-permute-start | bytes 737288 | tf_op jit(solution)/shard_map/ppermute | solution.py:16

commit v8 on v7

--- a/solution.py
+++ b/solution.py
@@ -205,7 +205,10 @@
     target = lax.broadcasted_iota(jnp.int32, (1, cell_count, cell_count), 2)
     offset = source - target + shifts[:, None, None]
     total = None
-    for distance, block in enumerate(blocks):
+    arrival = [0] + list(range(2, far + 1))[:1] + [1] + list(range(3, far + 1))
+    arrival = [d for d in arrival if d < len(blocks)]
+    for distance in arrival:
+        block = blocks[distance]
         pick = (offset == distance * cell_count).astype(jnp.float32)
         part = jnp.einsum(
             "fitk,ikc->fitc",

time: 96.8 us -> 90.6 us (0.936)
  waiting for transfers between devices: 32.9 us -> 27.3 us
    ppermute x3, waiting for transfers between devices: 29.8 us -> 24.1 us  [shifted(): return lax.ppermute(block, axis, route)]
  transfers between devices with their start and end apart: 11 -> 11, of which waited for: 4 -> 5; matrix products, arithmetic and copies ran while one was open for 12% -> 13% of each run, Pallas kernels for 0% -> 0%
where the time goes in v8:
time: 90.6 us; the launch traced here: 90.3 us
  starting transfers between devices  45.4 us (50%)
  waiting for transfers between devices  27.3 us (30%)
  other arithmetic  11.6 us (13%)
  matrix products  3 us (3%)
  local copies, waits for them, and re-layouts  2.19 us (2%)
    ppermute x3, waiting for transfers between devices, shifted(): return lax.ppermute(block, axis, route)  24.1 us
    ppermute x2, starting transfers between devices, halos(): from_right = lax.ppermute(x[..., :width], 'az', ring_pairs(n_az, -1, True))  22.4 us
    ppermute x2, starting transfers between devices, halos(): from_below = lax.ppermute(x[:, -width:], 'rad', ring_pairs(n_rad, 1, False))  6.44 us
    ppermute x2, starting transfers between devices, halos(): from_left = lax.ppermute(x[..., -width:], 'az', ring_pairs(n_az, 1, True))  6.2 us
    ppermute x3, starting transfers between devices, shifted(): return lax.ppermute(block, axis, route)  5.75 us
    unnamed x27, other arithmetic  4.96 us
    ppermute x2, starting transfers between devices, halos(): from_above = lax.ppermute(x[:, :width], 'rad', ring_pairs(n_rad, -1, False))  4.62 us
    dot_general x4, matrix products, shift_rows(): jnp.einsum('fitk,ikc->fitc', block, pick, precision=lax.Precision.HIGHEST...  3 us
  transfers between devices with their start and end apart: 11, of which 5 were waited for; matrix products, arithmetic and copies ran while one was open for 13% of the time, Pallas kernels for 0%

profile of v8, /device:TPU:56, one launch (start us, length us, event | category | flops | bytes accessed | tf_op | source)
XLA Modules:
  0.0 90.3 jit_solution(12984984569011250845)
XLA Ops:
  0.0 1.0 %fusion.232 = (f32[5,3,8,256]{3,2,0,1:T(8,128)S(1)}, f32[5,3,8,256]{3,2,0,1:T(8,128)S(1)}) fusion(f32[5,6,8,256]{3,2,1,0:T(8,128)} %param.2), kind=kLoop, calls=%fused_computation.426 | loop fusion | bytes 491520 | tf_op jit(solution)/shard_map/slice | solution.py:181
  1.0 2.7 %collective-permute-start.1 = (f32[5,3,8,256]{3,2,0,1:T(8,128)S(1)}, f32[5,3,8,256]{3,2,0,1:T(8,128)S(1)}, u32[]{:S(2)}, u32[]{:S(2)}) collective-permute-start(f32[5,3,8,256]{3,2,0,1:T(8,128)S(1)} %get-tuple-element.32), channel_id=1, source_target_pairs={{24,0},{48,24},{72,48},{96,72},{120,96},{144,120},{168,144},{192,1... | collective-permute-start | bytes 368648 | tf_op jit(solution)/shard_map/ppermute | solution.py:182
  3.7 1.9 %collective-permute-start = (f32[5,3,8,256]{3,2,0,1:T(8,128)S(1)}, f32[5,3,8,256]{3,2,0,1:T(8,128)S(1)}, u32[]{:S(2)}, u32[]{:S(2)}) collective-permute-start(f32[5,3,8,256]{3,2,0,1:T(8,128)S(1)} %get-tuple-element.31), channel_id=1, source_target_pairs={{0,24},{24,48},{48,72},{72,96},{96,120},{120,144},{144,168},{168,1... | collective-permute-start | bytes 368648 | tf_op jit(solution)/shard_map/ppermute | solution.py:181
  5.8 4.3 %collective-permute-start.2 = (f32[5,6,8,3]{3,2,0,1:T(8,128)S(1)}, f32[5,6,8,3]{3,2,0,1:T(8,128)S(1)}, u32[]{:S(2)}, u32[]{:S(2)}) collective-permute-start(f32[5,6,8,3]{3,2,0,1:T(8,128)S(1)} %get-tuple-element.35), channel_id=1, source_target_pairs={{0,1},{1,2},{2,3},{3,4},{4,5},{5,6},{6,7},{7,8},{8,9},{9,10},{10,1... | collective-permute-start | bytes 8648 | tf_op jit(solution)/shard_map/ppermute | solution.py:183
  10.1 14.7 %collective-permute-start.3 = (f32[5,6,8,3]{3,2,0,1:T(8,128)S(1)}, f32[5,6,8,3]{3,2,0,1:T(8,128)S(1)}, u32[]{:S(2)}, u32[]{:S(2)}) collective-permute-start(f32[5,6,8,3]{3,2,0,1:T(8,128)S(1)} %get-tuple-element.36), channel_id=1, source_target_pairs={{0,23},{1,0},{2,1},{3,2},{4,3},{5,4},{6,5},{7,6},{8,7},{9,8},{10,9... | collective-permute-start | bytes 8648 | tf_op jit(solution)/shard_map/ppermute | solution.py:184
  25.3 0.5 subtract_select_fusion.2
  31.2 4.5 %collective-permute-start.4 = (f32[5,3,8,256]{3,2,0,1:T(8,128)S(1)}, f32[5,3,8,256]{3,2,0,1:T(8,128)S(1)}, u32[]{:S(2)}, u32[]{:S(2)}) collective-permute-start(f32[5,3,8,256]{3,2,0,1:T(8,128)S(1)} %get-tuple-element.21), channel_id=1, source_target_pairs={{0,24},{24,48},{48,72},{72,96},{96,120},{120,144},{144,168},{168,1... | collective-permute-start | bytes 368648 | tf_op jit(solution)/shard_map/ppermute | solution.py:181
  35.7 1.9 %collective-permute-start.5 = (f32[5,3,8,256]{3,2,0,1:T(8,128)S(1)}, f32[5,3,8,256]{3,2,0,1:T(8,128)S(1)}, u32[]{:S(2)}, u32[]{:S(2)}) collective-permute-start(f32[5,3,8,256]{3,2,0,1:T(8,128)S(1)} %get-tuple-element.22), channel_id=1, source_target_pairs={{24,0},{48,24},{72,48},{96,72},{120,96},{144,120},{168,144},{192,1... | collective-permute-start | bytes 368648 | tf_op jit(solution)/shard_map/ppermute | solution.py:182
  38.1 0.5 subtract_select_fusion
  40.0 1.9 %collective-permute-start.6 = (f32[5,6,8,3]{3,2,0,1:T(8,128)S(1)}, f32[5,6,8,3]{3,2,0,1:T(8,128)S(1)}, u32[]{:S(2)}, u32[]{:S(2)}) collective-permute-start(f32[5,6,8,3]{3,2,0,1:T(8,128)S(1)} %get-tuple-element.25), channel_id=1, source_target_pairs={{0,1},{1,2},{2,3},{3,4},{4,5},{5,6},{6,7},{7,8},{8,9},{9,10},{10,1... | collective-permute-start | bytes 8648 | tf_op jit(solution)/shard_map/ppermute | solution.py:183
  41.9 7.7 %collective-permute-start.7 = (f32[5,6,8,3]{3,2,0,1:T(8,128)S(1)}, f32[5,6,8,3]{3,2,0,1:T(8,128)S(1)}, u32[]{:S(2)}, u32[]{:S(2)}) collective-permute-start(f32[5,6,8,3]{3,2,0,1:T(8,128)S(1)} %get-tuple-element.26), channel_id=1, source_target_pairs={{0,23},{1,0},{2,1},{3,2},{4,3},{5,4},{6,5},{7,6},{8,7},{9,8},{10,9... | collective-permute-start | bytes 8648 | tf_op jit(solution)/shard_map/ppermute | solution.py:184
  49.6 2.0 %collective-permute-done.6 = f32[5,6,8,3]{3,2,0,1:T(8,128)S(1)} collective-permute-done((f32[5,6,8,3]{3,2,0,1:T(8,128)S(1)}, f32[5,6,8,3]{3,2,0,1:T(8,128)S(1)}, u32[]{:S(2)}, u32[]{:S(2)}) %collective-permute-start.6) | collective-permute-done | bytes 2912 | tf_op jit(solution)/shard_map/ppermute | solution.py:183
  51.6 1.2 %collective-permute-done.7 = f32[5,6,8,3]{3,2,0,1:T(8,128)S(1)} collective-permute-done((f32[5,6,8,3]{3,2,0,1:T(8,128)S(1)}, f32[5,6,8,3]{3,2,0,1:T(8,128)S(1)}, u32[]{:S(2)}, u32[]{:S(2)}) %collective-permute-start.7) | collective-permute-done | bytes 2912 | tf_op jit(solution)/shard_map/ppermute | solution.py:184
  56.6 1.9 %collective-permute-start.8 = (f32[5,6,8,256]{3,2,0,1:T(8,128)S(1)}, f32[5,6,8,256]{3,2,0,1:T(8,128)S(1)}, u32[]{:S(2)}, u32[]{:S(2)}) collective-permute-start(f32[5,6,8,256]{3,2,0,1:T(8,128)S(1)} %pad_maximum_fusion.7), channel_id=1, source_target_pairs={{22,0},{23,1},{0,2},{1,3},{2,4},{3,5},{4,6},{5,7},{6,8},{7,9},{8,1... | collective-permute-start | bytes 737288 | tf_op jit(solution)/shard_map/ppermute | solution.py:16
  58.5 1.9 %collective-permute-start.9 = (f32[5,6,8,256]{3,2,0,1:T(8,128)S(1)}, f32[5,6,8,256]{3,2,0,1:T(8,128)S(1)}, u32[]{:S(2)}, u32[]{:S(2)}) collective-permute-start(f32[5,6,8,256]{3,2,0,1:T(8,128)S(1)} %pad_maximum_fusion.7), channel_id=1, source_target_pairs={{23,0},{0,1},{1,2},{2,3},{3,4},{4,5},{5,6},{6,7},{7,8},{8,9},{9,10... | collective-permute-start | bytes 737288 | tf_op jit(solution)/shard_map/ppermute | solution.py:16
  60.5 0.7 fusion.1
  61.2 15.8 %collective-permute-done.8 = f32[5,6,8,256]{3,2,0,1:T(8,128)S(1)} collective-permute-done((f32[5,6,8,256]{3,2,0,1:T(8,128)S(1)}, f32[5,6,8,256]{3,2,0,1:T(8,128)S(1)}, u32[]{:S(2)}, u32[]{:S(2)}) %collective-permute-start.8) | collective-permute-done | bytes 245792 | tf_op jit(solution)/shard_map/ppermute | solution.py:16
  77.1 1.9 %collective-permute-start.10 = (f32[5,6,8,256]{3,2,0,1:T(8,128)S(1)}, f32[5,6,8,256]{3,2,0,1:T(8,128)S(1)}, u32[]{:S(2)}, u32[]{:S(2)}) collective-permute-start(f32[5,6,8,256]{3,2,0,1:T(8,128)S(1)} %collective-permute-done.8), channel_id=1, source_target_pairs={{23,0},{0,1},{1,2},{2,3},{3,4},{4,5},{5,6},{6,7},{7,8},{8,9},{9,10... | collective-permute-start | bytes 737288 | tf_op jit(solution)/shard_map/ppermute | solution.py:16
  79.0 0.8 fusion.21
  79.8 1.5 %collective-permute-done.9 = f32[5,6,8,256]{3,2,0,1:T(8,128)S(1)} collective-permute-done((f32[5,6,8,256]{3,2,0,1:T(8,128)S(1)}, f32[5,6,8,256]{3,2,0,1:T(8,128)S(1)}, u32[]{:S(2)}, u32[]{:S(2)}) %collective-permute-start.9) | collective-permute-done | bytes 245792 | tf_op jit(solution)/shard_map/ppermute | solution.py:16
  81.3 0.8 fusion.18
  82.0 6.8 %collective-permute-done.10 = f32[5,6,8,256]{3,2,0,1:T(8,128)S(1)} collective-permute-done((f32[5,6,8,256]{3,2,0,1:T(8,128)S(1)}, f32[5,6,8,256]{3,2,0,1:T(8,128)S(1)}, u32[]{:S(2)}, u32[]{:S(2)}) %collective-permute-start.10) | collective-permute-done | bytes 245792 | tf_op jit(solution)/shard_map/ppermute | solution.py:16
  88.8 0.8 fusion.15
  89.5 0.7 copy.50
  (91 shorter events, 11.1 us)
Async XLA Ops:
  0.0 5.7 %copy-start = (f32[5,6,8,256]{3,2,1,0:T(8,128)S(1)}, f32[5,6,8,256]{3,2,1,0:T(8,128)}, u32[]{:S(2)}) copy-start(f32[5,6,8,256]{3,2,1,0:T(8,128)} %param.2) | copy-start | bytes 737284
  1.0 28.5 %collective-permute-start.1 = (f32[5,3,8,256]{3,2,0,1:T(8,128)S(1)}, f32[5,3,8,256]{3,2,0,1:T(8,128)S(1)}, u32[]{:S(2)}, u32[]{:S(2)}) collective-permute-start(f32[5,3,8,256]{3,2,0,1:T(8,128)S(1)} %get-tuple-element.32), channel_id=1, source_target_pairs={{24,0},{48,24},{72,48},{96,72},{120,96},{144,120},{168,144},{192,1... | collective-permute-start | bytes 368648 | tf_op jit(solution)/shard_map/ppermute | solution.py:182
  3.7 25.8 %collective-permute-start = (f32[5,3,8,256]{3,2,0,1:T(8,128)S(1)}, f32[5,3,8,256]{3,2,0,1:T(8,128)S(1)}, u32[]{:S(2)}, u32[]{:S(2)}) collective-permute-start(f32[5,3,8,256]{3,2,0,1:T(8,128)S(1)} %get-tuple-element.31), channel_id=1, source_target_pairs={{0,24},{24,48},{48,72},{72,96},{96,120},{120,144},{144,168},{168,1... | collective-permute-start | bytes 368648 | tf_op jit(solution)/shard_map/ppermute | solution.py:181
  5.8 21.5 %collective-permute-start.2 = (f32[5,6,8,3]{3,2,0,1:T(8,128)S(1)}, f32[5,6,8,3]{3,2,0,1:T(8,128)S(1)}, u32[]{:S(2)}, u32[]{:S(2)}) collective-permute-start(f32[5,6,8,3]{3,2,0,1:T(8,128)S(1)} %get-tuple-element.35), channel_id=1, source_target_pairs={{0,1},{1,2},{2,3},{3,4},{4,5},{5,6},{6,7},{7,8},{8,9},{9,10},{10,1... | collective-permute-start | bytes 8648 | tf_op jit(solution)/shard_map/ppermute | solution.py:183
  10.1 17.2 %collective-permute-start.3 = (f32[5,6,8,3]{3,2,0,1:T(8,128)S(1)}, f32[5,6,8,3]{3,2,0,1:T(8,128)S(1)}, u32[]{:S(2)}, u32[]{:S(2)}) collective-permute-start(f32[5,6,8,3]{3,2,0,1:T(8,128)S(1)} %get-tuple-element.36), channel_id=1, source_target_pairs={{0,23},{1,0},{2,1},{3,2},{4,3},{5,4},{6,5},{7,6},{8,7},{9,8},{10,9... | collective-permute-start | bytes 8648 | tf_op jit(solution)/shard_map/ppermute | solution.py:184
  31.2 23.8 %collective-permute-start.4 = (f32[5,3,8,256]{3,2,0,1:T(8,128)S(1)}, f32[5,3,8,256]{3,2,0,1:T(8,128)S(1)}, u32[]{:S(2)}, u32[]{:S(2)}) collective-permute-start(f32[5,3,8,256]{3,2,0,1:T(8,128)S(1)} %get-tuple-element.21), channel_id=1, source_target_pairs={{0,24},{24,48},{48,72},{72,96},{96,120},{120,144},{144,168},{168,1... | collective-permute-start | bytes 368648 | tf_op jit(solution)/shard_map/ppermute | solution.py:181
  35.7 19.3 %collective-permute-start.5 = (f32[5,3,8,256]{3,2,0,1:T(8,128)S(1)}, f32[5,3,8,256]{3,2,0,1:T(8,128)S(1)}, u32[]{:S(2)}, u32[]{:S(2)}) collective-permute-start(f32[5,3,8,256]{3,2,0,1:T(8,128)S(1)} %get-tuple-element.22), channel_id=1, source_target_pairs={{24,0},{48,24},{72,48},{96,72},{120,96},{144,120},{168,144},{192,1... | collective-permute-start | bytes 368648 | tf_op jit(solution)/shard_map/ppermute | solution.py:182
  40.0 11.6 %collective-permute-start.6 = (f32[5,6,8,3]{3,2,0,1:T(8,128)S(1)}, f32[5,6,8,3]{3,2,0,1:T(8,128)S(1)}, u32[]{:S(2)}, u32[]{:S(2)}) collective-permute-start(f32[5,6,8,3]{3,2,0,1:T(8,128)S(1)} %get-tuple-element.25), channel_id=1, source_target_pairs={{0,1},{1,2},{2,3},{3,4},{4,5},{5,6},{6,7},{7,8},{8,9},{9,10},{10,1... | collective-permute-start | bytes 8648 | tf_op jit(solution)/shard_map/ppermute | solution.py:183
  41.9 10.9 %collective-permute-start.7 = (f32[5,6,8,3]{3,2,0,1:T(8,128)S(1)}, f32[5,6,8,3]{3,2,0,1:T(8,128)S(1)}, u32[]{:S(2)}, u32[]{:S(2)}) collective-permute-start(f32[5,6,8,3]{3,2,0,1:T(8,128)S(1)} %get-tuple-element.26), channel_id=1, source_target_pairs={{0,23},{1,0},{2,1},{3,2},{4,3},{5,4},{6,5},{7,6},{8,7},{9,8},{10,9... | collective-permute-start | bytes 8648 | tf_op jit(solution)/shard_map/ppermute | solution.py:184
  56.5 4.0 %copy-start.1 = (s32[6]{0:T(128)S(1)}, s32[6]{0:T(128)}, u32[]{:S(2)}) copy-start(s32[6]{0:T(128)} %param.3) | copy-start | bytes 76
  56.6 20.5 %collective-permute-start.8 = (f32[5,6,8,256]{3,2,0,1:T(8,128)S(1)}, f32[5,6,8,256]{3,2,0,1:T(8,128)S(1)}, u32[]{:S(2)}, u32[]{:S(2)}) collective-permute-start(f32[5,6,8,256]{3,2,0,1:T(8,128)S(1)} %pad_maximum_fusion.7), channel_id=1, source_target_pairs={{22,0},{23,1},{0,2},{1,3},{2,4},{3,5},{4,6},{5,7},{6,8},{7,9},{8,1... | collective-permute-start | bytes 737288 | tf_op jit(solution)/shard_map/ppermute | solution.py:16
  58.5 22.7 %collective-permute-start.9 = (f32[5,6,8,256]{3,2,0,1:T(8,128)S(1)}, f32[5,6,8,256]{3,2,0,1:T(8,128)S(1)}, u32[]{:S(2)}, u32[]{:S(2)}) collective-permute-start(f32[5,6,8,256]{3,2,0,1:T(8,128)S(1)} %pad_maximum_fusion.7), channel_id=1, source_target_pairs={{23,0},{0,1},{1,2},{2,3},{3,4},{4,5},{5,6},{6,7},{7,8},{8,9},{9,10... | collective-permute-start | bytes 737288 | tf_op jit(solution)/shard_map/ppermute | solution.py:16
  77.1 11.7 %collective-permute-start.10 = (f32[5,6,8,256]{3,2,0,1:T(8,128)S(1)}, f32[5,6,8,256]{3,2,0,1:T(8,128)S(1)}, u32[]{:S(2)}, u32[]{:S(2)}) collective-permute-start(f32[5,6,8,256]{3,2,0,1:T(8,128)S(1)} %collective-permute-done.8), channel_id=1, source_target_pairs={{23,0},{0,1},{1,2},{2,3},{3,4},{4,5},{5,6},{6,7},{7,8},{8,9},{9,10... | collective-permute-start | bytes 737288 | tf_op jit(solution)/shard_map/ppermute | solution.py:16

commit v9 on v7

--- a/solution.py
+++ b/solution.py
@@ -196,16 +196,14 @@
     cell_count = primitive.shape[3]
     far = -(-MAX_SHIFT // cell_count)
     blocks = [primitive]
-    for distance in range(1, far + 1):
-        if distance <= 2:
-            blocks.append(shifted(primitive, "az", distance))
-        else:
-            blocks.append(shifted(blocks[-1], "az", 1))
+    for _ in range(1, far + 1):
+        blocks.append(shifted(blocks[-1], "az", 1))
     source = lax.broadcasted_iota(jnp.int32, (1, cell_count, cell_count), 1)
     target = lax.broadcasted_iota(jnp.int32, (1, cell_count, cell_count), 2)
     offset = source - target + shifts[:, None, None]
     total = None
-    for distance, block in enumerate(blocks):
+    for distance in range(len(blocks)):
+        block = blocks[distance]
         pick = (offset == distance * cell_count).astype(jnp.float32)
         part = jnp.einsum(
             "fitk,ikc->fitc",

time: 96.8 us -> 97.5 us (level)
  transfers between devices with their start and end apart: 11 -> 11, of which waited for: 4 -> 5; matrix products, arithmetic and copies ran while one was open for 12% -> 12% of each run, Pallas kernels for 0% -> 0%
where the time goes in v9:
time: 97.5 us; the launch traced here: 96.2 us
  starting transfers between devices  45.4 us (47%)
  waiting for transfers between devices  33.2 us (34%)
  other arithmetic  11.6 us (12%)
  matrix products  3 us (3%)
  local copies, waits for them, and re-layouts  2.19 us (2%)
    ppermute x3, waiting for transfers between devices, shifted(): return lax.ppermute(block, axis, route)  30.1 us
    ppermute x2, starting transfers between devices, halos(): from_right = lax.ppermute(x[..., :width], 'az', ring_pairs(n_az, -1, True))  22.4 us
    ppermute x2, starting transfers between devices, halos(): from_below = lax.ppermute(x[:, -width:], 'rad', ring_pairs(n_rad, 1, False))  6.44 us
    ppermute x2, starting transfers between devices, halos(): from_left = lax.ppermute(x[..., -width:], 'az', ring_pairs(n_az, 1, True))  6.2 us
    ppermute x3, starting transfers between devices, shifted(): return lax.ppermute(block, axis, route)  5.74 us
    unnamed x27, other arithmetic  4.96 us
    ppermute x2, starting transfers between devices, halos(): from_above = lax.ppermute(x[:, :width], 'rad', ring_pairs(n_rad, -1, False))  4.62 us
    dot_general x4, matrix products, shift_rows(): jnp.einsum('fitk,ikc->fitc', block, pick, precision=lax.Precision.HIGHEST...  3 us
  transfers between devices with their start and end apart: 11, of which 5 were waited for; matrix products, arithmetic and copies ran while one was open for 12% of the time, Pallas kernels for 0%

profile of v9, /device:TPU:56, one launch (start us, length us, event | category | flops | bytes accessed | tf_op | source)
XLA Modules:
  0.0 96.2 jit_solution(1853989188512983422)
XLA Ops:
  0.0 1.0 %fusion.232 = (f32[5,3,8,256]{3,2,0,1:T(8,128)S(1)}, f32[5,3,8,256]{3,2,0,1:T(8,128)S(1)}) fusion(f32[5,6,8,256]{3,2,1,0:T(8,128)} %param.2), kind=kLoop, calls=%fused_computation.426 | loop fusion | bytes 491520 | tf_op jit(solution)/shard_map/slice | solution.py:181
  1.0 2.7 %collective-permute-start.1 = (f32[5,3,8,256]{3,2,0,1:T(8,128)S(1)}, f32[5,3,8,256]{3,2,0,1:T(8,128)S(1)}, u32[]{:S(2)}, u32[]{:S(2)}) collective-permute-start(f32[5,3,8,256]{3,2,0,1:T(8,128)S(1)} %get-tuple-element.32), channel_id=1, source_target_pairs={{24,0},{48,24},{72,48},{96,72},{120,96},{144,120},{168,144},{192,1... | collective-permute-start | bytes 368648 | tf_op jit(solution)/shard_map/ppermute | solution.py:182
  3.7 1.9 %collective-permute-start = (f32[5,3,8,256]{3,2,0,1:T(8,128)S(1)}, f32[5,3,8,256]{3,2,0,1:T(8,128)S(1)}, u32[]{:S(2)}, u32[]{:S(2)}) collective-permute-start(f32[5,3,8,256]{3,2,0,1:T(8,128)S(1)} %get-tuple-element.31), channel_id=1, source_target_pairs={{0,24},{24,48},{48,72},{72,96},{96,120},{120,144},{144,168},{168,1... | collective-permute-start | bytes 368648 | tf_op jit(solution)/shard_map/ppermute | solution.py:181
  5.8 4.3 %collective-permute-start.2 = (f32[5,6,8,3]{3,2,0,1:T(8,128)S(1)}, f32[5,6,8,3]{3,2,0,1:T(8,128)S(1)}, u32[]{:S(2)}, u32[]{:S(2)}) collective-permute-start(f32[5,6,8,3]{3,2,0,1:T(8,128)S(1)} %get-tuple-element.35), channel_id=1, source_target_pairs={{0,1},{1,2},{2,3},{3,4},{4,5},{5,6},{6,7},{7,8},{8,9},{9,10},{10,1... | collective-permute-start | bytes 8648 | tf_op jit(solution)/shard_map/ppermute | solution.py:183
  10.1 14.7 %collective-permute-start.3 = (f32[5,6,8,3]{3,2,0,1:T(8,128)S(1)}, f32[5,6,8,3]{3,2,0,1:T(8,128)S(1)}, u32[]{:S(2)}, u32[]{:S(2)}) collective-permute-start(f32[5,6,8,3]{3,2,0,1:T(8,128)S(1)} %get-tuple-element.36), channel_id=1, source_target_pairs={{0,23},{1,0},{2,1},{3,2},{4,3},{5,4},{6,5},{7,6},{8,7},{9,8},{10,9... | collective-permute-start | bytes 8648 | tf_op jit(solution)/shard_map/ppermute | solution.py:184
  25.3 0.5 subtract_select_fusion.2
  31.2 4.5 %collective-permute-start.4 = (f32[5,3,8,256]{3,2,0,1:T(8,128)S(1)}, f32[5,3,8,256]{3,2,0,1:T(8,128)S(1)}, u32[]{:S(2)}, u32[]{:S(2)}) collective-permute-start(f32[5,3,8,256]{3,2,0,1:T(8,128)S(1)} %get-tuple-element.21), channel_id=1, source_target_pairs={{0,24},{24,48},{48,72},{72,96},{96,120},{120,144},{144,168},{168,1... | collective-permute-start | bytes 368648 | tf_op jit(solution)/shard_map/ppermute | solution.py:181
  35.7 1.9 %collective-permute-start.5 = (f32[5,3,8,256]{3,2,0,1:T(8,128)S(1)}, f32[5,3,8,256]{3,2,0,1:T(8,128)S(1)}, u32[]{:S(2)}, u32[]{:S(2)}) collective-permute-start(f32[5,3,8,256]{3,2,0,1:T(8,128)S(1)} %get-tuple-element.22), channel_id=1, source_target_pairs={{24,0},{48,24},{72,48},{96,72},{120,96},{144,120},{168,144},{192,1... | collective-permute-start | bytes 368648 | tf_op jit(solution)/shard_map/ppermute | solution.py:182
  38.1 0.5 subtract_select_fusion
  40.0 1.9 %collective-permute-start.6 = (f32[5,6,8,3]{3,2,0,1:T(8,128)S(1)}, f32[5,6,8,3]{3,2,0,1:T(8,128)S(1)}, u32[]{:S(2)}, u32[]{:S(2)}) collective-permute-start(f32[5,6,8,3]{3,2,0,1:T(8,128)S(1)} %get-tuple-element.25), channel_id=1, source_target_pairs={{0,1},{1,2},{2,3},{3,4},{4,5},{5,6},{6,7},{7,8},{8,9},{9,10},{10,1... | collective-permute-start | bytes 8648 | tf_op jit(solution)/shard_map/ppermute | solution.py:183
  41.9 7.7 %collective-permute-start.7 = (f32[5,6,8,3]{3,2,0,1:T(8,128)S(1)}, f32[5,6,8,3]{3,2,0,1:T(8,128)S(1)}, u32[]{:S(2)}, u32[]{:S(2)}) collective-permute-start(f32[5,6,8,3]{3,2,0,1:T(8,128)S(1)} %get-tuple-element.26), channel_id=1, source_target_pairs={{0,23},{1,0},{2,1},{3,2},{4,3},{5,4},{6,5},{7,6},{8,7},{9,8},{10,9... | collective-permute-start | bytes 8648 | tf_op jit(solution)/shard_map/ppermute | solution.py:184
  49.6 2.0 %collective-permute-done.6 = f32[5,6,8,3]{3,2,0,1:T(8,128)S(1)} collective-permute-done((f32[5,6,8,3]{3,2,0,1:T(8,128)S(1)}, f32[5,6,8,3]{3,2,0,1:T(8,128)S(1)}, u32[]{:S(2)}, u32[]{:S(2)}) %collective-permute-start.6) | collective-permute-done | bytes 2912 | tf_op jit(solution)/shard_map/ppermute | solution.py:183
  51.6 1.2 %collective-permute-done.7 = f32[5,6,8,3]{3,2,0,1:T(8,128)S(1)} collective-permute-done((f32[5,6,8,3]{3,2,0,1:T(8,128)S(1)}, f32[5,6,8,3]{3,2,0,1:T(8,128)S(1)}, u32[]{:S(2)}, u32[]{:S(2)}) %collective-permute-start.7) | collective-permute-done | bytes 2912 | tf_op jit(solution)/shard_map/ppermute | solution.py:184
  56.6 1.9 %collective-permute-start.8 = (f32[5,6,8,256]{3,2,0,1:T(8,128)S(1)}, f32[5,6,8,256]{3,2,0,1:T(8,128)S(1)}, u32[]{:S(2)}, u32[]{:S(2)}) collective-permute-start(f32[5,6,8,256]{3,2,0,1:T(8,128)S(1)} %pad_maximum_fusion.7), channel_id=1, source_target_pairs={{23,0},{0,1},{1,2},{2,3},{3,4},{4,5},{5,6},{6,7},{7,8},{8,9},{9,10... | collective-permute-start | bytes 737288 | tf_op jit(solution)/shard_map/ppermute | solution.py:16
  58.5 0.8 fusion.1
  59.3 11.2 %collective-permute-done.8 = f32[5,6,8,256]{3,2,0,1:T(8,128)S(1)} collective-permute-done((f32[5,6,8,256]{3,2,0,1:T(8,128)S(1)}, f32[5,6,8,256]{3,2,0,1:T(8,128)S(1)}, u32[]{:S(2)}, u32[]{:S(2)}) %collective-permute-start.8) | collective-permute-done | bytes 245792 | tf_op jit(solution)/shard_map/ppermute | solution.py:16
  70.5 1.9 %collective-permute-start.9 = (f32[5,6,8,256]{3,2,0,1:T(8,128)S(1)}, f32[5,6,8,256]{3,2,0,1:T(8,128)S(1)}, u32[]{:S(2)}, u32[]{:S(2)}) collective-permute-start(f32[5,6,8,256]{3,2,0,1:T(8,128)S(1)} %collective-permute-done.8), channel_id=1, source_target_pairs={{23,0},{0,1},{1,2},{2,3},{3,4},{4,5},{5,6},{6,7},{7,8},{8,9},{9,10... | collective-permute-start | bytes 737288 | tf_op jit(solution)/shard_map/ppermute | solution.py:16
  72.4 0.8 fusion.21
  73.1 9.9 %collective-permute-done.9 = f32[5,6,8,256]{3,2,0,1:T(8,128)S(1)} collective-permute-done((f32[5,6,8,256]{3,2,0,1:T(8,128)S(1)}, f32[5,6,8,256]{3,2,0,1:T(8,128)S(1)}, u32[]{:S(2)}, u32[]{:S(2)}) %collective-permute-start.9) | collective-permute-done | bytes 245792 | tf_op jit(solution)/shard_map/ppermute | solution.py:16
  83.0 1.9 %collective-permute-start.10 = (f32[5,6,8,256]{3,2,0,1:T(8,128)S(1)}, f32[5,6,8,256]{3,2,0,1:T(8,128)S(1)}, u32[]{:S(2)}, u32[]{:S(2)}) collective-permute-start(f32[5,6,8,256]{3,2,0,1:T(8,128)S(1)} %collective-permute-done.9), channel_id=1, source_target_pairs={{23,0},{0,1},{1,2},{2,3},{3,4},{4,5},{5,6},{6,7},{7,8},{8,9},{9,10... | collective-permute-start | bytes 737288 | tf_op jit(solution)/shard_map/ppermute | solution.py:16
  84.9 0.8 fusion.18
  85.7 9.0 %collective-permute-done.10 = f32[5,6,8,256]{3,2,0,1:T(8,128)S(1)} collective-permute-done((f32[5,6,8,256]{3,2,0,1:T(8,128)S(1)}, f32[5,6,8,256]{3,2,0,1:T(8,128)S(1)}, u32[]{:S(2)}, u32[]{:S(2)}) %collective-permute-start.10) | collective-permute-done | bytes 245792 | tf_op jit(solution)/shard_map/ppermute | solution.py:16
  94.7 0.7 fusion.15
  95.5 0.7 copy.50
  (91 shorter events, 11.1 us)
Async XLA Ops:
  0.0 5.7 %copy-start = (f32[5,6,8,256]{3,2,1,0:T(8,128)S(1)}, f32[5,6,8,256]{3,2,1,0:T(8,128)}, u32[]{:S(2)}) copy-start(f32[5,6,8,256]{3,2,1,0:T(8,128)} %param.2) | copy-start | bytes 737284
  1.0 28.5 %collective-permute-start.1 = (f32[5,3,8,256]{3,2,0,1:T(8,128)S(1)}, f32[5,3,8,256]{3,2,0,1:T(8,128)S(1)}, u32[]{:S(2)}, u32[]{:S(2)}) collective-permute-start(f32[5,3,8,256]{3,2,0,1:T(8,128)S(1)} %get-tuple-element.32), channel_id=1, source_target_pairs={{24,0},{48,24},{72,48},{96,72},{120,96},{144,120},{168,144},{192,1... | collective-permute-start | bytes 368648 | tf_op jit(solution)/shard_map/ppermute | solution.py:182
  3.7 25.8 %collective-permute-start = (f32[5,3,8,256]{3,2,0,1:T(8,128)S(1)}, f32[5,3,8,256]{3,2,0,1:T(8,128)S(1)}, u32[]{:S(2)}, u32[]{:S(2)}) collective-permute-start(f32[5,3,8,256]{3,2,0,1:T(8,128)S(1)} %get-tuple-element.31), channel_id=1, source_target_pairs={{0,24},{24,48},{48,72},{72,96},{96,120},{120,144},{144,168},{168,1... | collective-permute-start | bytes 368648 | tf_op jit(solution)/shard_map/ppermute | solution.py:181
  5.8 21.5 %collective-permute-start.2 = (f32[5,6,8,3]{3,2,0,1:T(8,128)S(1)}, f32[5,6,8,3]{3,2,0,1:T(8,128)S(1)}, u32[]{:S(2)}, u32[]{:S(2)}) collective-permute-start(f32[5,6,8,3]{3,2,0,1:T(8,128)S(1)} %get-tuple-element.35), channel_id=1, source_target_pairs={{0,1},{1,2},{2,3},{3,4},{4,5},{5,6},{6,7},{7,8},{8,9},{9,10},{10,1... | collective-permute-start | bytes 8648 | tf_op jit(solution)/shard_map/ppermute | solution.py:183
  10.1 17.2 %collective-permute-start.3 = (f32[5,6,8,3]{3,2,0,1:T(8,128)S(1)}, f32[5,6,8,3]{3,2,0,1:T(8,128)S(1)}, u32[]{:S(2)}, u32[]{:S(2)}) collective-permute-start(f32[5,6,8,3]{3,2,0,1:T(8,128)S(1)} %get-tuple-element.36), channel_id=1, source_target_pairs={{0,23},{1,0},{2,1},{3,2},{4,3},{5,4},{6,5},{7,6},{8,7},{9,8},{10,9... | collective-permute-start | bytes 8648 | tf_op jit(solution)/shard_map/ppermute | solution.py:184
  31.2 23.8 %collective-permute-start.4 = (f32[5,3,8,256]{3,2,0,1:T(8,128)S(1)}, f32[5,3,8,256]{3,2,0,1:T(8,128)S(1)}, u32[]{:S(2)}, u32[]{:S(2)}) collective-permute-start(f32[5,3,8,256]{3,2,0,1:T(8,128)S(1)} %get-tuple-element.21), channel_id=1, source_target_pairs={{0,24},{24,48},{48,72},{72,96},{96,120},{120,144},{144,168},{168,1... | collective-permute-start | bytes 368648 | tf_op jit(solution)/shard_map/ppermute | solution.py:181
  35.7 19.3 %collective-permute-start.5 = (f32[5,3,8,256]{3,2,0,1:T(8,128)S(1)}, f32[5,3,8,256]{3,2,0,1:T(8,128)S(1)}, u32[]{:S(2)}, u32[]{:S(2)}) collective-permute-start(f32[5,3,8,256]{3,2,0,1:T(8,128)S(1)} %get-tuple-element.22), channel_id=1, source_target_pairs={{24,0},{48,24},{72,48},{96,72},{120,96},{144,120},{168,144},{192,1... | collective-permute-start | bytes 368648 | tf_op jit(solution)/shard_map/ppermute | solution.py:182
  40.0 11.6 %collective-permute-start.6 = (f32[5,6,8,3]{3,2,0,1:T(8,128)S(1)}, f32[5,6,8,3]{3,2,0,1:T(8,128)S(1)}, u32[]{:S(2)}, u32[]{:S(2)}) collective-permute-start(f32[5,6,8,3]{3,2,0,1:T(8,128)S(1)} %get-tuple-element.25), channel_id=1, source_target_pairs={{0,1},{1,2},{2,3},{3,4},{4,5},{5,6},{6,7},{7,8},{8,9},{9,10},{10,1... | collective-permute-start | bytes 8648 | tf_op jit(solution)/shard_map/ppermute | solution.py:183
  41.9 10.9 %collective-permute-start.7 = (f32[5,6,8,3]{3,2,0,1:T(8,128)S(1)}, f32[5,6,8,3]{3,2,0,1:T(8,128)S(1)}, u32[]{:S(2)}, u32[]{:S(2)}) collective-permute-start(f32[5,6,8,3]{3,2,0,1:T(8,128)S(1)} %get-tuple-element.26), channel_id=1, source_target_pairs={{0,23},{1,0},{2,1},{3,2},{4,3},{5,4},{6,5},{7,6},{8,7},{9,8},{10,9... | collective-permute-start | bytes 8648 | tf_op jit(solution)/shard_map/ppermute | solution.py:184
  56.5 2.0 %copy-start.1 = (s32[6]{0:T(128)S(1)}, s32[6]{0:T(128)}, u32[]{:S(2)}) copy-start(s32[6]{0:T(128)} %param.3) | copy-start | bytes 76
  56.6 13.9 %collective-permute-start.8 = (f32[5,6,8,256]{3,2,0,1:T(8,128)S(1)}, f32[5,6,8,256]{3,2,0,1:T(8,128)S(1)}, u32[]{:S(2)}, u32[]{:S(2)}) collective-permute-start(f32[5,6,8,256]{3,2,0,1:T(8,128)S(1)} %pad_maximum_fusion.7), channel_id=1, source_target_pairs={{23,0},{0,1},{1,2},{2,3},{3,4},{4,5},{5,6},{6,7},{7,8},{8,9},{9,10... | collective-permute-start | bytes 737288 | tf_op jit(solution)/shard_map/ppermute | solution.py:16
  70.5 12.6 %collective-permute-start.9 = (f32[5,6,8,256]{3,2,0,1:T(8,128)S(1)}, f32[5,6,8,256]{3,2,0,1:T(8,128)S(1)}, u32[]{:S(2)}, u32[]{:S(2)}) collective-permute-start(f32[5,6,8,256]{3,2,0,1:T(8,128)S(1)} %collective-permute-done.8), channel_id=1, source_target_pairs={{23,0},{0,1},{1,2},{2,3},{3,4},{4,5},{5,6},{6,7},{7,8},{8,9},{9,10... | collective-permute-start | bytes 737288 | tf_op jit(solution)/shard_map/ppermute | solution.py:16
  83.0 11.7 %collective-permute-start.10 = (f32[5,6,8,256]{3,2,0,1:T(8,128)S(1)}, f32[5,6,8,256]{3,2,0,1:T(8,128)S(1)}, u32[]{:S(2)}, u32[]{:S(2)}) collective-permute-start(f32[5,6,8,256]{3,2,0,1:T(8,128)S(1)} %collective-permute-done.9), channel_id=1, source_target_pairs={{23,0},{0,1},{1,2},{2,3},{3,4},{4,5},{5,6},{6,7},{7,8},{8,9},{9,10... | collective-permute-start | bytes 737288 | tf_op jit(solution)/shard_map/ppermute | solution.py:16

commit v10 on v8

--- a/solution.py
+++ b/solution.py
@@ -197,15 +197,12 @@
     far = -(-MAX_SHIFT // cell_count)
     blocks = [primitive]
     for distance in range(1, far + 1):
-        if distance <= 2:
-            blocks.append(shifted(primitive, "az", distance))
-        else:
-            blocks.append(shifted(blocks[-1], "az", 1))
+        blocks.append(shifted(primitive, "az", distance))
     source = lax.broadcasted_iota(jnp.int32, (1, cell_count, cell_count), 1)
     target = lax.broadcasted_iota(jnp.int32, (1, cell_count, cell_count), 2)
     offset = source - target + shifts[:, None, None]
     total = None
-    arrival = [0] + list(range(2, far + 1))[:1] + [1] + list(range(3, far + 1))
+    arrival = [0, 1, 2, 3]
     arrival = [d for d in arrival if d < len(blocks)]
     for distance in arrival:
         block = blocks[distance]

time: 90.6 us -> 99.8 us (1.10)
  waiting for transfers between devices: 27.3 us -> 34.6 us
  starting transfers between devices: 45.4 us -> 47.3 us
    ppermute x3, waiting for transfers between devices: 24.1 us -> 31.4 us  [shifted(): return lax.ppermute(block, axis, route)]
    ppermute x3, starting transfers between devices: 5.75 us -> 7.67 us  [shifted(): return lax.ppermute(block, axis, route)]
  transfers between devices with their start and end apart: 11 -> 11, of which waited for: 5 -> 5; matrix products, arithmetic and copies ran while one was open for 13% -> 11% of each run, Pallas kernels for 0% -> 0%
where the time goes in v10:
time: 99.8 us; the launch traced here: 99.5 us
  starting transfers between devices  47.3 us (47%)
  waiting for transfers between devices  34.6 us (35%)
  other arithmetic  11.6 us (12%)
  matrix products  3 us (3%)
  local copies, waits for them, and re-layouts  2.19 us (2%)
    ppermute x3, waiting for transfers between devices, shifted(): return lax.ppermute(block, axis, route)  31.4 us
    ppermute x2, starting transfers between devices, halos(): from_right = lax.ppermute(x[..., :width], 'az', ring_pairs(n_az, -1, True))  22.4 us
    ppermute x3, starting transfers between devices, shifted(): return lax.ppermute(block, axis, route)  7.67 us
    ppermute x2, starting transfers between devices, halos(): from_below = lax.ppermute(x[:, -width:], 'rad', ring_pairs(n_rad, 1, False))  6.44 us
    ppermute x2, starting transfers between devices, halos(): from_left = lax.ppermute(x[..., -width:], 'az', ring_pairs(n_az, 1, True))  6.2 us
    unnamed x27, other arithmetic  4.96 us
    ppermute x2, starting transfers between devices, halos(): from_above = lax.ppermute(x[:, :width], 'rad', ring_pairs(n_rad, -1, False))  4.62 us
    dot_general x4, matrix products, shift_rows(): jnp.einsum('fitk,ikc->fitc', block, pick, precision=lax.Precision.HIGHEST...  3 us
  transfers between devices with their start and end apart: 11, of which 5 were waited for; matrix products, arithmetic and copies ran while one was open for 11% of the time, Pallas kernels for 0%

profile of v10, /device:TPU:56, one launch (start us, length us, event | category | flops | bytes accessed | tf_op | source)
XLA Modules:
  0.0 99.5 jit_solution(2201445451122785405)
XLA Ops:
  0.0 1.0 %fusion.232 = (f32[5,3,8,256]{3,2,0,1:T(8,128)S(1)}, f32[5,3,8,256]{3,2,0,1:T(8,128)S(1)}) fusion(f32[5,6,8,256]{3,2,1,0:T(8,128)} %param.2), kind=kLoop, calls=%fused_computation.426 | loop fusion | bytes 491520 | tf_op jit(solution)/shard_map/slice | solution.py:181
  1.0 2.7 %collective-permute-start.1 = (f32[5,3,8,256]{3,2,0,1:T(8,128)S(1)}, f32[5,3,8,256]{3,2,0,1:T(8,128)S(1)}, u32[]{:S(2)}, u32[]{:S(2)}) collective-permute-start(f32[5,3,8,256]{3,2,0,1:T(8,128)S(1)} %get-tuple-element.32), channel_id=1, source_target_pairs={{24,0},{48,24},{72,48},{96,72},{120,96},{144,120},{168,144},{192,1... | collective-permute-start | bytes 368648 | tf_op jit(solution)/shard_map/ppermute | solution.py:182
  3.7 1.9 %collective-permute-start = (f32[5,3,8,256]{3,2,0,1:T(8,128)S(1)}, f32[5,3,8,256]{3,2,0,1:T(8,128)S(1)}, u32[]{:S(2)}, u32[]{:S(2)}) collective-permute-start(f32[5,3,8,256]{3,2,0,1:T(8,128)S(1)} %get-tuple-element.31), channel_id=1, source_target_pairs={{0,24},{24,48},{48,72},{72,96},{96,120},{120,144},{144,168},{168,1... | collective-permute-start | bytes 368648 | tf_op jit(solution)/shard_map/ppermute | solution.py:181
  5.8 4.3 %collective-permute-start.2 = (f32[5,6,8,3]{3,2,0,1:T(8,128)S(1)}, f32[5,6,8,3]{3,2,0,1:T(8,128)S(1)}, u32[]{:S(2)}, u32[]{:S(2)}) collective-permute-start(f32[5,6,8,3]{3,2,0,1:T(8,128)S(1)} %get-tuple-element.35), channel_id=1, source_target_pairs={{0,1},{1,2},{2,3},{3,4},{4,5},{5,6},{6,7},{7,8},{8,9},{9,10},{10,1... | collective-permute-start | bytes 8648 | tf_op jit(solution)/shard_map/ppermute | solution.py:183
  10.1 14.7 %collective-permute-start.3 = (f32[5,6,8,3]{3,2,0,1:T(8,128)S(1)}, f32[5,6,8,3]{3,2,0,1:T(8,128)S(1)}, u32[]{:S(2)}, u32[]{:S(2)}) collective-permute-start(f32[5,6,8,3]{3,2,0,1:T(8,128)S(1)} %get-tuple-element.36), channel_id=1, source_target_pairs={{0,23},{1,0},{2,1},{3,2},{4,3},{5,4},{6,5},{7,6},{8,7},{9,8},{10,9... | collective-permute-start | bytes 8648 | tf_op jit(solution)/shard_map/ppermute | solution.py:184
  25.3 0.5 subtract_select_fusion.2
  31.2 4.5 %collective-permute-start.4 = (f32[5,3,8,256]{3,2,0,1:T(8,128)S(1)}, f32[5,3,8,256]{3,2,0,1:T(8,128)S(1)}, u32[]{:S(2)}, u32[]{:S(2)}) collective-permute-start(f32[5,3,8,256]{3,2,0,1:T(8,128)S(1)} %get-tuple-element.21), channel_id=1, source_target_pairs={{0,24},{24,48},{48,72},{72,96},{96,120},{120,144},{144,168},{168,1... | collective-permute-start | bytes 368648 | tf_op jit(solution)/shard_map/ppermute | solution.py:181
  35.7 1.9 %collective-permute-start.5 = (f32[5,3,8,256]{3,2,0,1:T(8,128)S(1)}, f32[5,3,8,256]{3,2,0,1:T(8,128)S(1)}, u32[]{:S(2)}, u32[]{:S(2)}) collective-permute-start(f32[5,3,8,256]{3,2,0,1:T(8,128)S(1)} %get-tuple-element.22), channel_id=1, source_target_pairs={{24,0},{48,24},{72,48},{96,72},{120,96},{144,120},{168,144},{192,1... | collective-permute-start | bytes 368648 | tf_op jit(solution)/shard_map/ppermute | solution.py:182
  38.1 0.5 subtract_select_fusion
  40.0 1.9 %collective-permute-start.6 = (f32[5,6,8,3]{3,2,0,1:T(8,128)S(1)}, f32[5,6,8,3]{3,2,0,1:T(8,128)S(1)}, u32[]{:S(2)}, u32[]{:S(2)}) collective-permute-start(f32[5,6,8,3]{3,2,0,1:T(8,128)S(1)} %get-tuple-element.25), channel_id=1, source_target_pairs={{0,1},{1,2},{2,3},{3,4},{4,5},{5,6},{6,7},{7,8},{8,9},{9,10},{10,1... | collective-permute-start | bytes 8648 | tf_op jit(solution)/shard_map/ppermute | solution.py:183
  41.9 7.7 %collective-permute-start.7 = (f32[5,6,8,3]{3,2,0,1:T(8,128)S(1)}, f32[5,6,8,3]{3,2,0,1:T(8,128)S(1)}, u32[]{:S(2)}, u32[]{:S(2)}) collective-permute-start(f32[5,6,8,3]{3,2,0,1:T(8,128)S(1)} %get-tuple-element.26), channel_id=1, source_target_pairs={{0,23},{1,0},{2,1},{3,2},{4,3},{5,4},{6,5},{7,6},{8,7},{9,8},{10,9... | collective-permute-start | bytes 8648 | tf_op jit(solution)/shard_map/ppermute | solution.py:184
  49.6 2.0 %collective-permute-done.6 = f32[5,6,8,3]{3,2,0,1:T(8,128)S(1)} collective-permute-done((f32[5,6,8,3]{3,2,0,1:T(8,128)S(1)}, f32[5,6,8,3]{3,2,0,1:T(8,128)S(1)}, u32[]{:S(2)}, u32[]{:S(2)}) %collective-permute-start.6) | collective-permute-done | bytes 2912 | tf_op jit(solution)/shard_map/ppermute | solution.py:183
  51.6 1.2 %collective-permute-done.7 = f32[5,6,8,3]{3,2,0,1:T(8,128)S(1)} collective-permute-done((f32[5,6,8,3]{3,2,0,1:T(8,128)S(1)}, f32[5,6,8,3]{3,2,0,1:T(8,128)S(1)}, u32[]{:S(2)}, u32[]{:S(2)}) %collective-permute-start.7) | collective-permute-done | bytes 2912 | tf_op jit(solution)/shard_map/ppermute | solution.py:184
  56.6 1.9 %collective-permute-start.8 = (f32[5,6,8,256]{3,2,0,1:T(8,128)S(1)}, f32[5,6,8,256]{3,2,0,1:T(8,128)S(1)}, u32[]{:S(2)}, u32[]{:S(2)}) collective-permute-start(f32[5,6,8,256]{3,2,0,1:T(8,128)S(1)} %pad_maximum_fusion.7), channel_id=1, source_target_pairs={{23,0},{0,1},{1,2},{2,3},{3,4},{4,5},{5,6},{6,7},{7,8},{8,9},{9,10... | collective-permute-start | bytes 737288 | tf_op jit(solution)/shard_map/ppermute | solution.py:16
  58.5 1.9 %collective-permute-start.10 = (f32[5,6,8,256]{3,2,0,1:T(8,128)S(1)}, f32[5,6,8,256]{3,2,0,1:T(8,128)S(1)}, u32[]{:S(2)}, u32[]{:S(2)}) collective-permute-start(f32[5,6,8,256]{3,2,0,1:T(8,128)S(1)} %pad_maximum_fusion.7), channel_id=1, source_target_pairs={{21,0},{22,1},{23,2},{0,3},{1,4},{2,5},{3,6},{4,7},{5,8},{6,9},{7,... | collective-permute-start | bytes 737288 | tf_op jit(solution)/shard_map/ppermute | solution.py:16
  60.5 3.8 %collective-permute-start.9 = (f32[5,6,8,256]{3,2,0,1:T(8,128)S(1)}, f32[5,6,8,256]{3,2,0,1:T(8,128)S(1)}, u32[]{:S(2)}, u32[]{:S(2)}) collective-permute-start(f32[5,6,8,256]{3,2,0,1:T(8,128)S(1)} %pad_maximum_fusion.7), channel_id=1, source_target_pairs={{22,0},{23,1},{0,2},{1,3},{2,4},{3,5},{4,6},{5,7},{6,8},{7,9},{8,1... | collective-permute-start | bytes 737288 | tf_op jit(solution)/shard_map/ppermute | solution.py:16
  64.3 0.8 fusion.1
  65.1 7.6 %collective-permute-done.8 = f32[5,6,8,256]{3,2,0,1:T(8,128)S(1)} collective-permute-done((f32[5,6,8,256]{3,2,0,1:T(8,128)S(1)}, f32[5,6,8,256]{3,2,0,1:T(8,128)S(1)}, u32[]{:S(2)}, u32[]{:S(2)}) %collective-permute-start.8) | collective-permute-done | bytes 245792 | tf_op jit(solution)/shard_map/ppermute | solution.py:16
  72.7 0.7 fusion.15
  73.4 15.7 %collective-permute-done.10 = f32[5,6,8,256]{3,2,0,1:T(8,128)S(1)} collective-permute-done((f32[5,6,8,256]{3,2,0,1:T(8,128)S(1)}, f32[5,6,8,256]{3,2,0,1:T(8,128)S(1)}, u32[]{:S(2)}, u32[]{:S(2)}) %collective-permute-start.10) | collective-permute-done | bytes 245792 | tf_op jit(solution)/shard_map/ppermute | solution.py:16
  89.1 0.7 fusion.10
  89.9 8.1 %collective-permute-done.9 = f32[5,6,8,256]{3,2,0,1:T(8,128)S(1)} collective-permute-done((f32[5,6,8,256]{3,2,0,1:T(8,128)S(1)}, f32[5,6,8,256]{3,2,0,1:T(8,128)S(1)}, u32[]{:S(2)}, u32[]{:S(2)}) %collective-permute-start.9) | collective-permute-done | bytes 245792 | tf_op jit(solution)/shard_map/ppermute | solution.py:16
  98.0 0.8 fusion.21
  98.7 0.7 copy.50
  (91 shorter events, 11.1 us)
Async XLA Ops:
  0.0 5.7 %copy-start = (f32[5,6,8,256]{3,2,1,0:T(8,128)S(1)}, f32[5,6,8,256]{3,2,1,0:T(8,128)}, u32[]{:S(2)}) copy-start(f32[5,6,8,256]{3,2,1,0:T(8,128)} %param.2) | copy-start | bytes 737284
  1.0 28.5 %collective-permute-start.1 = (f32[5,3,8,256]{3,2,0,1:T(8,128)S(1)}, f32[5,3,8,256]{3,2,0,1:T(8,128)S(1)}, u32[]{:S(2)}, u32[]{:S(2)}) collective-permute-start(f32[5,3,8,256]{3,2,0,1:T(8,128)S(1)} %get-tuple-element.32), channel_id=1, source_target_pairs={{24,0},{48,24},{72,48},{96,72},{120,96},{144,120},{168,144},{192,1... | collective-permute-start | bytes 368648 | tf_op jit(solution)/shard_map/ppermute | solution.py:182
  3.7 25.8 %collective-permute-start = (f32[5,3,8,256]{3,2,0,1:T(8,128)S(1)}, f32[5,3,8,256]{3,2,0,1:T(8,128)S(1)}, u32[]{:S(2)}, u32[]{:S(2)}) collective-permute-start(f32[5,3,8,256]{3,2,0,1:T(8,128)S(1)} %get-tuple-element.31), channel_id=1, source_target_pairs={{0,24},{24,48},{48,72},{72,96},{96,120},{120,144},{144,168},{168,1... | collective-permute-start | bytes 368648 | tf_op jit(solution)/shard_map/ppermute | solution.py:181
  5.8 21.5 %collective-permute-start.2 = (f32[5,6,8,3]{3,2,0,1:T(8,128)S(1)}, f32[5,6,8,3]{3,2,0,1:T(8,128)S(1)}, u32[]{:S(2)}, u32[]{:S(2)}) collective-permute-start(f32[5,6,8,3]{3,2,0,1:T(8,128)S(1)} %get-tuple-element.35), channel_id=1, source_target_pairs={{0,1},{1,2},{2,3},{3,4},{4,5},{5,6},{6,7},{7,8},{8,9},{9,10},{10,1... | collective-permute-start | bytes 8648 | tf_op jit(solution)/shard_map/ppermute | solution.py:183
  10.1 17.2 %collective-permute-start.3 = (f32[5,6,8,3]{3,2,0,1:T(8,128)S(1)}, f32[5,6,8,3]{3,2,0,1:T(8,128)S(1)}, u32[]{:S(2)}, u32[]{:S(2)}) collective-permute-start(f32[5,6,8,3]{3,2,0,1:T(8,128)S(1)} %get-tuple-element.36), channel_id=1, source_target_pairs={{0,23},{1,0},{2,1},{3,2},{4,3},{5,4},{6,5},{7,6},{8,7},{9,8},{10,9... | collective-permute-start | bytes 8648 | tf_op jit(solution)/shard_map/ppermute | solution.py:184
  31.2 23.8 %collective-permute-start.4 = (f32[5,3,8,256]{3,2,0,1:T(8,128)S(1)}, f32[5,3,8,256]{3,2,0,1:T(8,128)S(1)}, u32[]{:S(2)}, u32[]{:S(2)}) collective-permute-start(f32[5,3,8,256]{3,2,0,1:T(8,128)S(1)} %get-tuple-element.21), channel_id=1, source_target_pairs={{0,24},{24,48},{48,72},{72,96},{96,120},{120,144},{144,168},{168,1... | collective-permute-start | bytes 368648 | tf_op jit(solution)/shard_map/ppermute | solution.py:181
  35.7 19.3 %collective-permute-start.5 = (f32[5,3,8,256]{3,2,0,1:T(8,128)S(1)}, f32[5,3,8,256]{3,2,0,1:T(8,128)S(1)}, u32[]{:S(2)}, u32[]{:S(2)}) collective-permute-start(f32[5,3,8,256]{3,2,0,1:T(8,128)S(1)} %get-tuple-element.22), channel_id=1, source_target_pairs={{24,0},{48,24},{72,48},{96,72},{120,96},{144,120},{168,144},{192,1... | collective-permute-start | bytes 368648 | tf_op jit(solution)/shard_map/ppermute | solution.py:182
  40.0 11.6 %collective-permute-start.6 = (f32[5,6,8,3]{3,2,0,1:T(8,128)S(1)}, f32[5,6,8,3]{3,2,0,1:T(8,128)S(1)}, u32[]{:S(2)}, u32[]{:S(2)}) collective-permute-start(f32[5,6,8,3]{3,2,0,1:T(8,128)S(1)} %get-tuple-element.25), channel_id=1, source_target_pairs={{0,1},{1,2},{2,3},{3,4},{4,5},{5,6},{6,7},{7,8},{8,9},{9,10},{10,1... | collective-permute-start | bytes 8648 | tf_op jit(solution)/shard_map/ppermute | solution.py:183
  41.9 10.9 %collective-permute-start.7 = (f32[5,6,8,3]{3,2,0,1:T(8,128)S(1)}, f32[5,6,8,3]{3,2,0,1:T(8,128)S(1)}, u32[]{:S(2)}, u32[]{:S(2)}) collective-permute-start(f32[5,6,8,3]{3,2,0,1:T(8,128)S(1)} %get-tuple-element.26), channel_id=1, source_target_pairs={{0,23},{1,0},{2,1},{3,2},{4,3},{5,4},{6,5},{7,6},{8,7},{9,8},{10,9... | collective-permute-start | bytes 8648 | tf_op jit(solution)/shard_map/ppermute | solution.py:184
  56.5 7.8 %copy-start.1 = (s32[6]{0:T(128)S(1)}, s32[6]{0:T(128)}, u32[]{:S(2)}) copy-start(s32[6]{0:T(128)} %param.3) | copy-start | bytes 76
  56.6 16.1 %collective-permute-start.8 = (f32[5,6,8,256]{3,2,0,1:T(8,128)S(1)}, f32[5,6,8,256]{3,2,0,1:T(8,128)S(1)}, u32[]{:S(2)}, u32[]{:S(2)}) collective-permute-start(f32[5,6,8,256]{3,2,0,1:T(8,128)S(1)} %pad_maximum_fusion.7), channel_id=1, source_target_pairs={{23,0},{0,1},{1,2},{2,3},{3,4},{4,5},{5,6},{6,7},{7,8},{8,9},{9,10... | collective-permute-start | bytes 737288 | tf_op jit(solution)/shard_map/ppermute | solution.py:16
  58.5 30.6 %collective-permute-start.10 = (f32[5,6,8,256]{3,2,0,1:T(8,128)S(1)}, f32[5,6,8,256]{3,2,0,1:T(8,128)S(1)}, u32[]{:S(2)}, u32[]{:S(2)}) collective-permute-start(f32[5,6,8,256]{3,2,0,1:T(8,128)S(1)} %pad_maximum_fusion.7), channel_id=1, source_target_pairs={{21,0},{22,1},{23,2},{0,3},{1,4},{2,5},{3,6},{4,7},{5,8},{6,9},{7,... | collective-permute-start | bytes 737288 | tf_op jit(solution)/shard_map/ppermute | solution.py:16
  60.5 37.5 %collective-permute-start.9 = (f32[5,6,8,256]{3,2,0,1:T(8,128)S(1)}, f32[5,6,8,256]{3,2,0,1:T(8,128)S(1)}, u32[]{:S(2)}, u32[]{:S(2)}) collective-permute-start(f32[5,6,8,256]{3,2,0,1:T(8,128)S(1)} %pad_maximum_fusion.7), channel_id=1, source_target_pairs={{22,0},{23,1},{0,2},{1,3},{2,4},{3,5},{4,6},{5,7},{6,8},{7,9},{8,1... | collective-permute-start | bytes 737288 | tf_op jit(solution)/shard_map/ppermute | solution.py:16
